TPU v7x, 128 devices: a whole 4x4x4 slice. The times are simulated.
128 devices in a mesh: req: 16 (over y, z), mlp: 8 (over x, core).
Axes of the slice: x: 4, y: 4, z: 4, core: 2. Of those that a mesh axis runs over, the one named last changes fastest.
Arguments:
- tokens: bfloat16 [32768, 1536], P(('req', 'mlp')), may hold values from -6 to 6
- attn_gain: float32 [1536], replicated, may hold values from 0.1 to 1.9
- w_query: bfloat16 [1536, 1536], replicated, may hold values from -0.15625 to 0.15625
- w_keyval: bfloat16 [1536, 256], replicated, may hold values from -0.15625 to 0.15625
- w_out: bfloat16 [1536, 1536], replicated, may hold values from -0.15625 to 0.15625
- ffn_gain: float32 [1536], replicated, may hold values from 0.1 to 1.9
- w_gate: bfloat16 [1536, 4608], P('req', 'mlp'), may hold values from -0.15625 to 0.15625
- w_up: bfloat16 [1536, 4608], P('req', 'mlp'), may hold values from -0.15625 to 0.15625
- w_down: bfloat16 [1536, 4608], P('req', 'mlp'), may hold values from -0.09375 to 0.09375
- prefix_kv: bfloat16 [2, 128, 512, 256], P(None, 'req'), may hold values from -60 to 60, as said below
- own_prefix: bfloat16 [16, 512, 256], P('req'), may hold values from -60 to 60, as said below
- leaf_parent: int32 [16], replicated, may hold values from 0 to 127
- node_parent: int32 [128], replicated, may hold values from 0 to 127
- seg_lengths: int32 [3, 128], replicated, may hold values from 1 to 512
Outputs:
- layer_out: bfloat16 [32768, 1536], P(('req', 'mlp'))
Inputs may be any that keep to these rules, and one draw needn't show every extreme that they name: `prefix_kv`: columns below 128 are keys, the rest values. `own_prefix`: columns below 128 are keys, the rest values.
All inputs are finite; a program needn't handle non-finite values.
Results may differ from a plain program's by a relative error of at most 0.018.
Values may be sent and summed in bfloat16 or wider, within the bound.
No kernel may reach another device: no remote copies, remote signals or barrier semaphores. Data moves between devices by JAX's collectives and lax.ppermute only.
A program may use at most 192 MiB of HBM per device.

v0:
```python
import jax
import jax.numpy as jnp
from jax import lax
from jax.sharding import PartitionSpec as P

HEADS = 12
HD = 128
WINDOW = 1024


EPS = 1e-06


def rms_scale(values, gain):
    wide = values.astype(jnp.float32)
    return wide * lax.rsqrt(jnp.mean(wide * wide, axis=-1, keepdims=True) + EPS) * gain


def rotate(values, where_at):
    half_dim = values.shape[-1] // 2
    freqs = 10000.0 ** (-jnp.arange(half_dim, dtype=jnp.float32) / half_dim)
    angles = where_at.astype(jnp.float32)[:, None] * freqs[None, :]
    cosine = jnp.cos(angles)[:, None, :]
    sine = jnp.sin(angles)[:, None, :]
    first = values[..., :half_dim]
    second = values[..., half_dim:]
    return jnp.concatenate([first * cosine - second * sine, first * sine + second * cosine], -1)


def attend(queries, piece, key_at, key_live, query_at):
    scores = jnp.einsum("thd,kd->thk", queries, piece[:, :HD], preferred_element_type=jnp.float32)
    spacing = query_at[:, None] - key_at[None, :]
    allowed = (key_live[None, :] & (spacing >= 0) & (spacing < WINDOW))[:, None, :]
    top = jnp.max(jnp.where(allowed, scores, -jnp.inf), axis=-1)
    safe_top = jnp.where(jnp.isfinite(top), top, 0.0)
    weights = jnp.where(allowed, jnp.exp(scores - safe_top[..., None]), 0.0)
    mixed = jnp.einsum(
        "thk,kd->thd",
        weights.astype(jnp.bfloat16),
        piece[:, HD:],
        preferred_element_type=jnp.float32,
    )
    return (top, jnp.sum(weights, axis=-1), mixed)


def combine(first, second):
    top = jnp.maximum(first[0], second[0])
    safe_top = jnp.where(jnp.isfinite(top), top, 0.0)
    scale_first = jnp.exp(first[0] - safe_top)
    scale_second = jnp.exp(second[0] - safe_top)
    denom = first[1] * scale_first + second[1] * scale_second
    mixed = first[2] * scale_first[..., None] + second[2] * scale_second[..., None]
    return (top, denom, mixed)


def body(
    tokens,
    attn_gain,
    w_query,
    w_keyval,
    w_out,
    ffn_gain,
    w_gate,
    w_up,
    w_down,
    prefix_kv,
    own_prefix,
    leaf_parent,
    node_parent,
    seg_lengths,
):
    tok_rows = tokens.shape[0]
    requests = lax.axis_size("req")
    mine = lax.axis_index("req")
    position_group = lax.axis_index("mlp")
    node_dev = prefix_kv.shape[1]
    seg_slot = prefix_kv.shape[2]
    leaf = leaf_parent[mine]
    upper = node_parent[leaf]
    len_zero = seg_lengths[0, upper]
    len_one = seg_lengths[1, leaf]
    len_two = seg_lengths[2, mine]
    total = len_zero + len_one + len_two
    query_at = total + position_group * tok_rows + jnp.arange(tok_rows, dtype=jnp.int32)
    normed = rms_scale(tokens, attn_gain).astype(jnp.bfloat16)
    query_full = jnp.dot(normed, w_query, preferred_element_type=jnp.float32).reshape(
        tok_rows, HEADS, HD
    )
    queries = (rotate(query_full, query_at) * HD ** (-0.5)).astype(jnp.bfloat16)
    keyval_full = jnp.dot(normed, w_keyval, preferred_element_type=jnp.float32)
    new_keys = rotate(keyval_full[:, None, :HD], query_at)[:, 0].astype(jnp.bfloat16)
    new_vals = keyval_full[:, HD:].astype(jnp.bfloat16)
    new_keyval = jnp.concatenate([new_keys, new_vals], 1)
    start_state = (
        jnp.full((tok_rows, HEADS), -jnp.inf, jnp.float32),
        jnp.zeros((tok_rows, HEADS), jnp.float32),
        jnp.zeros((tok_rows, HEADS, HD), jnp.float32),
    )
    piece = lax.all_gather(new_keyval, "mlp", axis=0, tiled=True)
    piece_at = total + jnp.arange(piece.shape[0], dtype=jnp.int32)
    live = jnp.ones((piece.shape[0],), dtype=bool)
    own_state = combine(start_state, attend(queries, piece, piece_at, live, query_at))
    level_zero = node_parent[leaf_parent]
    wanted = jnp.stack([level_zero, leaf_parent], 1)
    owned = wanted // node_dev == mine
    local_slot = wanted % node_dev
    picker = (
        (local_slot[:, :, None] == jnp.arange(node_dev, dtype=jnp.int32)[None, None, :])
        & owned[:, :, None]
    ).astype(jnp.bfloat16)
    owners = wanted[mine] // node_dev
    from_owner = (jnp.arange(requests, dtype=jnp.int32)[:, None] == owners[None, :]).astype(
        jnp.bfloat16
    )
    outgoing = jnp.einsum(
        "rln,lnsc->rlsc", picker, prefix_kv, preferred_element_type=jnp.float32
    ).astype(jnp.bfloat16)
    arrived = lax.all_to_all(outgoing, "req", split_axis=0, concat_axis=0, tiled=True)
    levels = jnp.einsum(
        "rl,rlsc->lsc", from_owner, arrived, preferred_element_type=jnp.float32
    ).astype(jnp.bfloat16)
    offsets = jnp.arange(seg_slot, dtype=jnp.int32)
    cached = jnp.concatenate([levels[0], levels[1], own_prefix[0]], 0)
    cached_at = jnp.concatenate([offsets, len_zero + offsets, len_zero + len_one + offsets], 0)
    cached_live = jnp.concatenate([offsets < len_zero, offsets < len_one, offsets < len_two], 0)
    merged = combine(own_state, attend(queries, cached, cached_at, cached_live, query_at))
    context = (merged[2] / merged[1][..., None]).reshape(tok_rows, HEADS * HD).astype(jnp.bfloat16)
    attn_out = jnp.dot(context, w_out, preferred_element_type=jnp.float32)
    resid = (tokens.astype(jnp.float32) + attn_out).astype(jnp.bfloat16)
    ffn_in = rms_scale(resid, ffn_gain).astype(jnp.bfloat16)
    all_rows = lax.all_gather(ffn_in, "mlp", axis=0, tiled=True)
    gate_full, up_full, down_full = (
        lax.all_gather(w_gate, "req", axis=0, tiled=True),
        lax.all_gather(w_up, "req", axis=0, tiled=True),
        lax.all_gather(w_down, "req", axis=0, tiled=True),
    )
    gate = jnp.dot(all_rows, gate_full, preferred_element_type=jnp.float32)
    upward = jnp.dot(all_rows, up_full, preferred_element_type=jnp.float32)
    hidden = (jax.nn.gelu(gate, approximate=True) * upward).astype(jnp.bfloat16)
    summed = lax.psum_scatter(
        lax.dot_general(
            hidden, down_full, (((1,), (1,)), ((), ())), preferred_element_type=jnp.float32
        ).astype(jnp.bfloat16),
        "mlp",
        scatter_dimension=0,
        tiled=True,
    ).astype(jnp.float32)
    return (resid.astype(jnp.float32) + summed).astype(jnp.bfloat16)


def solution(mesh):
    return jax.shard_map(
        body,
        mesh=mesh,
        in_specs=(
            P(("req", "mlp"), None),
            P(),
            P(),
            P(),
            P(),
            P(),
            P("req", "mlp"),
            P("req", "mlp"),
            P("req", "mlp"),
            P(None, "req", None, None),
            P("req", None, None),
            P(),
            P(),
            P(),
        ),
        out_specs=P(("req", "mlp"), None),
        check_vma=False,
    )
```

profile of v0, /device:TPU:1, one launch (start us, length us, event | category | flops | bytes accessed | tf_op | source)
XLA Modules:
  0.0 438.2 jit_solution(3613787128685627271)
XLA Ops:
  6.6 1.3 dynamic_slice.18
  9.8 1.2 dynamic_slice.19
  12.4 1.4 fusion.25
  13.8 1.7 fusion.35
  16.1 1.5 constant_dynamic-slice_fusion
  19.5 0.3 fusion.44
  19.8 0.7 pad_maximum_fusion.1
  20.5 0.0 all-gather.6.cloned.1.call-update
  20.5 0.7 compare_select_fusion
  21.2 0.7 gather_fusion
  21.9 7.2 %convert_bitcast_fusion = bf16[16,2,512,256]{3,0,2,1:T(8,128)(2,1)} fusion(bf16[2,8,512,256]{3,2,1,0:T(8,128)(2,1)} %param.23, s32[16,2]{0,1:T(2,128)S(1)} %get-tuple-element.24, pred[16,2]{0,1:T(4,128)(4,1)S(1)} %fusion.54), kind=kOutput, calls=%fused_computation.15 | convolution fusion | flops 71303680 | bytes 12583072 | tf_op jit(solution)/shard_map/rln,lnsc->rlsc/dot_general | solution.py:115
  29.1 9.6 %copy.33 = bf16[16,2,512,256]{3,2,1,0:T(8,128)(2,1)} copy(bf16[16,2,512,256]{3,0,2,1:T(8,128)(2,1)} %convert_bitcast_fusion) | data formatting | bytes 16777216 | tf_op jit(solution)/shard_map/convert_element_type | solution.py:117
  38.8 8.9 %all-to-all-start = ((bf16[16,2,512,256]{3,2,1,0:T(8,128)(2,1)}), bf16[16,2,512,256]{3,2,1,0:T(8,128)(2,1)}, u32[]{:S(2)}, u32[]{:S(2)}) async-start(bf16[16,2,512,256]{3,2,1,0:T(8,128)(2,1)} %copy.33), calls=%async_computation | async-start | bytes 16777216 | tf_op jit(solution)/shard_map/all_to_all | solution.py:118
  47.7 0.0 all-gather.10.cloned.1.call-start
  47.7 0.7 all-gather.10.cloned.1.call-update
  48.4 0.3 all-gather.8.cloned.1.call-start
  48.8 0.0 copy-done.3
  48.8 0.0 copy-done.9
  48.8 4.3 fusion.37
  53.1 0.1 fusion.62
  53.3 0.5 copy.45
  53.8 1.6 copy.44
  55.4 0.2 fusion.53
  55.6 0.1 copy.38
  55.7 0.6 iota_compare_fusion.4
  56.4 1.3 iota_compare_fusion.2
  57.6 0.6 iota_add_fusion.1
  58.3 0.5 multiply_cosine_fusion
  58.8 1.9 multiply_subtract_fusion
  60.7 0.5 fusion.28
  61.2 0.5 fusion.24
  61.7 0.5 fusion.30
  62.3 0.0 all-gather.6.cloned.1.call-done
  62.3 11.8 %select_reduce_fusion = (f32[256,12]{0,1:T(8,128)S(1)}, f32[256,12,2048]{2,0,1:T(8,128)}) fusion(pred[256,2048]{1,0:T(8,128)(4,1)S(1)} %fusion.24, bf16[256,12,128]{2,0,1:T(8,128)(2,1)S(1)} %fusion.28, bf16[2048,256]{0,1:T(8,128)(2,1)} %all-gather.6.cloned.1.call-done), kind=kOutput, calls=%fused_computation.2 | convolution fusion | flops 1623192576 | bytes 27013120 | tf_op jit(solution)/shard_map/thd,kd->thk/dot_general | solution.py:31
  74.2 11.3 %fusion = f32[256,12]{0,1:T(8,128)S(1)} fusion(f32[256,12,2048]{2,0,1:T(8,128)} %get-tuple-element.27, f32[256,12]{0,1:T(8,128)S(1)} %get-tuple-element.18, pred[256,2048]{1,0:T(8,128)(4,1)S(1)} %fusion.24), kind=kLoop, calls=%fused_computation.3 | loop fusion | flops 18871296 | bytes 25714688 | tf_op jit(solution)/shard_map/reduce_sum | solution.py:43
  85.5 11.8 %fusion.4 = f32[256,12,128]{0,2,1:T(8,128)} fusion(f32[256,12,2048]{2,0,1:T(8,128)} %get-tuple-element.27, f32[256,12]{0,1:T(8,128)S(1)} %get-tuple-element.18, pred[256,2048]{1,0:T(8,128)(4,1)S(1)} %fusion.24, bf16[2048,256]{0,1:T(8,128)(2,1)S(1)} %copy-done.5), kind=kOutput, calls=%fused_computation.9 | convolution fusion | flops 1629487104 | bytes 27803648 | tf_op jit(solution)/shard_map/thk,kd->thd/dot_general | solution.py:37
  97.3 97.6 %all-to-all-done = bf16[16,2,512,256]{3,2,1,0:T(8,128)(2,1)} async-done(((bf16[16,2,512,256]{3,2,1,0:T(8,128)(2,1)}), bf16[16,2,512,256]{3,2,1,0:T(8,128)(2,1)}, u32[]{:S(2)}, u32[]{:S(2)}) %all-to-all-start) | async-done | bytes 8388640 | tf_op jit(solution)/shard_map/all_to_all | solution.py:118
  194.9 8.3 %fusion.10 = bf16[2,1,512,256]{3,1,2,0:T(2,128)(2,1)S(1)} fusion(pred[16,2,1,1]{0,2,3,1:T(4,128)(4,1)S(1)} %copy.38, bf16[16,2,512,256]{3,2,1,0:T(8,128)(2,1)} %all-to-all-done), kind=kOutput, calls=%fused_computation.13 | convolution fusion | flops 8388608 | bytes 8912928 | tf_op jit(solution)/shard_map/rl,rlsc->lsc/dot_general | solution.py:119
  203.2 0.1 copy.51
  203.3 0.1 pad_maximum_fusion
  203.4 8.0 %select_reduce_fusion.1 = (f32[256,12]{0,1:T(8,128)S(1)}, f32[256,12,1536]{2,0,1:T(8,128)}) fusion(pred[256,1536]{1,0:T(8,128)(4,1)S(1)} %fusion.30, bf16[256,12,128]{2,0,1:T(8,128)(2,1)S(1)} %fusion.28, bf16[1536,256]{1,0:T(8,128)(2,1)S(1)} %pad_maximum_fusion), kind=kOutput, calls=%fused_computation.6 | convolution fusion | flops 1217393664 | bytes 20459520 | tf_op jit(solution)/shard_map/thd,kd->thk/dot_general | solution.py:31
  211.5 0.0 slice-start
  211.5 10.5 %fusion.2 = f32[256,12]{0,1:T(8,128)S(1)} fusion(f32[256,12,1536]{2,0,1:T(8,128)} %get-tuple-element.29, f32[256,12]{0,1:T(8,128)S(1)} %is-finite_select_fusion, pred[256,1536]{1,0:T(8,128)(4,1)S(1)} %fusion.30), kind=kLoop, calls=%fused_computation.7 | loop fusion | flops 14152704 | bytes 19292160 | tf_op jit(solution)/shard_map/reduce_sum | solution.py:43
  222.0 0.0 slice-start.1
  222.0 0.0 copy-start.4
  222.0 8.7 %divide_convert_fusion = bf16[256,12,128]{0,2,1:T(8,128)(2,1)S(1)} fusion(f32[256,12,128]{0,2,1:T(8,128)} %fusion.4, f32[256,12,1536]{2,0,1:T(8,128)} %get-tuple-element.29, f32[256,12]{0,1:T(8,128)S(1)} %is-finite_select_fusion, pred[256,1536]{1,0:T(8,128)(4,1)S(1)} %fusion.30, f32[256,12]{0,1:T(8,128)S(1)} %get-tuple-element.5, ...), kind=kOutput, calls=%fused_computation.46 | convolution fusion | flops 1224867840 | bytes 22118400 | tf_op jit(solution)/shard_map/thk,kd->thd/dot_general | solution.py:37
  230.8 0.0 copy-start.7
  230.8 1.5 multiply_reduce_fusion
  232.3 1.1 multiply_convert_fusion
  233.4 0.0 all-gather.8.cloned.1.call-update
  233.4 0.0 all-gather.14.cloned.1.call-start
  233.5 0.5 all-gather.14.cloned.1.call-update
  234.0 0.0 all-gather.12.cloned.1.call-start
  234.1 0.5 all-gather.12.cloned.1.call-update
  234.6 0.0 reduce-scatter.2.cloned.1.call-start
  234.7 0.0 all-gather.10.cloned.1.call-done
  234.7 44.8 %all-gather.8.cloned.1.call-done = bf16[2048,1536]{1,0:T(8,128)(2,1)} async-done(((bf16[256,1536]{1,0:T(8,128)(2,1)}), bf16[2048,1536]{1,0:T(8,128)(2,1)}) %all-gather.8.cloned.1.call-update) | async-done | bytes 6291472 | tf_op jit(solution)/shard_map/all_gather | solution.py:131
  279.4 9.3 %fusion.63 = f32[2048,576]{0,1:T(8,128)} fusion(bf16[2048,1536]{1,0:T(8,128)(2,1)} %all-gather.8.cloned.1.call-done, bf16[1536,576]{1,0:T(8,128)(2,1)} %all-gather.10.cloned.1.call-done), kind=kOutput, calls=%fused_computation.133 | convolution fusion | flops 3623878656 | bytes 12779520 | tf_op jit(solution)/shard_map/dot_general | solution.py:137
  288.8 36.4 %all-gather.14.cloned.1.call-done = bf16[1536,576]{1,0:T(8,128)(2,1)} async-done(((bf16[96,576]{1,0:T(8,128)(2,1)}), bf16[1536,576]{1,0:T(8,128)(2,1)}) %all-gather.14.cloned.1.call-update) | async-done | bytes 1769488 | tf_op jit(solution)/shard_map/all_gather | solution.py:135
  325.2 46.1 %all-gather.12.cloned.1.call-done = bf16[1536,576]{1,0:T(8,128)(2,1)} async-done(((bf16[96,576]{1,0:T(8,128)(2,1)}), bf16[1536,576]{1,0:T(8,128)(2,1)}) %all-gather.12.cloned.1.call-update) | async-done | bytes 1769488 | tf_op jit(solution)/shard_map/all_gather | solution.py:134
  371.2 15.6 %convolution_convert_fusion = bf16[2048,1536]{1,0:T(8,128)(2,1)} fusion(bf16[1536,576]{1,0:T(8,128)(2,1)} %all-gather.14.cloned.1.call-done, f32[2048,576]{0,1:T(8,128)} %fusion.63, bf16[2048,1536]{1,0:T(8,128)(2,1)} %all-gather.8.cloned.1.call-done, bf16[1536,576]{1,0:T(8,128)(2,1)} %all-gather.12.cloned.1.call-done), kind=kOutput, calls=%fused_computation.16 | convolution fusion | flops 7262699520 | bytes 20840448 | tf_op jit(solution)/shard_map/dot_general | solution.py:141
  386.8 0.0 reduce-scatter.2.cloned.1.call-update
  386.8 42.0 %reduce-scatter.2.cloned.1.call-done = bf16[256,1536]{1,0:T(8,128)(2,1)} async-done(((bf16[2048,1536]{1,0:T(8,128)(2,1)}), bf16[256,1536]{1,0:T(8,128)(2,1)}) %reduce-scatter.2.cloned.1.call-update) | async-done | bytes 786448 | tf_op jit(solution)/shard_map/reduce_scatter | solution.py:140
  428.9 2.2 add_convert_fusion
  (40 shorter events, 0.3 us)
Async XLA Ops:
  6.5 7.2 %copy-start = (bf16[1536,256]{1,0:T(8,128)(2,1)S(1)}, bf16[1536,256]{1,0:T(8,128)(2,1)}, u32[]{:S(2)}) copy-start(bf16[1536,256]{1,0:T(8,128)(2,1)} %param.17) | copy-start | bytes 2359300
  6.5 15.3 %copy-start.8 = (s32[16]{0:T(128)S(1)}, s32[16]{0:T(128)}, u32[]{:S(2)}) copy-start(s32[16]{0:T(128)} %param.25) | copy-start | bytes 196
  6.5 14.7 %copy-start.2 = (s32[128]{0:T(128)S(1)}, s32[128]{0:T(128)}, u32[]{:S(2)}) copy-start(s32[128]{0:T(128)} %param.26) | copy-start | bytes 1540
  6.5 55.8 %all-gather.6.cloned.1.call-start = ((), (), s32[]{:S(2)}) async-start(), calls=%async_computation.2 | async-start | bytes 1179648 | tf_op jit(solution)/shard_map/all_gather | solution.py:99
  38.8 10.0 %copy-start.3 = (bf16[256,1536]{1,0:T(8,128)(2,1)S(1)}, bf16[256,1536]{1,0:T(8,128)(2,1)}, u32[]{:S(2)}) copy-start(bf16[256,1536]{1,0:T(8,128)(2,1)} %param.14) | copy-start | bytes 2359300
  38.8 10.0 %copy-start.9 = (f32[1536]{0:T(1024)S(1)}, f32[1536]{0:T(1024)}, u32[]{:S(2)}) copy-start(f32[1536]{0:T(1024)} %param.15) | copy-start | bytes 18436
  38.8 156.1 %all-to-all-start = ((bf16[16,2,512,256]{3,2,1,0:T(8,128)(2,1)}), bf16[16,2,512,256]{3,2,1,0:T(8,128)(2,1)}, u32[]{:S(2)}, u32[]{:S(2)}) async-start(bf16[16,2,512,256]{3,2,1,0:T(8,128)(2,1)} %copy.33), calls=%async_computation | async-start | bytes 16777216 | tf_op jit(solution)/shard_map/all_to_all | solution.py:118
  47.7 187.0 %all-gather.10.cloned.1.call-start = ((), (), s32[]{:S(2)}) async-start(), calls=%async_computation.4 | async-start | bytes 2088960 | tf_op jit(solution)/shard_map/all_gather | solution.py:133
  48.4 231.0 %all-gather.8.cloned.1.call-start = ((), (), s32[]{:S(2)}) async-start(), calls=%async_computation.3 | async-start | bytes 7077888 | tf_op jit(solution)/shard_map/all_gather | solution.py:131
  74.2 11.4 %copy-start.5 = (bf16[2048,256]{0,1:T(8,128)(2,1)S(1)}, bf16[2048,256]{0,1:T(8,128)(2,1)}, u32[]{:S(2)}) copy-start(bf16[2048,256]{0,1:T(8,128)(2,1)} %all-gather.6.cloned.1.call-done) | copy-start | bytes 3145732
  97.3 106.0 %copy-start.6 = (bf16[1,512,256]{2,1,0:T(8,128)(2,1)S(1)}, bf16[1,512,256]{2,1,0:T(8,128)(2,1)}, u32[]{:S(2)}) copy-start(bf16[1,512,256]{2,1,0:T(8,128)(2,1)} %param.24) | copy-start | bytes 786436
  211.5 19.3 %slice-start = ((s8[4718592]{0:T(1024)(128)(4,1)}), s8[524288]{0:T(1024)(128)(4,1)S(1)}, s32[]{:S(2)}) async-start(s8[4718592]{0:T(1024)(128)(4,1)} %bitcast.58), calls=%async_computation.8 | async-start | bytes 1048576
  222.0 8.8 %slice-start.1 = ((s8[4718592]{0:T(1024)(128)(4,1)}), s8[4194304]{0:T(1024)(128)(4,1)S(1)}, s32[]{:S(2)}) async-start(s8[4718592]{0:T(1024)(128)(4,1)} %bitcast.58), calls=%async_computation.9 | async-start | bytes 8388608
  222.0 8.8 %copy-start.4 = (bf16[256,1536]{1,0:T(8,128)(2,1)S(1)}, bf16[256,1536]{1,0:T(8,128)(2,1)}, u32[]{:S(2)}) copy-start(bf16[256,1536]{1,0:T(8,128)(2,1)} %param.14) | copy-start | bytes 2359300
  230.8 1.5 copy-start.7
  233.4 91.7 %all-gather.14.cloned.1.call-start = ((), (), s32[]{:S(2)}) async-start(), calls=%async_computation.6 | async-start | bytes 2088960 | tf_op jit(solution)/shard_map/all_gather | solution.py:135
  234.0 137.2 %all-gather.12.cloned.1.call-start = ((), (), s32[]{:S(2)}) async-start(), calls=%async_computation.5 | async-start | bytes 2088960 | tf_op jit(solution)/shard_map/all_gather | solution.py:134
  234.6 194.3 %reduce-scatter.2.cloned.1.call-start = ((), (), s32[]{:S(2)}) async-start(), calls=%async_computation.7 | async-start | bytes 7077888 | tf_op jit(solution)/shard_map/reduce_scatter | solution.py:140
  386.8 44.3 %copy-start.1 = (bf16[1536,256]{1,0:T(8,128)(2,1)S(1)}, bf16[1536,256]{1,0:T(8,128)(2,1)}, u32[]{:S(2)}) copy-start(bf16[1536,256]{1,0:T(8,128)(2,1)} %param.17) | copy-start | bytes 2359300
Sparse Core Ops, SparseCore 0:
  20.7 26.9 all-gather.5
  50.7 139.0 all-gather.9
  233.6 45.8 all-gather.7
  281.5 43.6 all-gather.13
  327.2 43.9 all-gather.11
  387.0 41.8 reduce-scatter.1
where the time goes:
time: 444 us; the launch traced here: 438 us
  waiting for transfers between devices  269 us (61%)
  matrix products  88.4 us (20%)
  other arithmetic  35 us (8%)
  between operations  19.9 us (4%)
  local copies, waits for them, and re-layouts  16.9 us (4%)
  starting transfers between devices  9.38 us (2%)
    all_to_all x1, waiting for transfers between devices, body(): lax.all_to_all(outgoing, 'req', split_axis=0, concat_axis=0, tiled=True)  97.6 us
    all_gather x1, waiting for transfers between devices, body(): lax.all_gather(w_up, 'req', axis=0, tiled=True)  46.1 us
    all_gather x1, waiting for transfers between devices, body(): all_rows = lax.all_gather(ffn_in, 'mlp', axis=0, tiled=True)  44.8 us
    reduce_scatter x1, waiting for transfers between devices, body(): lax.psum_scatter(lax.dot_general(hidden, down_full, (((1,), (1,)), ((), (...  42 us
    all_gather x1, waiting for transfers between devices, body(): lax.all_gather(w_down, 'req', axis=0, tiled=True)  36.4 us
    reduce_sum x2, other arithmetic, attend(): return (top, jnp.sum(weights, axis=-1), mixed)  21.8 us
    dot_general x2, matrix products, attend(): jnp.einsum('thk,kd->thd', weights.astype(jnp.bfloat16), piece[:, HD:], pr...  20.5 us
    dot_general x2, matrix products, attend(): jnp.einsum('thd,kd->thk', queries, piece[:, :HD], preferred_element_type=...  19.9 us
  transfers between devices with their start and end apart: 7, of which 5 were waited for; matrix products, arithmetic and copies ran while one was open for 26% of the time, Pallas kernels for 0%

commit v1 on v0

v1 whole, which is shorter than its diff:
```python
import jax
import jax.numpy as jnp
from jax import lax
from jax.sharding import PartitionSpec as P

HEADS = 12
HD = 128
WINDOW = 1024


EPS = 1e-06


def rms_scale(values, gain):
    wide = values.astype(jnp.float32)
    return wide * lax.rsqrt(jnp.mean(wide * wide, axis=-1, keepdims=True) + EPS) * gain


def rotate(values, where_at):
    half_dim = values.shape[-1] // 2
    freqs = 10000.0 ** (-jnp.arange(half_dim, dtype=jnp.float32) / half_dim)
    angles = where_at.astype(jnp.float32)[:, None] * freqs[None, :]
    cosine = jnp.cos(angles)[:, None, :]
    sine = jnp.sin(angles)[:, None, :]
    first = values[..., :half_dim]
    second = values[..., half_dim:]
    return jnp.concatenate([first * cosine - second * sine, first * sine + second * cosine], -1)


def body(
    tokens,
    attn_gain,
    w_query,
    w_keyval,
    w_out,
    ffn_gain,
    w_gate,
    w_up,
    w_down,
    prefix_kv,
    own_prefix,
    leaf_parent,
    node_parent,
    seg_lengths,
):
    tok_rows = tokens.shape[0]
    mine = lax.axis_index("req")
    n_mlp = lax.axis_size("mlp")
    position_group = lax.axis_index("mlp")
    node_dev = prefix_kv.shape[1]
    seg_slot = prefix_kv.shape[2]
    share = seg_slot // n_mlp
    leaf = leaf_parent[mine]
    upper = node_parent[leaf]
    len_zero = seg_lengths[0, upper]
    len_one = seg_lengths[1, leaf]
    len_two = seg_lengths[2, mine]
    total = len_zero + len_one + len_two

    ff_cols = w_gate.shape[1]
    packed = lax.all_gather(
        jnp.concatenate([w_gate, w_up, w_down], 1), "req", axis=0, tiled=True
    )
    gate_full = packed[:, :ff_cols]
    up_full = packed[:, ff_cols : 2 * ff_cols]
    down_full = packed[:, 2 * ff_cols :]

    level_zero = node_parent[leaf_parent]
    wanted = jnp.stack([level_zero, leaf_parent], 1)
    local_slot = wanted % node_dev
    my_rows = lax.dynamic_slice_in_dim(prefix_kv, position_group * share, share, 2)
    outgoing = my_rows[jnp.arange(2)[None, :], local_slot]
    arrived = lax.all_to_all(outgoing, "req", split_axis=0, concat_axis=0, tiled=True)
    owners = wanted[mine] // node_dev
    my_part = arrived[owners, jnp.arange(2)]
    levels = lax.all_gather(my_part, "mlp", axis=1, tiled=True)

    query_at = total + position_group * tok_rows + jnp.arange(tok_rows, dtype=jnp.int32)
    normed = rms_scale(tokens, attn_gain).astype(jnp.bfloat16)
    query_full = jnp.dot(normed, w_query, preferred_element_type=jnp.float32).reshape(
        tok_rows, HEADS, HD
    )
    queries = (rotate(query_full, query_at) * HD ** (-0.5)).astype(jnp.bfloat16)
    keyval_full = jnp.dot(normed, w_keyval, preferred_element_type=jnp.float32)
    new_keys = rotate(keyval_full[:, None, :HD], query_at)[:, 0].astype(jnp.bfloat16)
    new_vals = keyval_full[:, HD:].astype(jnp.bfloat16)
    new_keyval = jnp.concatenate([new_keys, new_vals], 1)
    piece = lax.all_gather(new_keyval, "mlp", axis=0, tiled=True)

    seq_len = 3 * seg_slot + piece.shape[0]
    seq = jnp.zeros((seq_len, piece.shape[1]), jnp.bfloat16)
    seq = lax.dynamic_update_slice(seq, levels[0], (0, 0))
    seq = lax.dynamic_update_slice(seq, levels[1], (len_zero, 0))
    seq = lax.dynamic_update_slice(seq, own_prefix[0], (len_zero + len_one, 0))
    seq = lax.dynamic_update_slice(seq, piece, (total, 0))
    span = WINDOW + tok_rows
    first = jnp.clip(total + position_group * tok_rows - WINDOW, 0, seq_len - span)
    window = lax.dynamic_slice_in_dim(seq, first, span, 0)
    key_at = first + jnp.arange(span, dtype=jnp.int32)
    spacing = query_at[:, None] - key_at[None, :]
    allowed = ((spacing >= 0) & (spacing < WINDOW))[:, None, :]
    scores = jnp.einsum(
        "thd,kd->thk", queries, window[:, :HD], preferred_element_type=jnp.float32
    )
    top = jnp.max(jnp.where(allowed, scores, -jnp.inf), axis=-1, keepdims=True)
    weights = jnp.where(allowed, jnp.exp(scores - top), 0.0)
    denom = jnp.sum(weights, axis=-1)
    mixed = jnp.einsum(
        "thk,kd->thd",
        weights.astype(jnp.bfloat16),
        window[:, HD:],
        preferred_element_type=jnp.float32,
    )
    context = (mixed / denom[..., None]).reshape(tok_rows, HEADS * HD).astype(jnp.bfloat16)
    attn_out = jnp.dot(context, w_out, preferred_element_type=jnp.float32)
    resid = (tokens.astype(jnp.float32) + attn_out).astype(jnp.bfloat16)
    ffn_in = rms_scale(resid, ffn_gain).astype(jnp.bfloat16)
    all_rows = lax.all_gather(ffn_in, "mlp", axis=0, tiled=True)
    gate = jnp.dot(all_rows, gate_full, preferred_element_type=jnp.float32)
    upward = jnp.dot(all_rows, up_full, preferred_element_type=jnp.float32)
    hidden = (jax.nn.gelu(gate, approximate=True) * upward).astype(jnp.bfloat16)
    summed = lax.psum_scatter(
        lax.dot_general(
            hidden, down_full, (((1,), (1,)), ((), ())), preferred_element_type=jnp.float32
        ).astype(jnp.bfloat16),
        "mlp",
        scatter_dimension=0,
        tiled=True,
    ).astype(jnp.float32)
    return (resid.astype(jnp.float32) + summed).astype(jnp.bfloat16)


def solution(mesh):
    return jax.shard_map(
        body,
        mesh=mesh,
        in_specs=(
            P(("req", "mlp"), None),
            P(),
            P(),
            P(),
            P(),
            P(),
            P("req", "mlp"),
            P("req", "mlp"),
            P("req", "mlp"),
            P(None, "req", None, None),
            P("req", None, None),
            P(),
            P(),
            P(),
        ),
        out_specs=P(("req", "mlp"), None),
        check_vma=False,
    )
```

time: 444 us -> 226 us (0.51); the launches traced: 438 us -> 225 us
  waiting for transfers between devices: 269 us -> 89.5 us
  matrix products: 88.4 us -> 51.5 us
  other arithmetic: 35 us -> 10.9 us
  blocking collectives: 0 us -> 16.2 us
  local copies, waits for them, and re-layouts: 16.9 us -> 26.9 us
    all_to_all x1, waiting for transfers between devices: 97.6 us -> 0.01 us  [body(): lax.all_to_all(outgoing, 'req', split_axis=0, concat_axis=0, tiled=True)]
    all_gather x3 -> x1, waiting for transfers between devices: 82.5 us -> 5.09 us  [body(): lax.all_gather(jnp.concatenate([w_gate, w_up, w_down], 1), 'req', axis=0,...]
    dot_general x6 -> x2, matrix products: 55.9 us -> 14 us  [the longest x1 7.81 us: body(): upward = jnp.dot(all_rows, up_full, preferred_element_type=jnp.float32)]
    reduce_sum x2 -> x0, other arithmetic: 21.8 us -> none  [attend(): return (top, jnp.sum(weights, axis=-1), mixed)]
    all_gather x0 -> x1, blocking collectives: none -> 16.2 us  [body(): levels = lax.all_gather(my_part, 'mlp', axis=1, tiled=True)]
    sub x0 -> x1, matrix products: none -> 10.7 us  [body(): weights = jnp.where(allowed, jnp.exp(scores - top), 0.0)]
    dynamic_update_slice x0 -> x4, local copies, waits for them, and re-layouts: none -> 10.1 us  [the longest x1 6.18 us: body(): seq = lax.dynamic_update_slice(seq, piece, (total, 0))]
    convert_element_type x1 -> x0, local copies, waits for them, and re-layouts: 9.64 us -> none  [body(): outgoing = jnp.einsum('rln,lnsc->rlsc', picker, prefix_kv, preferred_elem...]
  transfers between devices with their start and end apart: 7 -> 5, of which waited for: 5 -> 3; matrix products, arithmetic and copies ran while one was open for 26% -> 24% of each run, Pallas kernels for 0% -> 0%
where the time goes in v1:
time: 226 us; the launch traced here: 225 us
  waiting for transfers between devices  89.5 us (40%)
  matrix products  51.5 us (23%)
  local copies, waits for them, and re-layouts  26.9 us (12%)
  between operations  21.1 us (9%)
  blocking collectives  16.2 us (7%)
  other arithmetic  10.9 us (5%)
  starting transfers between devices  9 us (4%)
    all_gather x1, waiting for transfers between devices, body(): all_rows = lax.all_gather(ffn_in, 'mlp', axis=0, tiled=True)  42.6 us
    reduce_scatter x1, waiting for transfers between devices, body(): lax.psum_scatter(lax.dot_general(hidden, down_full, (((1,), (1,)), ((), (...  41.7 us
    all_gather x1, blocking collectives, body(): levels = lax.all_gather(my_part, 'mlp', axis=1, tiled=True)  16.2 us
    sub x1, matrix products, body(): weights = jnp.where(allowed, jnp.exp(scores - top), 0.0)  10.7 us
    dot_general x1, matrix products, body(): gate = jnp.dot(all_rows, gate_full, preferred_element_type=jnp.float32)  9.5 us
    all_to_all x1, starting transfers between devices, body(): lax.all_to_all(outgoing, 'req', split_axis=0, concat_axis=0, tiled=True)  8.65 us
    dot_general x1, matrix products, body(): upward = jnp.dot(all_rows, up_full, preferred_element_type=jnp.float32)  7.81 us
    dot_general x1, matrix products, body(): lax.dot_general(hidden, down_full, (((1,), (1,)), ((), ())), preferred_el...  7.2 us
  transfers between devices with their start and end apart: 5, of which 3 were waited for; matrix products, arithmetic and copies ran while one was open for 24% of the time, Pallas kernels for 0%

profile of v1, /device:TPU:1, one launch (start us, length us, event | category | flops | bytes accessed | tf_op | source)
XLA Modules:
  0.0 225.0 jit_solution(15433072898862234801)
XLA Ops:
  6.5 0.0 copy-start
  6.5 0.0 all-gather.4.cloned.1.call-start
  6.5 1.3 dynamic_slice.24
  9.8 1.2 dynamic_slice.25
  12.4 1.4 fusion.25
  13.7 0.0 copy-start.8
  13.7 0.0 copy-start.9
  13.8 0.0 copy-done
  13.8 0.0 copy-start.11
  13.8 0.0 copy-start.2
  13.8 1.8 fusion.33
  16.3 0.0 copy-done.12
  16.3 0.7 constant_dynamic-slice_fusion.2
  18.8 0.3 fusion.42
  19.2 0.7 pad_maximum_fusion
  19.9 0.0 all-gather.4.cloned.1.call-update
  19.9 0.0 all-gather.8.cloned.1.call-start
  20.0 0.9 concatenate.43
  20.9 0.0 all-gather.8.cloned.1.call-update
  20.9 0.0 copy-done.2
  20.9 0.7 gather_fusion
  21.6 0.1 copy.23
  21.7 0.1 reshape.371
  21.8 1.1 constant_dynamic-slice_fusion
  22.9 0.0 copy-start.3
  22.9 0.0 copy-start.15
  22.9 1.6 gather_fusion.1
  24.5 8.6 %all-to-all-start = ((bf16[16,2,64,256]{3,2,1,0:T(8,128)(2,1)}), bf16[16,2,64,256]{3,2,1,0:T(8,128)(2,1)}, u32[]{:S(2)}, u32[]{:S(2)}) async-start(bf16[16,2,64,256]{3,2,1,0:T(8,128)(2,1)} %bitcast.8), calls=%async_computation | async-start | bytes 2097152 | tf_op jit(solution)/shard_map/all_to_all | solution.py:73
  33.2 0.0 all-gather.6.cloned.1.call-start
  33.2 0.2 dynamic-slice_reduce_fusion
  33.4 0.5 multiply_cosine_fusion
  34.0 4.4 %fusion.35 = f32[256,1536]{0,1:T(8,128)S(1)} fusion(bf16[1536,1536]{1,0:T(8,128)(2,1)} %param.16, bf16[256,1536]{1,0:T(8,128)(2,1)S(1)} %copy-done.3, f32[1536]{0:T(1024)S(1)} %copy-done.15, f32[256]{0:T(256)S(1)} %add_rsqrt_fusion.1), kind=kOutput, calls=%fused_computation.52 | convolution fusion | flops 1209532416 | bytes 7085056 | tf_op jit(solution)/shard_map/dot_general | solution.py:80
  38.4 1.0 fusion.59
  40.7 1.6 copy.29
  42.3 1.7 copy.30
  44.6 3.5 %multiply_subtract_fusion = (f32[256,12,64]{2,0,1:T(8,128)}, f32[256,12,64]{2,0,1:T(8,128)}) fusion(f32[256,12,64]{2,0,1:T(8,128)} %copy.30, f32[256,12,64]{2,0,1:T(8,128)S(1)} %copy.29, f32[256,64]{1,0:T(8,128)S(1)} %get-tuple-element.17, f32[256,64]{1,0:T(8,128)S(1)} %get-tuple-element.16), kind=kLoop, calls=%fused_computation.44 | loop fusion | flops 1179648 | bytes 3276800 | tf_op jit(solution)/shard_map/sub | solution.py:27
  48.1 1.1 fusion.31
  49.1 0.0 all-to-all-done
  49.1 1.8 gather_fusion.2
  50.9 16.2 %all_gather.12 = bf16[2,512,256]{2,1,0:T(8,128)(2,1)S(1)} all-gather(bf16[2,64,256]{2,1,0:T(8,128)(2,1)S(1)} %gather_fusion.2), channel_id=1, replica_groups=mesh['req'=16,'mlp'=8] {'mlp'}, dimensions={1}, use_global_device_ids=true | all-gather | bytes 589824 | tf_op jit(solution)/shard_map/all_gather | solution.py:76
  67.2 0.1 dynamic_update_slice.12
  67.3 1.9 dynamic_update_slice.13
  69.2 0.0 copy-done.6
  69.2 1.9 dynamic_update_slice.14
  71.1 0.0 copy-start.4
  71.1 1.2 copy-done.4
  72.3 1.6 copy.24
  73.9 6.2 %dynamic_update_slice.15 = bf16[3584,256]{1,0:T(8,128)(2,1)} dynamic-update-slice(bf16[3584,256]{1,0:T(8,128)(2,1)} %copy-done.4, bf16[2048,256]{1,0:T(8,128)(2,1)S(1)} %copy.24, s32[]{:T(128)S(6)} %select_n.97, s32[]{:T(128)} %constant.31.clone.1) | dynamic-update-slice | bytes 2097156 | tf_op jit(solution)/shard_map/dynamic_update_slice | solution.py:95
  80.1 10.7 %fusion.60 = (f32[256,12]{0,1:T(8,128)S(1)}, bf16[256,12,1280]{2,0,1:T(8,128)(2,1)}) fusion(pred[256,1280]{1,0:T(8,128)(4,1)} %fusion.31, bf16[3584,256]{1,0:T(8,128)(2,1)} %dynamic_update_slice.15, s32[]{:T(128)S(6)} %min.4, f32[256,12,64]{2,0,1:T(8,128)} %get-tuple-element.6, f32[256,12,64]{2,0,1:T(8,128)S(1)} %copy-done.5), kind=kOutput, calls=%fused_computation.105 | convolution fusion | flops 2035287296 | bytes 15479808 | tf_op jit(solution)/shard_map/sub | solution.py:106
  90.8 6.2 %divide_convert_fusion = bf16[256,12,128]{0,2,1:T(8,128)(2,1)S(1)} fusion(bf16[256,12,1280]{2,0,1:T(8,128)(2,1)} %get-tuple-element.19, f32[256,12]{0,1:T(8,128)S(1)} %get-tuple-element.18, bf16[3584,256]{1,0:T(8,128)(2,1)} %dynamic_update_slice.15, s32[]{:T(128)S(6)} %min.4, s32[]{:T(128)S(6)} %add.181), kind=kOutput, calls=%fused_computation.42 | convolution fusion | flops 1007419392 | bytes 8990728 | tf_op jit(solution)/shard_map/thk,kd->thd/dot_general | solution.py:108
  97.0 0.0 copy-start.10
  97.1 3.9 %multiply_reduce_fusion = (f32[256]{0:T(256)S(1)}, f32[256,1536]{1,0:T(8,128)S(1)}) fusion(bf16[256,1536]{0,1:T(8,128)(2,1)S(1)} %bitcast.58, bf16[1536,1536]{1,0:T(8,128)(2,1)} %param.18, bf16[256,1536]{1,0:T(8,128)(2,1)S(1)} %copy-done.3), kind=kOutput, calls=%fused_computation.41 | convolution fusion | flops 1210318592 | bytes 7865344 | tf_op jit(solution)/shard_map/dot_general | solution.py:115
  101.0 1.1 multiply_convert_fusion
  102.1 0.0 all-gather.6.cloned.1.call-update
  102.1 0.3 reduce-scatter.2.cloned.1.call-start
  102.4 5.1 %all-gather.8.cloned.1.call-done = bf16[1536,1728]{1,0:T(8,128)(2,1)} async-done(((bf16[96,1728]{1,0:T(8,128)(2,1)}), bf16[1536,1728]{1,0:T(8,128)(2,1)}) %all-gather.8.cloned.1.call-update) | async-done | bytes 5308432 | tf_op jit(solution)/shard_map/all_gather | solution.py:61
  107.4 42.6 %all-gather.6.cloned.1.call-done = bf16[2048,1536]{1,0:T(8,128)(2,1)} async-done(((bf16[256,1536]{1,0:T(8,128)(2,1)}), bf16[2048,1536]{1,0:T(8,128)(2,1)}) %all-gather.6.cloned.1.call-update) | async-done | bytes 6291472 | tf_op jit(solution)/shard_map/all_gather | solution.py:118
  150.0 9.5 %fusion.23 = f32[2048,576]{0,1:T(8,128)} fusion(bf16[2048,1536]{1,0:T(8,128)(2,1)} %all-gather.6.cloned.1.call-done, bf16[1536,1728]{1,0:T(8,128)(2,1)} %all-gather.8.cloned.1.call-done), kind=kOutput, calls=%fused_computation.30 | convolution fusion | flops 3623878656 | bytes 12976128 | tf_op jit(solution)/shard_map/dot_general | solution.py:119
  159.6 7.8 %fusion.16 = bf16[2048,576]{0,1:T(8,128)(2,1)S(1)} fusion(f32[2048,576]{0,1:T(8,128)} %fusion.23, bf16[2048,1536]{1,0:T(8,128)(2,1)S(1)} %copy-done.13, bf16[1536,1728]{1,0:T(8,128)(2,1)S(1)} %copy-done.14), kind=kOutput, calls=%fused_computation.21 | convolution fusion | flops 3635675136 | bytes 15335424 | tf_op jit(solution)/shard_map/dot_general | solution.py:120
  167.4 7.2 %convolution_convert_fusion = bf16[2048,1536]{1,0:T(8,128)(2,1)} fusion(bf16[2048,576]{0,1:T(8,128)(2,1)S(1)} %fusion.16, bf16[1536,1728]{1,0:T(8,128)(2,1)S(1)} %copy-done.14), kind=kOutput, calls=%fused_computation.11 | convolution fusion | flops 3627024384 | bytes 10616832 | tf_op jit(solution)/shard_map/dot_general | solution.py:123
  174.6 0.0 reduce-scatter.2.cloned.1.call-update
  174.6 0.0 copy-start.1
  174.6 41.7 %reduce-scatter.2.cloned.1.call-done = bf16[256,1536]{1,0:T(8,128)(2,1)} async-done(((bf16[2048,1536]{1,0:T(8,128)(2,1)}), bf16[256,1536]{1,0:T(8,128)(2,1)}) %reduce-scatter.2.cloned.1.call-update) | async-done | bytes 786448 | tf_op jit(solution)/shard_map/reduce_scatter | solution.py:122
  216.3 2.2 add_convert_fusion
  (33 shorter events, 0.2 us)
Async XLA Ops:
  6.5 7.2 %copy-start = (bf16[1536,256]{1,0:T(8,128)(2,1)S(1)}, bf16[1536,256]{1,0:T(8,128)(2,1)}, u32[]{:S(2)}) copy-start(bf16[1536,256]{1,0:T(8,128)(2,1)} %param.17) | copy-start | bytes 2359300
  6.5 9.8 %copy-start.12 = (s32[3,128]{1,0:T(4,128)S(1)}, s32[3,128]{1,0:T(4,128)}, u32[]{:S(2)}) copy-start(s32[3,128]{1,0:T(4,128)} %param.27) | copy-start | bytes 4612
  6.5 65.8 %all-gather.4.cloned.1.call-start = ((), (), s32[]{:S(2)}) async-start(), calls=%async_computation.2 | async-start | bytes 1179648 | tf_op jit(solution)/shard_map/all_gather | solution.py:88
  13.7 6.2 %copy-start.7 = (bf16[96,576]{1,0:T(8,128)(2,1)S(1)}, bf16[96,576]{1,0:T(8,128)(2,1)}, u32[]{:S(2)}) copy-start(bf16[96,576]{1,0:T(8,128)(2,1)} %param.20) | copy-start | bytes 331780
  13.7 6.2 %copy-start.8 = (bf16[96,576]{1,0:T(8,128)(2,1)S(1)}, bf16[96,576]{1,0:T(8,128)(2,1)}, u32[]{:S(2)}) copy-start(bf16[96,576]{1,0:T(8,128)(2,1)} %param.21) | copy-start | bytes 331780
  13.7 6.2 %copy-start.9 = (bf16[96,576]{1,0:T(8,128)(2,1)S(1)}, bf16[96,576]{1,0:T(8,128)(2,1)}, u32[]{:S(2)}) copy-start(bf16[96,576]{1,0:T(8,128)(2,1)} %param.22) | copy-start | bytes 331780
  13.8 7.1 %copy-start.11 = (s32[16]{0:T(128)S(1)}, s32[16]{0:T(128)}, u32[]{:S(2)}) copy-start(s32[16]{0:T(128)} %param.25) | copy-start | bytes 196
  13.8 7.1 %copy-start.2 = (s32[128]{0:T(128)S(1)}, s32[128]{0:T(128)}, u32[]{:S(2)}) copy-start(s32[128]{0:T(128)} %param.26) | copy-start | bytes 1540
  19.9 87.6 %all-gather.8.cloned.1.call-start = ((), (), s32[]{:S(2)}) async-start(), calls=%async_computation.4 | async-start | bytes 5849088 | tf_op jit(solution)/shard_map/all_gather | solution.py:61
  22.9 11.1 %copy-start.3 = (bf16[256,1536]{1,0:T(8,128)(2,1)S(1)}, bf16[256,1536]{1,0:T(8,128)(2,1)}, u32[]{:S(2)}) copy-start(bf16[256,1536]{1,0:T(8,128)(2,1)} %param.14) | copy-start | bytes 2359300
  22.9 11.1 %copy-start.15 = (f32[1536]{0:T(1024)S(1)}, f32[1536]{0:T(1024)}, u32[]{:S(2)}) copy-start(f32[1536]{0:T(1024)} %param.15) | copy-start | bytes 18436
  24.5 24.6 %all-to-all-start = ((bf16[16,2,64,256]{3,2,1,0:T(8,128)(2,1)}), bf16[16,2,64,256]{3,2,1,0:T(8,128)(2,1)}, u32[]{:S(2)}, u32[]{:S(2)}) async-start(bf16[16,2,64,256]{3,2,1,0:T(8,128)(2,1)} %bitcast.8), calls=%async_computation | async-start | bytes 2097152 | tf_op jit(solution)/shard_map/all_to_all | solution.py:73
  33.2 116.9 %all-gather.6.cloned.1.call-start = ((), (), s32[]{:S(2)}) async-start(), calls=%async_computation.3 | async-start | bytes 7077888 | tf_op jit(solution)/shard_map/all_gather | solution.py:118
  67.1 2.1 copy-start.6
  71.1 1.2 copy-start.4
  72.3 7.8 %copy-start.5 = (f32[256,12,64]{2,0,1:T(8,128)S(1)}, f32[256,12,64]{2,0,1:T(8,128)}, u32[]{:S(2)}) copy-start(f32[256,12,64]{2,0,1:T(8,128)} %get-tuple-element.5) | copy-start | bytes 2359300
  97.0 3.9 %copy-start.10 = (f32[1536]{0:T(1024)S(1)}, f32[1536]{0:T(1024)}, u32[]{:S(2)}) copy-start(f32[1536]{0:T(1024)} %param.19) | copy-start | bytes 18436
  102.1 114.2 %reduce-scatter.2.cloned.1.call-start = ((), (), s32[]{:S(2)}) async-start(), calls=%async_computation.5 | async-start | bytes 7077888 | tf_op jit(solution)/shard_map/reduce_scatter | solution.py:122
  150.0 9.5 %copy-start.13 = (bf16[2048,1536]{1,0:T(8,128)(2,1)S(1)}, bf16[2048,1536]{1,0:T(8,128)(2,1)}, u32[]{:S(2)}) copy-start(bf16[2048,1536]{1,0:T(8,128)(2,1)} %all-gather.6.cloned.1.call-done) | copy-start | bytes 18874372
  150.0 9.5 %copy-start.14 = (bf16[1536,1728]{1,0:T(8,128)(2,1)S(1)}, bf16[1536,1728]{1,0:T(8,128)(2,1)}, u32[]{:S(2)}) copy-start(bf16[1536,1728]{1,0:T(8,128)(2,1)} %all-gather.8.cloned.1.call-done) | copy-start | bytes 15925252
  174.6 43.9 %copy-start.1 = (bf16[1536,256]{1,0:T(8,128)(2,1)S(1)}, bf16[1536,256]{1,0:T(8,128)(2,1)}, u32[]{:S(2)}) copy-start(bf16[1536,256]{1,0:T(8,128)(2,1)} %param.17) | copy-start | bytes 2359300
Sparse Core Ops, SparseCore 0:
  20.0 26.9 all-gather.3
  49.2 58.2 all-gather.7
  109.1 40.8 all-gather.5
  174.7 41.5 reduce-scatter.1

commit v2 on v1

--- a/solution.py
+++ b/solution.py
@@ -45,8 +45,9 @@
 ):
     tok_rows = tokens.shape[0]
     mine = lax.axis_index("req")
-    n_mlp = lax.axis_size("mlp")
-    position_group = lax.axis_index("mlp")
+    n_core = lax.axis_size("core")
+    n_mlp = lax.axis_size("x") * n_core
+    position_group = lax.axis_index("x") * n_core + lax.axis_index("core")
     node_dev = prefix_kv.shape[1]
     seg_slot = prefix_kv.shape[2]
     share = seg_slot // n_mlp
@@ -61,9 +62,6 @@
     packed = lax.all_gather(
         jnp.concatenate([w_gate, w_up, w_down], 1), "req", axis=0, tiled=True
     )
-    gate_full = packed[:, :ff_cols]
-    up_full = packed[:, ff_cols : 2 * ff_cols]
-    down_full = packed[:, 2 * ff_cols :]
 
     level_zero = node_parent[leaf_parent]
     wanted = jnp.stack([level_zero, leaf_parent], 1)
@@ -73,7 +71,9 @@
     arrived = lax.all_to_all(outgoing, "req", split_axis=0, concat_axis=0, tiled=True)
     owners = wanted[mine] // node_dev
     my_part = arrived[owners, jnp.arange(2)]
-    levels = lax.all_gather(my_part, "mlp", axis=1, tiled=True)
+    fanned = jnp.broadcast_to(my_part[None], (n_mlp,) + my_part.shape)
+    levels = lax.all_to_all(fanned, ("x", "core"), split_axis=0, concat_axis=0, tiled=True)
+    levels = jnp.swapaxes(levels, 0, 1).reshape(2, seg_slot, my_part.shape[-1])
 
     query_at = total + position_group * tok_rows + jnp.arange(tok_rows, dtype=jnp.int32)
     normed = rms_scale(tokens, attn_gain).astype(jnp.bfloat16)
@@ -85,7 +85,7 @@
     new_keys = rotate(keyval_full[:, None, :HD], query_at)[:, 0].astype(jnp.bfloat16)
     new_vals = keyval_full[:, HD:].astype(jnp.bfloat16)
     new_keyval = jnp.concatenate([new_keys, new_vals], 1)
-    piece = lax.all_gather(new_keyval, "mlp", axis=0, tiled=True)
+    piece = lax.all_gather(new_keyval, ("x", "core"), axis=0, tiled=True)
 
     seq_len = 3 * seg_slot + piece.shape[0]
     seq = jnp.zeros((seq_len, piece.shape[1]), jnp.bfloat16)
@@ -115,41 +115,46 @@
     attn_out = jnp.dot(context, w_out, preferred_element_type=jnp.float32)
     resid = (tokens.astype(jnp.float32) + attn_out).astype(jnp.bfloat16)
     ffn_in = rms_scale(resid, ffn_gain).astype(jnp.bfloat16)
-    all_rows = lax.all_gather(ffn_in, "mlp", axis=0, tiled=True)
+    ffn_in, packed = lax.optimization_barrier((ffn_in, packed))
+    gate_full = packed[:, :ff_cols]
+    up_full = packed[:, ff_cols : 2 * ff_cols]
+    down_full = packed[:, 2 * ff_cols :]
+    chip_rows = lax.all_gather(ffn_in, "x", axis=0, tiled=True)
+    all_rows = lax.all_gather(chip_rows, "core", axis=0, tiled=True)
     gate = jnp.dot(all_rows, gate_full, preferred_element_type=jnp.float32)
     upward = jnp.dot(all_rows, up_full, preferred_element_type=jnp.float32)
     hidden = (jax.nn.gelu(gate, approximate=True) * upward).astype(jnp.bfloat16)
-    summed = lax.psum_scatter(
-        lax.dot_general(
-            hidden, down_full, (((1,), (1,)), ((), ())), preferred_element_type=jnp.float32
-        ).astype(jnp.bfloat16),
-        "mlp",
-        scatter_dimension=0,
-        tiled=True,
-    ).astype(jnp.float32)
+    partial_down = lax.dot_general(
+        hidden, down_full, (((1,), (1,)), ((), ())), preferred_element_type=jnp.float32
+    ).astype(jnp.bfloat16)
+    pair_sum = lax.psum_scatter(partial_down, "core", scatter_dimension=0, tiled=True)
+    summed = lax.psum_scatter(pair_sum, "x", scatter_dimension=0, tiled=True).astype(jnp.float32)
     return (resid.astype(jnp.float32) + summed).astype(jnp.bfloat16)
 
 
 def solution(mesh):
+    n_req, n_mlp = mesh.devices.shape
+    fine = jax.sharding.Mesh(mesh.devices.reshape(n_req, n_mlp // 2, 2), ("req", "x", "core"))
+    cols = ("x", "core")
     return jax.shard_map(
         body,
-        mesh=mesh,
+        mesh=fine,
         in_specs=(
-            P(("req", "mlp"), None),
+            P(("req", "x", "core"), None),
             P(),
             P(),
             P(),
             P(),
             P(),
-            P("req", "mlp"),
-            P("req", "mlp"),
-            P("req", "mlp"),
+            P("req", cols),
+            P("req", cols),
+            P("req", cols),
             P(None, "req", None, None),
             P("req", None, None),
             P(),
             P(),
             P(),
         ),
-        out_specs=P(("req", "mlp"), None),
+        out_specs=P(("req", "x", "core"), None),
         check_vma=False,
     )

time: 226 us -> 264 us (1.17)
  waiting for transfers between devices: 89.5 us -> 136 us
  blocking collectives: 16.2 us -> 0 us
  starting transfers between devices: 9 us -> 16.5 us
    all_gather x2 -> x3, waiting for transfers between devices: 42.6 us -> 62.1 us  [the longest x1 40.7 us: body(): chip_rows = lax.all_gather(ffn_in, 'x', axis=0, tiled=True)]
    reduce_scatter x1 -> x2, waiting for transfers between devices: 41.7 us -> 60.2 us  [the longest x1 41.6 us: body(): lax.psum_scatter(pair_sum, 'x', scatter_dimension=0, tiled=True)]
    all_gather x1 -> x0, blocking collectives: 16.2 us -> none  [body(): levels = lax.all_gather(my_part, 'mlp', axis=1, tiled=True)]
    all_to_all x0 -> x1, waiting for transfers between devices: none -> 8.39 us  [body(): lax.all_to_all(fanned, ('x', 'core'), split_axis=0, concat_axis=0, tiled=...]
    all_to_all x0 -> x1, starting transfers between devices: none -> 7.44 us  [body(): lax.all_to_all(fanned, ('x', 'core'), split_axis=0, concat_axis=0, tiled=...]
    dot_general x1, matrix products: 9.5 us -> 6.76 us  [body(): gate = jnp.dot(all_rows, gate_full, preferred_element_type=jnp.float32)]
  transfers between devices with their start and end apart: 5 -> 8, of which waited for: 3 -> 7; matrix products, arithmetic and copies ran while one was open for 24% -> 21% of each run, Pallas kernels for 0% -> 0%
where the time goes in v2:
time: 264 us; the launch traced here: 263 us
  waiting for transfers between devices  136 us (52%)
  matrix products  50.2 us (19%)
  local copies, waits for them, and re-layouts  27.7 us (10%)
  between operations  21.8 us (8%)
  starting transfers between devices  16.5 us (6%)
  other arithmetic  10.9 us (4%)
    reduce_scatter x1, waiting for transfers between devices, body(): lax.psum_scatter(pair_sum, 'x', scatter_dimension=0, tiled=True)  41.6 us
    all_gather x1, waiting for transfers between devices, body(): chip_rows = lax.all_gather(ffn_in, 'x', axis=0, tiled=True)  40.7 us
    all_gather x1, waiting for transfers between devices, body(): all_rows = lax.all_gather(chip_rows, 'core', axis=0, tiled=True)  21.3 us
    reduce_scatter x1, waiting for transfers between devices, body(): lax.psum_scatter(partial_down, 'core', scatter_dimension=0, tiled=True)  18.6 us
    sub x1, matrix products, body(): weights = jnp.where(allowed, jnp.exp(scores - top), 0.0)  10.7 us
    all_to_all x1, starting transfers between devices, body(): lax.all_to_all(outgoing, 'req', split_axis=0, concat_axis=0, tiled=True)  8.65 us
    dot_general x1, matrix products, body(): lax.dot_general(hidden, down_full, (((1,), (1,)), ((), ())), preferred_el...  8.64 us
    all_to_all x1, waiting for transfers between devices, body(): lax.all_to_all(fanned, ('x', 'core'), split_axis=0, concat_axis=0, tiled=...  8.39 us
  transfers between devices with their start and end apart: 8, of which 7 were waited for; matrix products, arithmetic and copies ran while one was open for 21% of the time, Pallas kernels for 0%

profile of v2, /device:TPU:1, one launch (start us, length us, event | category | flops | bytes accessed | tf_op | source)
XLA Modules:
  0.0 262.7 jit_solution(6243298992258970621)
XLA Ops:
  6.5 1.3 dynamic_slice.24
  9.8 1.2 dynamic_slice.25
  12.4 1.4 fusion.25
  13.7 0.0 copy-start.8
  13.7 0.0 copy-start.9
  13.8 0.0 copy-start.11
  13.8 0.0 copy-start.2
  13.8 1.8 fusion.33
  16.3 0.7 constant_dynamic-slice_fusion.2
  19.0 0.3 fusion.42
  19.3 0.7 pad_maximum_fusion
  20.0 0.0 all-gather.5.cloned.1.call-update
  20.0 0.0 all-gather.7.cloned.1.call-start
  20.1 0.9 concatenate.43
  21.0 0.0 all-gather.7.cloned.1.call-update
  21.1 0.7 gather_fusion
  21.8 0.1 copy.29
  21.8 0.1 reshape.377
  21.9 1.1 constant_dynamic-slice_fusion
  23.0 0.0 copy-start.3
  23.0 0.0 copy-start.14
  23.0 1.6 gather_fusion.1
  24.7 8.6 %all-to-all-start = ((bf16[16,2,64,256]{3,2,1,0:T(8,128)(2,1)}), bf16[16,2,64,256]{3,2,1,0:T(8,128)(2,1)}, u32[]{:S(2)}, u32[]{:S(2)}) async-start(bf16[16,2,64,256]{3,2,1,0:T(8,128)(2,1)} %bitcast.8), calls=%async_computation | async-start | bytes 2097152 | tf_op jit(solution)/shard_map/all_to_all | solution.py:71
  33.3 4.4 %fusion.35 = f32[256,1536]{0,1:T(8,128)S(1)} fusion(bf16[1536,1536]{1,0:T(8,128)(2,1)} %param.16, bf16[256,1536]{1,0:T(8,128)(2,1)S(1)} %copy-done.3, f32[1536]{0:T(1024)S(1)} %copy-done.14, f32[256]{0:T(256)S(1)} %add_rsqrt_fusion.1), kind=kOutput, calls=%fused_computation.50 | convolution fusion | flops 1209532416 | bytes 7085056 | tf_op jit(solution)/shard_map/dot_general | solution.py:80
  37.7 1.0 fusion.59
  40.2 0.2 dynamic-slice_reduce_fusion
  40.4 1.6 copy.35
  42.0 1.6 copy.36
  44.3 0.5 multiply_cosine_fusion
  44.9 3.5 %multiply_subtract_fusion = (f32[256,12,64]{2,0,1:T(8,128)}, f32[256,12,64]{2,0,1:T(8,128)}) fusion(f32[256,12,64]{2,0,1:T(8,128)} %copy.36, f32[256,12,64]{2,0,1:T(8,128)S(1)} %copy.35, f32[256,64]{1,0:T(8,128)S(1)} %get-tuple-element.21, f32[256,64]{1,0:T(8,128)S(1)} %get-tuple-element.20), kind=kLoop, calls=%fused_computation.44 | loop fusion | flops 1179648 | bytes 3276800 | tf_op jit(solution)/shard_map/sub | solution.py:27
  48.4 0.5 all-to-all-done
  48.9 1.8 gather_fusion.2
  50.7 0.8 broadcast_in_dim.25
  51.5 7.4 %all-to-all-start.1 = ((bf16[8,2,64,256]{3,2,1,0:T(8,128)(2,1)}), bf16[8,2,64,256]{3,2,1,0:T(8,128)(2,1)S(1)}, u32[]{:S(2)}, u32[]{:S(2)}) async-start(bf16[8,2,64,256]{3,2,1,0:T(8,128)(2,1)} %broadcast_in_dim.25), calls=%async_computation.1 | async-start | bytes 1048576 | tf_op jit(solution)/shard_map/all_to_all | solution.py:75
  58.9 1.1 fusion.31
  60.0 8.4 %all-to-all-done.1 = bf16[8,2,64,256]{3,2,1,0:T(8,128)(2,1)S(1)} async-done(((bf16[8,2,64,256]{3,2,1,0:T(8,128)(2,1)}), bf16[8,2,64,256]{3,2,1,0:T(8,128)(2,1)S(1)}, u32[]{:S(2)}, u32[]{:S(2)}) %all-to-all-start.1) | async-done | bytes 524320 | tf_op jit(solution)/shard_map/all_to_all | solution.py:75
  68.5 0.1 dynamic_update_slice.12
  68.6 1.9 dynamic_update_slice.13
  70.5 1.9 dynamic_update_slice.14
  72.4 1.2 copy-done.4
  73.6 1.6 copy.30
  75.2 6.2 %dynamic_update_slice.15 = bf16[3584,256]{1,0:T(8,128)(2,1)} dynamic-update-slice(bf16[3584,256]{1,0:T(8,128)(2,1)} %copy-done.4, bf16[2048,256]{1,0:T(8,128)(2,1)S(1)} %copy.30, s32[]{:T(128)S(6)} %select_n.97, s32[]{:T(128)} %constant.31.clone.1) | dynamic-update-slice | bytes 2097156 | tf_op jit(solution)/shard_map/dynamic_update_slice | solution.py:95
  81.4 10.7 %fusion.61 = (f32[256,12]{0,1:T(8,128)S(1)}, bf16[256,12,1280]{2,0,1:T(8,128)(2,1)}) fusion(pred[256,1280]{1,0:T(8,128)(4,1)} %fusion.31, bf16[3584,256]{1,0:T(8,128)(2,1)} %dynamic_update_slice.15, s32[]{:T(128)S(6)} %min.4, f32[256,12,64]{2,0,1:T(8,128)} %get-tuple-element.10, f32[256,12,64]{2,0,1:T(8,128)S(1)} %copy-done.5), kind=kOutput, calls=%fused_computation.104 | convolution fusion | flops 2035287296 | bytes 15479808 | tf_op jit(solution)/shard_map/sub | solution.py:106
  92.1 6.1 %divide_convert_fusion = bf16[256,12,128]{0,2,1:T(8,128)(2,1)S(1)} fusion(bf16[256,12,1280]{2,0,1:T(8,128)(2,1)} %get-tuple-element.23, f32[256,12]{0,1:T(8,128)S(1)} %get-tuple-element.22, bf16[3584,256]{1,0:T(8,128)(2,1)} %dynamic_update_slice.15, s32[]{:T(128)S(6)} %min.4, s32[]{:T(128)S(6)} %add.187), kind=kOutput, calls=%fused_computation.42 | convolution fusion | flops 1007419392 | bytes 8990728 | tf_op jit(solution)/shard_map/thk,kd->thd/dot_general | solution.py:108
  98.2 0.0 copy-start.10
  98.3 3.9 %multiply_reduce_fusion = (f32[256]{0:T(256)S(1)}, f32[256,1536]{1,0:T(8,128)S(1)}) fusion(bf16[256,1536]{0,1:T(8,128)(2,1)S(1)} %bitcast.57, bf16[1536,1536]{1,0:T(8,128)(2,1)} %param.18, bf16[256,1536]{1,0:T(8,128)(2,1)S(1)} %copy-done.3), kind=kOutput, calls=%fused_computation.41 | convolution fusion | flops 1210318592 | bytes 7865344 | tf_op jit(solution)/shard_map/dot_general | solution.py:115
  102.2 1.1 multiply_convert_fusion
  103.3 4.3 %all-gather.7.cloned.1.call-done = bf16[1536,1728]{1,0:T(8,128)(2,1)} async-done(((bf16[96,1728]{1,0:T(8,128)(2,1)}), bf16[1536,1728]{1,0:T(8,128)(2,1)}) %all-gather.7.cloned.1.call-update) | async-done | bytes 5308432 | tf_op jit(solution)/shard_map/all_gather | solution.py:62
  107.6 0.0 all-gather.9.cloned.1.call-update
  107.6 0.0 all-gather.11.cloned.1.call-start
  107.7 40.7 %all-gather.9.cloned.1.call-done = bf16[1024,1536]{1,0:T(8,128)(2,1)} async-done(((bf16[256,1536]{1,0:T(8,128)(2,1)}), bf16[1024,1536]{1,0:T(8,128)(2,1)}) %all-gather.9.cloned.1.call-update) | async-done | bytes 3145744 | tf_op jit(solution)/shard_map/all_gather | solution.py:122
  148.4 0.0 all-gather.11.cloned.1.call-update
  148.4 0.3 reduce-scatter.3.cloned.1.call-start
  148.7 21.3 %all-gather.11.cloned.1.call-done = bf16[2048,1536]{1,0:T(8,128)(2,1)} async-done(((bf16[1024,1536]{1,0:T(8,128)(2,1)}), bf16[2048,1536]{1,0:T(8,128)(2,1)}) %all-gather.11.cloned.1.call-update) | async-done | bytes 6291472 | tf_op jit(solution)/shard_map/all_gather | solution.py:123
  170.0 6.8 %fusion.23 = f32[2048,576]{0,1:T(8,128)S(1)} fusion(bf16[2048,1536]{1,0:T(8,128)(2,1)} %all-gather.11.cloned.1.call-done, bf16[1536,1728]{1,0:T(8,128)(2,1)} %all-gather.7.cloned.1.call-done), kind=kOutput, calls=%fused_computation.30 | convolution fusion | flops 3623878656 | bytes 12976128 | tf_op jit(solution)/shard_map/dot_general | solution.py:124
  176.8 7.9 %fusion.16 = bf16[2048,576]{0,1:T(8,128)(2,1)S(1)} fusion(f32[2048,576]{0,1:T(8,128)S(1)} %fusion.23, bf16[2048,1536]{1,0:T(8,128)(2,1)S(1)} %copy-done.13, bf16[1536,1728]{1,0:T(8,128)(2,1)} %all-gather.7.cloned.1.call-done), kind=kOutput, calls=%fused_computation.21 | convolution fusion | flops 3635675136 | bytes 15335424 | tf_op jit(solution)/shard_map/dot_general | solution.py:125
  184.7 8.6 %convolution_convert_fusion = bf16[2048,1536]{1,0:T(8,128)(2,1)} fusion(bf16[2048,576]{0,1:T(8,128)(2,1)S(1)} %fusion.16, bf16[1536,1728]{1,0:T(8,128)(2,1)} %all-gather.7.cloned.1.call-done), kind=kOutput, calls=%fused_computation.11 | convolution fusion | flops 3627024384 | bytes 10616832 | tf_op jit(solution)/shard_map/dot_general | solution.py:127
  193.3 0.0 reduce-scatter.3.cloned.1.call-update
  193.3 0.0 reduce-scatter.5.cloned.1.call-start
  193.4 18.6 %reduce-scatter.3.cloned.1.call-done = bf16[1024,1536]{1,0:T(8,128)(2,1)} async-done(((bf16[2048,1536]{1,0:T(8,128)(2,1)}), bf16[1024,1536]{1,0:T(8,128)(2,1)}) %reduce-scatter.3.cloned.1.call-update) | async-done | bytes 3145744 | tf_op jit(solution)/shard_map/reduce_scatter | solution.py:130
  211.9 0.0 reduce-scatter.5.cloned.1.call-update
  212.0 0.0 copy-start.1
  212.0 41.6 %reduce-scatter.5.cloned.1.call-done = bf16[256,1536]{1,0:T(8,128)(2,1)} async-done(((bf16[1024,1536]{1,0:T(8,128)(2,1)}), bf16[256,1536]{1,0:T(8,128)(2,1)}) %reduce-scatter.5.cloned.1.call-update) | async-done | bytes 786448 | tf_op jit(solution)/shard_map/reduce_scatter | solution.py:131
  253.6 2.2 add_convert_fusion
  (39 shorter events, 0.2 us)
Async XLA Ops:
  6.5 7.2 %copy-start = (bf16[1536,256]{1,0:T(8,128)(2,1)S(1)}, bf16[1536,256]{1,0:T(8,128)(2,1)}, u32[]{:S(2)}) copy-start(bf16[1536,256]{1,0:T(8,128)(2,1)} %param.17) | copy-start | bytes 2359300
  6.5 9.8 %copy-start.12 = (s32[3,128]{1,0:T(4,128)S(1)}, s32[3,128]{1,0:T(4,128)}, u32[]{:S(2)}) copy-start(s32[3,128]{1,0:T(4,128)} %param.27) | copy-start | bytes 4612
  6.5 67.1 %all-gather.5.cloned.1.call-start = ((), (), s32[]{:S(2)}) async-start(), calls=%async_computation.4 | async-start | bytes 1179648 | tf_op jit(solution)/shard_map/all_gather | solution.py:88
  13.7 6.3 %copy-start.7 = (bf16[96,576]{1,0:T(8,128)(2,1)S(1)}, bf16[96,576]{1,0:T(8,128)(2,1)}, u32[]{:S(2)}) copy-start(bf16[96,576]{1,0:T(8,128)(2,1)} %param.20) | copy-start | bytes 331780
  13.7 6.4 %copy-start.8 = (bf16[96,576]{1,0:T(8,128)(2,1)S(1)}, bf16[96,576]{1,0:T(8,128)(2,1)}, u32[]{:S(2)}) copy-start(bf16[96,576]{1,0:T(8,128)(2,1)} %param.21) | copy-start | bytes 331780
  13.7 6.3 %copy-start.9 = (bf16[96,576]{1,0:T(8,128)(2,1)S(1)}, bf16[96,576]{1,0:T(8,128)(2,1)}, u32[]{:S(2)}) copy-start(bf16[96,576]{1,0:T(8,128)(2,1)} %param.22) | copy-start | bytes 331780
  13.8 7.2 %copy-start.11 = (s32[16]{0:T(128)S(1)}, s32[16]{0:T(128)}, u32[]{:S(2)}) copy-start(s32[16]{0:T(128)} %param.25) | copy-start | bytes 196
  13.8 7.3 %copy-start.2 = (s32[128]{0:T(128)S(1)}, s32[128]{0:T(128)}, u32[]{:S(2)}) copy-start(s32[128]{0:T(128)} %param.26) | copy-start | bytes 1540
  20.0 87.6 %all-gather.7.cloned.1.call-start = ((), (), s32[]{:S(2)}) async-start(), calls=%async_computation.5 | async-start | bytes 5849088 | tf_op jit(solution)/shard_map/all_gather | solution.py:62
  23.0 10.3 %copy-start.3 = (bf16[256,1536]{1,0:T(8,128)(2,1)S(1)}, bf16[256,1536]{1,0:T(8,128)(2,1)}, u32[]{:S(2)}) copy-start(bf16[256,1536]{1,0:T(8,128)(2,1)} %param.14) | copy-start | bytes 2359300
  23.0 10.3 %copy-start.14 = (f32[1536]{0:T(1024)S(1)}, f32[1536]{0:T(1024)}, u32[]{:S(2)}) copy-start(f32[1536]{0:T(1024)} %param.15) | copy-start | bytes 18436
  24.7 24.2 %all-to-all-start = ((bf16[16,2,64,256]{3,2,1,0:T(8,128)(2,1)}), bf16[16,2,64,256]{3,2,1,0:T(8,128)(2,1)}, u32[]{:S(2)}, u32[]{:S(2)}) async-start(bf16[16,2,64,256]{3,2,1,0:T(8,128)(2,1)} %bitcast.8), calls=%async_computation | async-start | bytes 2097152 | tf_op jit(solution)/shard_map/all_to_all | solution.py:71
  51.5 16.9 %all-to-all-start.1 = ((bf16[8,2,64,256]{3,2,1,0:T(8,128)(2,1)}), bf16[8,2,64,256]{3,2,1,0:T(8,128)(2,1)S(1)}, u32[]{:S(2)}, u32[]{:S(2)}) async-start(bf16[8,2,64,256]{3,2,1,0:T(8,128)(2,1)} %broadcast_in_dim.25), calls=%async_computation.1 | async-start | bytes 1048576 | tf_op jit(solution)/shard_map/all_to_all | solution.py:75
  58.9 89.4 %all-gather.9.cloned.1.call-start = ((), (), s32[]{:S(2)}) async-start(), calls=%async_computation.6 | async-start | bytes 3932160 | tf_op jit(solution)/shard_map/all_gather | solution.py:122
  68.4 2.1 copy-start.6
  72.4 1.2 copy-start.4
  73.6 7.8 %copy-start.5 = (f32[256,12,64]{2,0,1:T(8,128)S(1)}, f32[256,12,64]{2,0,1:T(8,128)}, u32[]{:S(2)}) copy-start(f32[256,12,64]{2,0,1:T(8,128)} %get-tuple-element.9) | copy-start | bytes 2359300
  98.2 4.0 %copy-start.10 = (f32[1536]{0:T(1024)S(1)}, f32[1536]{0:T(1024)}, u32[]{:S(2)}) copy-start(f32[1536]{0:T(1024)} %param.19) | copy-start | bytes 18436
  107.6 62.4 %all-gather.11.cloned.1.call-start = ((), (), s32[]{:S(2)}) async-start(), calls=%async_computation.7 | async-start | bytes 9437184 | tf_op jit(solution)/shard_map/all_gather | solution.py:123
  148.4 63.5 %reduce-scatter.3.cloned.1.call-start = ((), (), s32[]{:S(2)}) async-start(), calls=%async_computation.8 | async-start | bytes 9437184 | tf_op jit(solution)/shard_map/reduce_scatter | solution.py:130
  170.0 6.8 %copy-start.13 = (bf16[2048,1536]{1,0:T(8,128)(2,1)S(1)}, bf16[2048,1536]{1,0:T(8,128)(2,1)}, u32[]{:S(2)}) copy-start(bf16[2048,1536]{1,0:T(8,128)(2,1)} %all-gather.11.cloned.1.call-done) | copy-start | bytes 18874372
  193.3 60.3 %reduce-scatter.5.cloned.1.call-start = ((), (), s32[]{:S(2)}) async-start(), calls=%async_computation.9 | async-start | bytes 3932160 | tf_op jit(solution)/shard_map/reduce_scatter | solution.py:131
  212.0 43.9 %copy-start.1 = (bf16[1536,256]{1,0:T(8,128)(2,1)S(1)}, bf16[1536,256]{1,0:T(8,128)(2,1)}, u32[]{:S(2)}) copy-start(bf16[1536,256]{1,0:T(8,128)(2,1)} %param.17) | copy-start | bytes 2359300
Sparse Core Ops, SparseCore 0:
  20.1 26.9 all-gather.4
  49.3 58.2 all-gather.6
  109.2 39.0 all-gather.8
  149.9 20.0 all-gather.10
  193.5 18.4 reduce-scatter.2
  214.3 39.2 reduce-scatter.4

commit v3 on v2

--- a/solution.py
+++ b/solution.py
@@ -119,16 +119,25 @@
     gate_full = packed[:, :ff_cols]
     up_full = packed[:, ff_cols : 2 * ff_cols]
     down_full = packed[:, 2 * ff_cols :]
-    chip_rows = lax.all_gather(ffn_in, "x", axis=0, tiled=True)
-    all_rows = lax.all_gather(chip_rows, "core", axis=0, tiled=True)
-    gate = jnp.dot(all_rows, gate_full, preferred_element_type=jnp.float32)
-    upward = jnp.dot(all_rows, up_full, preferred_element_type=jnp.float32)
-    hidden = (jax.nn.gelu(gate, approximate=True) * upward).astype(jnp.bfloat16)
-    partial_down = lax.dot_general(
-        hidden, down_full, (((1,), (1,)), ((), ())), preferred_element_type=jnp.float32
-    ).astype(jnp.bfloat16)
-    pair_sum = lax.psum_scatter(partial_down, "core", scatter_dimension=0, tiled=True)
-    summed = lax.psum_scatter(pair_sum, "x", scatter_dimension=0, tiled=True).astype(jnp.float32)
+    n_chunks = 2
+    chunk = tok_rows // n_chunks
+    sums = []
+    pending = None
+    for index in range(n_chunks):
+        rows = lax.all_gather(
+            ffn_in[index * chunk : (index + 1) * chunk], ("x", "core"), axis=0, tiled=True
+        )
+        if pending is not None:
+            pending, rows = lax.optimization_barrier((pending, rows))
+            sums.append(lax.psum_scatter(pending, ("x", "core"), scatter_dimension=0, tiled=True))
+        gate = jnp.dot(rows, gate_full, preferred_element_type=jnp.float32)
+        upward = jnp.dot(rows, up_full, preferred_element_type=jnp.float32)
+        hidden = (jax.nn.gelu(gate, approximate=True) * upward).astype(jnp.bfloat16)
+        pending = lax.dot_general(
+            hidden, down_full, (((1,), (1,)), ((), ())), preferred_element_type=jnp.float32
+        ).astype(jnp.bfloat16)
+    sums.append(lax.psum_scatter(pending, ("x", "core"), scatter_dimension=0, tiled=True))
+    summed = jnp.concatenate(sums, 0).astype(jnp.float32)
     return (resid.astype(jnp.float32) + summed).astype(jnp.bfloat16)
 
 

time: 264 us -> 250 us (0.947)
  waiting for transfers between devices: 136 us -> 108 us
  matrix products: 50.2 us -> 61.2 us
    all_gather x2, waiting for transfers between devices: 62.1 us -> 39.8 us  [body(): lax.all_gather(ffn_in[index * chunk:(index + 1) * chunk], ('x', 'core'),...]
    dot_general x1 -> x2, matrix products: 8.64 us -> 21.2 us  [body(): lax.dot_general(hidden, down_full, (((1,), (1,)), ((), ())), preferred_el...]
    reduce_scatter x2, waiting for transfers between devices: 60.2 us -> 53.9 us  [body(): lax.psum_scatter(pending, ('x', 'core'), scatter_dimension=0, tiled=True)]
  transfers between devices with their start and end apart: 8 -> 8, of which waited for: 7 -> 7; matrix products, arithmetic and copies ran while one was open for 21% -> 36% of each run, Pallas kernels for 0% -> 0%
where the time goes in v3:
time: 250 us; the launch traced here: 247 us
  waiting for transfers between devices  108 us (43%)
  matrix products  61.2 us (24%)
  local copies, waits for them, and re-layouts  28.7 us (11%)
  between operations  21.8 us (9%)
  starting transfers between devices  16.9 us (7%)
  other arithmetic  9.95 us (4%)
    reduce_scatter x2, waiting for transfers between devices, body(): lax.psum_scatter(pending, ('x', 'core'), scatter_dimension=0, tiled=True)  53.9 us
    all_gather x2, waiting for transfers between devices, body(): lax.all_gather(ffn_in[index * chunk:(index + 1) * chunk], ('x', 'core'),...  39.8 us
    dot_general x2, matrix products, body(): lax.dot_general(hidden, down_full, (((1,), (1,)), ((), ())), preferred_el...  21.2 us
    dot_general x2, matrix products, body(): upward = jnp.dot(rows, up_full, preferred_element_type=jnp.float32)  13.2 us
    sub x1, matrix products, body(): weights = jnp.where(allowed, jnp.exp(scores - top), 0.0)  10.7 us
    all_to_all x1, starting transfers between devices, body(): lax.all_to_all(outgoing, 'req', split_axis=0, concat_axis=0, tiled=True)  8.65 us
    all_to_all x1, waiting for transfers between devices, body(): lax.all_to_all(fanned, ('x', 'core'), split_axis=0, concat_axis=0, tiled=...  8.39 us
    all_to_all x1, starting transfers between devices, body(): lax.all_to_all(fanned, ('x', 'core'), split_axis=0, concat_axis=0, tiled=...  7.57 us
  transfers between devices with their start and end apart: 8, of which 7 were waited for; matrix products, arithmetic and copies ran while one was open for 36% of the time, Pallas kernels for 0%

profile of v3, /device:TPU:1, one launch (start us, length us, event | category | flops | bytes accessed | tf_op | source)
XLA Modules:
  0.0 246.7 jit_solution(13580654884573359261)
XLA Ops:
  6.5 0.0 all-gather.5.cloned.1.call-start
  6.6 1.3 dynamic_slice.24
  9.9 1.2 dynamic_slice.25
  12.4 1.4 fusion.40
  13.8 0.0 copy-start.2
  13.8 1.7 fusion.56
  16.2 0.7 constant_dynamic-slice_fusion.2
  18.9 0.3 fusion.65
  19.2 0.7 pad_maximum_fusion
  19.9 0.0 all-gather.5.cloned.1.call-update
  19.9 0.0 all-gather.7.cloned.1.call-start
  20.0 0.9 concatenate.46
  20.9 0.0 all-gather.7.cloned.1.call-update
  21.0 0.7 gather_fusion
  21.7 0.1 copy.29
  21.7 0.1 reshape.377
  21.8 1.1 constant_dynamic-slice_fusion
  22.9 0.0 copy-start.3
  22.9 0.0 copy-start.13
  23.0 1.6 gather_fusion.1
  24.6 8.6 %all-to-all-start = ((bf16[16,2,64,256]{3,2,1,0:T(8,128)(2,1)}), bf16[16,2,64,256]{3,2,1,0:T(8,128)(2,1)}, u32[]{:S(2)}, u32[]{:S(2)}) async-start(bf16[16,2,64,256]{3,2,1,0:T(8,128)(2,1)} %bitcast.8), calls=%async_computation | async-start | bytes 2097152 | tf_op jit(solution)/shard_map/all_to_all | solution.py:71
  33.3 4.4 %fusion.58 = f32[256,1536]{0,1:T(8,128)S(1)} fusion(bf16[1536,1536]{1,0:T(8,128)(2,1)} %param.16, bf16[256,1536]{1,0:T(8,128)(2,1)S(1)} %copy-done.3, f32[1536]{0:T(1024)S(1)} %copy-done.13, f32[256]{0:T(256)S(1)} %add_rsqrt_fusion.1), kind=kOutput, calls=%fused_computation.67 | convolution fusion | flops 1209532416 | bytes 7085056 | tf_op jit(solution)/shard_map/dot_general | solution.py:80
  37.6 1.0 fusion.90
  40.1 0.2 dynamic-slice_reduce_fusion
  40.3 1.6 copy.35
  41.9 1.6 copy.36
  44.3 0.5 multiply_cosine_fusion
  44.8 3.5 %multiply_subtract_fusion = (f32[256,12,64]{2,0,1:T(8,128)}, f32[256,12,64]{2,0,1:T(8,128)}) fusion(f32[256,12,64]{2,0,1:T(8,128)} %copy.36, f32[256,12,64]{2,0,1:T(8,128)S(1)} %copy.35, f32[256,64]{1,0:T(8,128)S(1)} %get-tuple-element.27, f32[256,64]{1,0:T(8,128)S(1)} %get-tuple-element.26), kind=kLoop, calls=%fused_computation.61 | loop fusion | flops 1179648 | bytes 3276800 | tf_op jit(solution)/shard_map/sub | solution.py:27
  48.3 0.5 all-to-all-done
  48.8 1.8 gather_fusion.2
  50.6 0.8 broadcast_in_dim.25
  51.4 7.6 %all-to-all-start.1 = ((bf16[8,2,64,256]{3,2,1,0:T(8,128)(2,1)}), bf16[8,2,64,256]{3,2,1,0:T(8,128)(2,1)S(1)}, u32[]{:S(2)}, u32[]{:S(2)}) async-start(bf16[8,2,64,256]{3,2,1,0:T(8,128)(2,1)} %broadcast_in_dim.25), calls=%async_computation.1 | async-start | bytes 1048576 | tf_op jit(solution)/shard_map/all_to_all | solution.py:75
  59.0 1.1 fusion.50
  60.1 8.4 %all-to-all-done.1 = bf16[8,2,64,256]{3,2,1,0:T(8,128)(2,1)S(1)} async-done(((bf16[8,2,64,256]{3,2,1,0:T(8,128)(2,1)}), bf16[8,2,64,256]{3,2,1,0:T(8,128)(2,1)S(1)}, u32[]{:S(2)}, u32[]{:S(2)}) %all-to-all-start.1) | async-done | bytes 524320 | tf_op jit(solution)/shard_map/all_to_all | solution.py:75
  68.5 0.1 dynamic_update_slice.12
  68.6 1.9 dynamic_update_slice.13
  70.5 1.9 dynamic_update_slice.14
  72.5 1.2 copy-done.4
  73.7 1.6 copy.30
  75.3 6.2 %dynamic_update_slice.15 = bf16[3584,256]{1,0:T(8,128)(2,1)} dynamic-update-slice(bf16[3584,256]{1,0:T(8,128)(2,1)} %copy-done.4, bf16[2048,256]{1,0:T(8,128)(2,1)S(1)} %copy.30, s32[]{:T(128)S(6)} %select_n.97, s32[]{:T(128)} %constant.31.clone.1) | dynamic-update-slice | bytes 2097156 | tf_op jit(solution)/shard_map/dynamic_update_slice | solution.py:95
  81.5 10.7 %fusion.93 = (f32[256,12]{0,1:T(8,128)S(1)}, bf16[256,12,1280]{2,0,1:T(8,128)(2,1)}) fusion(pred[256,1280]{1,0:T(8,128)(4,1)} %fusion.50, bf16[3584,256]{1,0:T(8,128)(2,1)} %dynamic_update_slice.15, s32[]{:T(128)S(6)} %min.4, f32[256,12,64]{2,0,1:T(8,128)} %get-tuple-element.14, f32[256,12,64]{2,0,1:T(8,128)S(1)} %copy-done.5), kind=kOutput, calls=%fused_computation.130 | convolution fusion | flops 2035287296 | bytes 15479808 | tf_op jit(solution)/shard_map/sub | solution.py:106
  92.2 6.1 %divide_convert_fusion = bf16[256,12,128]{0,2,1:T(8,128)(2,1)S(1)} fusion(bf16[256,12,1280]{2,0,1:T(8,128)(2,1)} %get-tuple-element.29, f32[256,12]{0,1:T(8,128)S(1)} %get-tuple-element.28, bf16[3584,256]{1,0:T(8,128)(2,1)} %dynamic_update_slice.15, s32[]{:T(128)S(6)} %min.4, s32[]{:T(128)S(6)} %add.191), kind=kOutput, calls=%fused_computation.59 | convolution fusion | flops 1007419392 | bytes 8990728 | tf_op jit(solution)/shard_map/thk,kd->thd/dot_general | solution.py:108
  98.3 0.0 copy-start.10
  98.3 3.9 %multiply_reduce_fusion = (f32[256]{0:T(256)S(1)}, f32[256,1536]{1,0:T(8,128)S(1)}) fusion(bf16[256,1536]{0,1:T(8,128)(2,1)S(1)} %bitcast.58, bf16[1536,1536]{1,0:T(8,128)(2,1)} %param.18, bf16[256,1536]{1,0:T(8,128)(2,1)S(1)} %copy-done.3), kind=kOutput, calls=%fused_computation.58 | convolution fusion | flops 1210318592 | bytes 7865344 | tf_op jit(solution)/shard_map/dot_general | solution.py:115
  102.3 0.2 multiply_convert_fusion
  102.5 5.0 %all-gather.7.cloned.1.call-done = bf16[1536,1728]{1,0:T(8,128)(2,1)} async-done(((bf16[96,1728]{1,0:T(8,128)(2,1)}), bf16[1536,1728]{1,0:T(8,128)(2,1)}) %all-gather.7.cloned.1.call-update) | async-done | bytes 5308432 | tf_op jit(solution)/shard_map/all_gather | solution.py:62
  107.5 0.9 fusion.91
  108.4 0.0 all-gather.9.cloned.1.call-update
  108.4 0.0 all-gather.11.cloned.1.call-start
  108.5 0.5 all-gather.11.cloned.1.call-update
  109.0 0.3 reduce-scatter.3.cloned.1.call-start
  109.3 27.6 %all-gather.9.cloned.1.call-done = bf16[1024,1536]{1,0:T(8,128)(2,1)} async-done(((bf16[128,1536]{1,0:T(8,128)(2,1)}), bf16[1024,1536]{1,0:T(8,128)(2,1)}) %all-gather.9.cloned.1.call-update) | async-done | bytes 3145744 | tf_op jit(solution)/shard_map/all_gather | solution.py:127
  136.9 6.6 %fusion.34 = f32[1024,576]{0,1:T(8,128)} fusion(bf16[1024,1536]{1,0:T(8,128)(2,1)} %all-gather.9.cloned.1.call-done, bf16[1536,1728]{1,0:T(8,128)(2,1)} %all-gather.7.cloned.1.call-done), kind=kOutput, calls=%fused_computation.45 | convolution fusion | flops 1811939328 | bytes 7471104 | tf_op jit(solution)/shard_map/dot_general | solution.py:134
  143.5 10.6 %convolution_convert_fusion.1 = bf16[1024,1536]{1,0:T(8,128)(2,1)} fusion(bf16[1536,1728]{1,0:T(8,128)(2,1)} %all-gather.7.cloned.1.call-done, f32[1024,576]{0,1:T(8,128)} %fusion.34, bf16[1024,1536]{1,0:T(8,128)(2,1)} %all-gather.9.cloned.1.call-done), kind=kOutput, calls=%fused_computation.12 | convolution fusion | flops 3631349760 | bytes 12582912 | tf_op jit(solution)/shard_map/dot_general | solution.py:136
  154.2 12.1 %all-gather.11.cloned.1.call-done = bf16[1024,1536]{1,0:T(8,128)(2,1)} async-done(((bf16[128,1536]{1,0:T(8,128)(2,1)}), bf16[1024,1536]{1,0:T(8,128)(2,1)}) %all-gather.11.cloned.1.call-update) | async-done | bytes 3145744 | tf_op jit(solution)/shard_map/all_gather | solution.py:127
  166.3 0.0 reduce-scatter.3.cloned.1.call-update
  166.3 0.3 reduce-scatter.5.cloned.1.call-start
  166.6 6.6 %fusion.32 = f32[1024,576]{0,1:T(8,128)} fusion(bf16[1024,1536]{1,0:T(8,128)(2,1)} %all-gather.11.cloned.1.call-done, bf16[1536,1728]{1,0:T(8,128)(2,1)} %all-gather.7.cloned.1.call-done), kind=kOutput, calls=%fused_computation.43 | convolution fusion | flops 1811939328 | bytes 7471104 | tf_op jit(solution)/shard_map/dot_general | solution.py:134
  173.2 10.5 %convolution_convert_fusion = bf16[1024,1536]{1,0:T(8,128)(2,1)} fusion(bf16[1536,1728]{1,0:T(8,128)(2,1)} %all-gather.7.cloned.1.call-done, f32[1024,576]{0,1:T(8,128)} %fusion.32, bf16[1024,1536]{1,0:T(8,128)(2,1)} %all-gather.11.cloned.1.call-done), kind=kOutput, calls=%fused_computation.11 | convolution fusion | flops 3631349760 | bytes 12582912 | tf_op jit(solution)/shard_map/dot_general | solution.py:136
  183.7 0.0 reduce-scatter.5.cloned.1.call-update
  183.7 0.0 copy-start.1
  183.8 17.1 %reduce-scatter.3.cloned.1.call-done = bf16[128,1536]{1,0:T(8,128)(2,1)} async-done(((bf16[1024,1536]{1,0:T(8,128)(2,1)}), bf16[128,1536]{1,0:T(8,128)(2,1)}) %reduce-scatter.3.cloned.1.call-update) | async-done | bytes 393232 | tf_op jit(solution)/shard_map/reduce_scatter | solution.py:132
  200.9 36.8 %reduce-scatter.5.cloned.1.call-done = bf16[128,1536]{1,0:T(8,128)(2,1)} async-done(((bf16[1024,1536]{1,0:T(8,128)(2,1)}), bf16[128,1536]{1,0:T(8,128)(2,1)}) %reduce-scatter.5.cloned.1.call-update) | async-done | bytes 393232 | tf_op jit(solution)/shard_map/reduce_scatter | solution.py:139
  237.7 2.2 add_convert_fusion
  (39 shorter events, 0.2 us)
Async XLA Ops:
  6.5 7.3 %copy-start = (bf16[1536,256]{1,0:T(8,128)(2,1)S(1)}, bf16[1536,256]{1,0:T(8,128)(2,1)}, u32[]{:S(2)}) copy-start(bf16[1536,256]{1,0:T(8,128)(2,1)} %param.17) | copy-start | bytes 2359300
  6.5 9.7 %copy-start.12 = (s32[3,128]{1,0:T(4,128)S(1)}, s32[3,128]{1,0:T(4,128)}, u32[]{:S(2)}) copy-start(s32[3,128]{1,0:T(4,128)} %param.27) | copy-start | bytes 4612
  6.5 13.4 %copy-start.9 = (bf16[96,576]{1,0:T(8,128)(2,1)S(1)}, bf16[96,576]{1,0:T(8,128)(2,1)}, u32[]{:S(2)}) copy-start(bf16[96,576]{1,0:T(8,128)(2,1)} %param.22) | copy-start | bytes 331780
  6.5 13.4 %copy-start.8 = (bf16[96,576]{1,0:T(8,128)(2,1)S(1)}, bf16[96,576]{1,0:T(8,128)(2,1)}, u32[]{:S(2)}) copy-start(bf16[96,576]{1,0:T(8,128)(2,1)} %param.21) | copy-start | bytes 331780
  6.5 13.5 %copy-start.7 = (bf16[96,576]{1,0:T(8,128)(2,1)S(1)}, bf16[96,576]{1,0:T(8,128)(2,1)}, u32[]{:S(2)}) copy-start(bf16[96,576]{1,0:T(8,128)(2,1)} %param.20) | copy-start | bytes 331780
  6.5 67.1 %all-gather.5.cloned.1.call-start = ((), (), s32[]{:S(2)}) async-start(), calls=%async_computation.4 | async-start | bytes 1179648 | tf_op jit(solution)/shard_map/all_gather | solution.py:88
  13.8 7.1 %copy-start.11 = (s32[16]{0:T(128)S(1)}, s32[16]{0:T(128)}, u32[]{:S(2)}) copy-start(s32[16]{0:T(128)} %param.25) | copy-start | bytes 196
  13.8 7.2 %copy-start.2 = (s32[128]{0:T(128)S(1)}, s32[128]{0:T(128)}, u32[]{:S(2)}) copy-start(s32[128]{0:T(128)} %param.26) | copy-start | bytes 1540
  19.9 87.6 %all-gather.7.cloned.1.call-start = ((), (), s32[]{:S(2)}) async-start(), calls=%async_computation.5 | async-start | bytes 5849088 | tf_op jit(solution)/shard_map/all_gather | solution.py:62
  22.9 10.3 %copy-start.3 = (bf16[256,1536]{1,0:T(8,128)(2,1)S(1)}, bf16[256,1536]{1,0:T(8,128)(2,1)}, u32[]{:S(2)}) copy-start(bf16[256,1536]{1,0:T(8,128)(2,1)} %param.14) | copy-start | bytes 2359300
  22.9 10.3 %copy-start.13 = (f32[1536]{0:T(1024)S(1)}, f32[1536]{0:T(1024)}, u32[]{:S(2)}) copy-start(f32[1536]{0:T(1024)} %param.15) | copy-start | bytes 18436
  24.6 24.2 %all-to-all-start = ((bf16[16,2,64,256]{3,2,1,0:T(8,128)(2,1)}), bf16[16,2,64,256]{3,2,1,0:T(8,128)(2,1)}, u32[]{:S(2)}, u32[]{:S(2)}) async-start(bf16[16,2,64,256]{3,2,1,0:T(8,128)(2,1)} %bitcast.8), calls=%async_computation | async-start | bytes 2097152 | tf_op jit(solution)/shard_map/all_to_all | solution.py:71
  51.4 19.1 %copy-start.6 = (bf16[1,512,256]{2,1,0:T(8,128)(2,1)S(1)}, bf16[1,512,256]{2,1,0:T(8,128)(2,1)}, u32[]{:S(2)}) copy-start(bf16[1,512,256]{2,1,0:T(8,128)(2,1)} %param.24) | copy-start | bytes 786436
  51.4 17.1 %all-to-all-start.1 = ((bf16[8,2,64,256]{3,2,1,0:T(8,128)(2,1)}), bf16[8,2,64,256]{3,2,1,0:T(8,128)(2,1)S(1)}, u32[]{:S(2)}, u32[]{:S(2)}) async-start(bf16[8,2,64,256]{3,2,1,0:T(8,128)(2,1)} %broadcast_in_dim.25), calls=%async_computation.1 | async-start | bytes 1048576 | tf_op jit(solution)/shard_map/all_to_all | solution.py:75
  59.0 77.9 %all-gather.9.cloned.1.call-start = ((), (), s32[]{:S(2)}) async-start(), calls=%async_computation.6 | async-start | bytes 3538944 | tf_op jit(solution)/shard_map/all_gather | solution.py:127
  72.5 1.2 copy-start.4
  73.7 7.8 %copy-start.5 = (f32[256,12,64]{2,0,1:T(8,128)S(1)}, f32[256,12,64]{2,0,1:T(8,128)}, u32[]{:S(2)}) copy-start(f32[256,12,64]{2,0,1:T(8,128)} %get-tuple-element.13) | copy-start | bytes 2359300
  98.3 4.0 %copy-start.10 = (f32[1536]{0:T(1024)S(1)}, f32[1536]{0:T(1024)}, u32[]{:S(2)}) copy-start(f32[1536]{0:T(1024)} %param.19) | copy-start | bytes 18436
  108.4 57.8 %all-gather.11.cloned.1.call-start = ((), (), s32[]{:S(2)}) async-start(), calls=%async_computation.7 | async-start | bytes 3538944 | tf_op jit(solution)/shard_map/all_gather | solution.py:127
  109.0 91.9 %reduce-scatter.3.cloned.1.call-start = ((), (), s32[]{:S(2)}) async-start(), calls=%async_computation.8 | async-start | bytes 3538944 | tf_op jit(solution)/shard_map/reduce_scatter | solution.py:132
  166.3 71.4 %reduce-scatter.5.cloned.1.call-start = ((), (), s32[]{:S(2)}) async-start(), calls=%async_computation.9 | async-start | bytes 3538944 | tf_op jit(solution)/shard_map/reduce_scatter | solution.py:139
  183.7 56.1 %copy-start.1 = (bf16[1536,256]{1,0:T(8,128)(2,1)S(1)}, bf16[1536,256]{1,0:T(8,128)(2,1)}, u32[]{:S(2)}) copy-start(bf16[1536,256]{1,0:T(8,128)(2,1)} %param.17) | copy-start | bytes 2359300
Sparse Core Ops, SparseCore 0:
  20.0 26.9 all-gather.4
  49.2 58.2 all-gather.6
  109.2 27.6 all-gather.8
  138.5 27.7 all-gather.10
  168.5 32.3 reduce-scatter.2
  203.2 34.4 reduce-scatter.4

commit v4 on v1

--- a/solution.py
+++ b/solution.py
@@ -85,20 +85,24 @@
     new_keys = rotate(keyval_full[:, None, :HD], query_at)[:, 0].astype(jnp.bfloat16)
     new_vals = keyval_full[:, HD:].astype(jnp.bfloat16)
     new_keyval = jnp.concatenate([new_keys, new_vals], 1)
-    piece = lax.all_gather(new_keyval, "mlp", axis=0, tiled=True)
+    back = WINDOW // tok_rows
+    blocks = [
+        lax.ppermute(new_keyval, "mlp", [(i, (i + shift) % n_mlp) for i in range(n_mlp)])
+        for shift in range(back, 0, -1)
+    ]
+    new_part = jnp.concatenate(blocks + [new_keyval], 0)
+    span = new_part.shape[0]
 
-    seq_len = 3 * seg_slot + piece.shape[0]
-    seq = jnp.zeros((seq_len, piece.shape[1]), jnp.bfloat16)
-    seq = lax.dynamic_update_slice(seq, levels[0], (0, 0))
-    seq = lax.dynamic_update_slice(seq, levels[1], (len_zero, 0))
-    seq = lax.dynamic_update_slice(seq, own_prefix[0], (len_zero + len_one, 0))
-    seq = lax.dynamic_update_slice(seq, piece, (total, 0))
-    span = WINDOW + tok_rows
-    first = jnp.clip(total + position_group * tok_rows - WINDOW, 0, seq_len - span)
-    window = lax.dynamic_slice_in_dim(seq, first, span, 0)
-    key_at = first + jnp.arange(span, dtype=jnp.int32)
+    cbuf = jnp.zeros((WINDOW + 3 * seg_slot + span, new_part.shape[1]), jnp.bfloat16)
+    cbuf = lax.dynamic_update_slice(cbuf, levels[0], (WINDOW, 0))
+    cbuf = lax.dynamic_update_slice(cbuf, levels[1], (WINDOW + len_zero, 0))
+    cbuf = lax.dynamic_update_slice(cbuf, own_prefix[0], (WINDOW + len_zero + len_one, 0))
+    cached_win = lax.dynamic_slice_in_dim(cbuf, total + position_group * tok_rows, span, 0)
+    use_cached = (jnp.arange(span, dtype=jnp.int32) // tok_rows) < back - position_group
+    window = jnp.where(use_cached[:, None], cached_win, new_part)
+    key_at = total + position_group * tok_rows - WINDOW + jnp.arange(span, dtype=jnp.int32)
     spacing = query_at[:, None] - key_at[None, :]
-    allowed = ((spacing >= 0) & (spacing < WINDOW))[:, None, :]
+    allowed = ((key_at[None, :] >= 0) & (spacing >= 0) & (spacing < WINDOW))[:, None, :]
     scores = jnp.einsum(
         "thd,kd->thk", queries, window[:, :HD], preferred_element_type=jnp.float32
     )

time: 226 us -> 228 us (level)
  waiting for transfers between devices: 89.5 us -> 82.4 us
  starting transfers between devices: 9 us -> 14 us
  local copies, waits for them, and re-layouts: 26.9 us -> 30.1 us
    unnamed x34 -> x31, local copies, waits for them, and re-layouts: 4.56 us -> 11.3 us
    ppermute x0 -> x4, starting transfers between devices: none -> 5.88 us  [body(): lax.ppermute(new_keyval, 'mlp', [(i, (i + shift) % n_mlp) for i in range(...]
    all_gather x1, waiting for transfers between devices: 5.09 us -> 0.02 us  [body(): lax.all_gather(jnp.concatenate([w_gate, w_up, w_down], 1), 'req', axis=0,...]
    dynamic_update_slice x4 -> x3, local copies, waits for them, and re-layouts: 10.1 us -> 6.36 us  [the longest x1 3.12 us: body(): cbuf = lax.dynamic_update_slice(cbuf, levels[1], (WINDOW + len_zero, 0))]
  transfers between devices with their start and end apart: 5 -> 8, of which waited for: 3 -> 2; matrix products, arithmetic and copies ran while one was open for 24% -> 29% of each run, Pallas kernels for 0% -> 0%
where the time goes in v4:
time: 228 us; the launch traced here: 227 us
  waiting for transfers between devices  82.4 us (36%)
  matrix products  51.8 us (23%)
  local copies, waits for them, and re-layouts  30.1 us (13%)
  between operations  21 us (9%)
  blocking collectives  14.4 us (6%)
  starting transfers between devices  14 us (6%)
  other arithmetic  13.1 us (6%)
    reduce_scatter x1, waiting for transfers between devices, body(): lax.psum_scatter(lax.dot_general(hidden, down_full, (((1,), (1,)), ((), (...  41.7 us
    all_gather x1, waiting for transfers between devices, body(): all_rows = lax.all_gather(ffn_in, 'mlp', axis=0, tiled=True)  40.6 us
    all_gather x1, blocking collectives, body(): levels = lax.all_gather(my_part, 'mlp', axis=1, tiled=True)  14.4 us
    sub x1, matrix products, body(): weights = jnp.where(allowed, jnp.exp(scores - top), 0.0)  11.4 us
    unnamed x31, local copies, waits for them, and re-layouts  11.3 us
    dot_general x1, matrix products, body(): gate = jnp.dot(all_rows, gate_full, preferred_element_type=jnp.float32)  9.5 us
    all_to_all x1, starting transfers between devices, body(): lax.all_to_all(outgoing, 'req', split_axis=0, concat_axis=0, tiled=True)  7.82 us
    dot_general x1, matrix products, body(): upward = jnp.dot(all_rows, up_full, preferred_element_type=jnp.float32)  7.82 us
  transfers between devices with their start and end apart: 8, of which 2 were waited for; matrix products, arithmetic and copies ran while one was open for 29% of the time, Pallas kernels for 0%

profile of v4, /device:TPU:1, one launch (start us, length us, event | category | flops | bytes accessed | tf_op | source)
XLA Modules:
  0.0 226.9 jit_solution(2843298917692250581)
XLA Ops:
  6.5 2.0 concatenate.47
  8.5 0.0 all-gather.5.cloned.1.call-update
  8.5 1.2 dynamic_slice.24
  11.7 1.2 dynamic_slice.25
  14.3 0.0 copy-start.6
  14.3 0.0 copy-start.2
  14.3 1.4 fusion.25
  15.7 1.7 fusion.34
  18.1 0.6 constant_dynamic-slice_fusion.2
  20.5 0.3 fusion.43
  20.9 0.7 pad_maximum_fusion
  21.5 2.6 %collective-permute-start.3 = (bf16[256,256]{0,1:T(8,128)(2,1)}, bf16[256,256]{0,1:T(8,128)(2,1)}, u32[]{:S(2)}, u32[]{:S(2)}) collective-permute-start(bf16[256,256]{0,1:T(8,128)(2,1)} %pad_maximum_fusion), channel_id=1, source_target_pairs={{0,1},{1,2},{2,3},{3,4},{4,5},{5,6},{6,7},{7,0},{8,9},{9,10},{10,1... | collective-permute-start | bytes 393224 | tf_op jit(solution)/shard_map/ppermute | solution.py:90
  24.2 1.2 collective-permute-start.2
  25.4 1.6 collective-permute-start.1
  26.9 0.5 collective-permute-start
  27.5 0.7 gather_fusion
  28.1 0.1 copy.30
  28.2 0.1 reshape.401
  28.3 1.1 constant_dynamic-slice_fusion
  29.4 0.0 copy-start.3
  29.4 0.0 copy-start.10
  29.4 1.6 gather_fusion.1
  31.1 7.8 %all-to-all-start = ((bf16[16,2,64,256]{3,2,1,0:T(8,128)(2,1)}), bf16[16,2,64,256]{3,2,1,0:T(8,128)(2,1)}, u32[]{:S(2)}, u32[]{:S(2)}) async-start(bf16[16,2,64,256]{3,2,1,0:T(8,128)(2,1)} %bitcast.8), calls=%async_computation | async-start | bytes 2097152 | tf_op jit(solution)/shard_map/all_to_all | solution.py:73
  38.9 0.0 all-gather.3.cloned.1.call-start
  39.0 4.4 %fusion.36 = f32[256,1536]{0,1:T(8,128)S(1)} fusion(bf16[1536,1536]{1,0:T(8,128)(2,1)} %param.16, bf16[256,1536]{1,0:T(8,128)(2,1)S(1)} %copy-done.3, f32[1536]{0:T(1024)S(1)} %copy-done.10, f32[256]{0:T(256)S(1)} %add_rsqrt_fusion.1), kind=kOutput, calls=%fused_computation.52 | convolution fusion | flops 1209532416 | bytes 7085056 | tf_op jit(solution)/shard_map/dot_general | solution.py:80
  43.3 1.0 fusion.60
  44.3 1.8 copy.39
  46.2 1.7 copy.40
  47.9 0.5 multiply_cosine_fusion
  48.4 0.0 copy-start.4
  48.4 3.5 %multiply_subtract_fusion = (f32[256,12,64]{2,0,1:T(8,128)}, f32[256,12,64]{2,0,1:T(8,128)}) fusion(f32[256,12,64]{2,0,1:T(8,128)} %copy.40, f32[256,12,64]{2,0,1:T(8,128)S(1)} %copy.39, f32[256,64]{1,0:T(8,128)S(1)} %get-tuple-element.17, f32[256,64]{1,0:T(8,128)S(1)} %get-tuple-element.16), kind=kLoop, calls=%fused_computation.44 | loop fusion | flops 1179648 | bytes 3276800 | tf_op jit(solution)/shard_map/sub | solution.py:27
  51.9 1.2 fusion.32
  53.1 0.2 dynamic-slice_reduce_fusion
  55.2 0.1 copy.34
  55.4 1.6 constant_dynamic-update-slice_fusion.4
  56.9 1.6 constant_dynamic-update-slice_fusion.3
  58.5 1.6 constant_dynamic-update-slice_fusion.2
  60.1 1.6 constant_dynamic-update-slice_fusion.1
  61.7 0.7 constant_dynamic-update-slice_fusion
  62.3 1.8 gather_fusion.2
  64.2 0.1 copy.31
  64.2 14.4 %all_gather.9 = bf16[2,512,256]{2,0,1:T(2,128)(2,1)S(1)} all-gather(bf16[2,64,256]{2,0,1:T(2,128)(2,1)S(1)} %copy.31), channel_id=1, replica_groups=mesh['req'=16,'mlp'=8] {'mlp'}, dimensions={1}, use_global_device_ids=true | all-gather | bytes 589824 | tf_op jit(solution)/shard_map/all_gather | solution.py:76
  78.7 0.7 fusion.61
  79.4 0.7 copy.42
  80.1 0.7 copy.41
  80.8 0.1 dynamic_update_slice.9
  80.9 3.1 %dynamic_update_slice.10 = bf16[3840,256]{0,1:T(8,128)(2,1)S(1)} dynamic-update-slice(bf16[3840,256]{0,1:T(8,128)(2,1)S(1)} %dynamic_update_slice.9, bf16[512,256]{0,1:T(8,128)(2,1)S(1)} %bitcast.59, s32[]{:T(128)S(6)} %select_n.108, s32[]{:T(128)} %constant.36.clone.1) | dynamic-update-slice | bytes 524292 | tf_op jit(solution)/shard_map/dynamic_update_slice | solution.py:98
  84.0 3.1 %dynamic_update_slice.11 = bf16[3840,256]{0,1:T(8,128)(2,1)S(1)} dynamic-update-slice(bf16[3840,256]{0,1:T(8,128)(2,1)S(1)} %dynamic_update_slice.10, bf16[512,256]{0,1:T(8,128)(2,1)S(1)} %bitcast.60, s32[]{:T(128)S(6)} %select_n.109, s32[]{:T(128)} %constant.36.clone.1) | dynamic-update-slice | bytes 524292 | tf_op jit(solution)/shard_map/dynamic_update_slice | solution.py:99
  87.1 1.5 dynamic-slice_select_fusion
  88.6 11.4 %fusion.62 = (f32[256,12]{0,1:T(8,128)S(1)}, bf16[256,12,1280]{2,0,1:T(8,128)(2,1)}) fusion(pred[256,1280]{1,0:T(8,128)(4,1)} %fusion.32, bf16[1280,256]{0,1:T(8,128)(2,1)S(1)} %dynamic-slice_select_fusion, f32[256,12,64]{2,0,1:T(8,128)} %get-tuple-element.6, f32[256,12,64]{2,0,1:T(8,128)} %get-tuple-element.5), kind=kOutput, calls=%fused_computation.118 | convolution fusion | flops 2035287296 | bytes 15478784 | tf_op jit(solution)/shard_map/sub | solution.py:110
  100.0 5.9 %divide_convert_fusion = bf16[256,12,128]{0,2,1:T(8,128)(2,1)S(1)} fusion(bf16[256,12,1280]{2,0,1:T(8,128)(2,1)} %get-tuple-element.19, f32[256,12]{0,1:T(8,128)S(1)} %get-tuple-element.18, bf16[1280,256]{0,1:T(8,128)(2,1)S(1)} %dynamic-slice_select_fusion), kind=kOutput, calls=%fused_computation.42 | convolution fusion | flops 1007419392 | bytes 8994816 | tf_op jit(solution)/shard_map/thk,kd->thd/dot_general | solution.py:112
  106.0 3.8 %multiply_reduce_fusion = (f32[256]{0:T(256)S(1)}, f32[256,1536]{1,0:T(8,128)S(1)}) fusion(bf16[256,1536]{0,1:T(8,128)(2,1)S(1)} %bitcast.56, bf16[1536,1536]{1,0:T(8,128)(2,1)} %param.18, bf16[256,1536]{1,0:T(8,128)(2,1)S(1)} %copy-done.3), kind=kOutput, calls=%fused_computation.41 | convolution fusion | flops 1210318592 | bytes 7865344 | tf_op jit(solution)/shard_map/dot_general | solution.py:119
  109.8 1.1 multiply_convert_fusion
  110.9 0.0 all-gather.3.cloned.1.call-update
  110.9 0.3 reduce-scatter.2.cloned.1.call-start
  111.2 0.0 all-gather.5.cloned.1.call-done
  111.2 40.6 %all-gather.3.cloned.1.call-done = bf16[2048,1536]{1,0:T(8,128)(2,1)} async-done(((bf16[256,1536]{1,0:T(8,128)(2,1)}), bf16[2048,1536]{1,0:T(8,128)(2,1)}) %all-gather.3.cloned.1.call-update) | async-done | bytes 6291472 | tf_op jit(solution)/shard_map/all_gather | solution.py:122
  151.8 9.5 %fusion.23 = f32[2048,576]{0,1:T(8,128)} fusion(bf16[2048,1536]{1,0:T(8,128)(2,1)} %all-gather.3.cloned.1.call-done, bf16[1536,1728]{1,0:T(8,128)(2,1)} %all-gather.5.cloned.1.call-done), kind=kOutput, calls=%fused_computation.30 | convolution fusion | flops 3623878656 | bytes 12976128 | tf_op jit(solution)/shard_map/dot_general | solution.py:123
  161.3 7.8 %fusion.16 = bf16[2048,576]{0,1:T(8,128)(2,1)S(1)} fusion(f32[2048,576]{0,1:T(8,128)} %fusion.23, bf16[2048,1536]{1,0:T(8,128)(2,1)S(1)} %copy-done.8, bf16[1536,1728]{1,0:T(8,128)(2,1)S(1)} %copy-done.9), kind=kOutput, calls=%fused_computation.21 | convolution fusion | flops 3635675136 | bytes 15335424 | tf_op jit(solution)/shard_map/dot_general | solution.py:124
  169.1 7.3 %convolution_convert_fusion = bf16[2048,1536]{1,0:T(8,128)(2,1)} fusion(bf16[2048,576]{0,1:T(8,128)(2,1)S(1)} %fusion.16, bf16[1536,1728]{1,0:T(8,128)(2,1)S(1)} %copy-done.9), kind=kOutput, calls=%fused_computation.11 | convolution fusion | flops 3627024384 | bytes 10616832 | tf_op jit(solution)/shard_map/dot_general | solution.py:127
  176.4 0.0 reduce-scatter.2.cloned.1.call-update
  176.4 0.0 copy-start.1
  176.4 41.7 %reduce-scatter.2.cloned.1.call-done = bf16[256,1536]{1,0:T(8,128)(2,1)} async-done(((bf16[2048,1536]{1,0:T(8,128)(2,1)}), bf16[256,1536]{1,0:T(8,128)(2,1)}) %reduce-scatter.2.cloned.1.call-update) | async-done | bytes 786448 | tf_op jit(solution)/shard_map/reduce_scatter | solution.py:126
  218.1 2.2 add_convert_fusion
  (38 shorter events, 0.2 us)
Async XLA Ops:
  6.5 9.1 %copy-start = (bf16[1536,256]{1,0:T(8,128)(2,1)S(1)}, bf16[1536,256]{1,0:T(8,128)(2,1)}, u32[]{:S(2)}) copy-start(bf16[1536,256]{1,0:T(8,128)(2,1)} %param.17) | copy-start | bytes 2359300
  6.5 11.5 %copy-start.7 = (s32[3,128]{1,0:T(4,128)S(1)}, s32[3,128]{1,0:T(4,128)}, u32[]{:S(2)}) copy-start(s32[3,128]{1,0:T(4,128)} %param.27) | copy-start | bytes 4612
  6.5 104.7 %all-gather.5.cloned.1.call-start = ((), (), s32[]{:S(2)}) async-start(), calls=%async_computation.3 | async-start | bytes 5849088 | tf_op jit(solution)/shard_map/all_gather | solution.py:61
  14.3 13.2 %copy-start.6 = (s32[16]{0:T(128)S(1)}, s32[16]{0:T(128)}, u32[]{:S(2)}) copy-start(s32[16]{0:T(128)} %param.25) | copy-start | bytes 196
  14.3 13.2 %copy-start.2 = (s32[128]{0:T(128)S(1)}, s32[128]{0:T(128)}, u32[]{:S(2)}) copy-start(s32[128]{0:T(128)} %param.26) | copy-start | bytes 1540
  21.5 38.5 %collective-permute-start.3 = (bf16[256,256]{0,1:T(8,128)(2,1)}, bf16[256,256]{0,1:T(8,128)(2,1)}, u32[]{:S(2)}, u32[]{:S(2)}) collective-permute-start(bf16[256,256]{0,1:T(8,128)(2,1)} %pad_maximum_fusion), channel_id=1, source_target_pairs={{0,1},{1,2},{2,3},{3,4},{4,5},{5,6},{6,7},{7,0},{8,9},{9,10},{10,1... | collective-permute-start | bytes 393224 | tf_op jit(solution)/shard_map/ppermute | solution.py:90
  24.2 34.4 %collective-permute-start.2 = (bf16[256,256]{0,1:T(8,128)(2,1)}, bf16[256,256]{0,1:T(8,128)(2,1)}, u32[]{:S(2)}, u32[]{:S(2)}) collective-permute-start(bf16[256,256]{0,1:T(8,128)(2,1)} %pad_maximum_fusion), channel_id=1, source_target_pairs={{0,2},{1,3},{2,4},{3,5},{4,6},{5,7},{6,0},{7,1},{8,10},{9,11},{10,... | collective-permute-start | bytes 393224 | tf_op jit(solution)/shard_map/ppermute | solution.py:90
  25.4 31.6 %collective-permute-start.1 = (bf16[256,256]{0,1:T(8,128)(2,1)}, bf16[256,256]{0,1:T(8,128)(2,1)}, u32[]{:S(2)}, u32[]{:S(2)}) collective-permute-start(bf16[256,256]{0,1:T(8,128)(2,1)} %pad_maximum_fusion), channel_id=1, source_target_pairs={{0,3},{1,4},{2,5},{3,6},{4,7},{5,0},{6,1},{7,2},{8,11},{9,12},{10,... | collective-permute-start | bytes 393224 | tf_op jit(solution)/shard_map/ppermute | solution.py:90
  26.9 28.4 %collective-permute-start = (bf16[256,256]{0,1:T(8,128)(2,1)}, bf16[256,256]{0,1:T(8,128)(2,1)}, u32[]{:S(2)}, u32[]{:S(2)}) collective-permute-start(bf16[256,256]{0,1:T(8,128)(2,1)} %pad_maximum_fusion), channel_id=1, source_target_pairs={{0,4},{1,5},{2,6},{3,7},{4,0},{5,1},{6,2},{7,3},{8,12},{9,13},{10,... | collective-permute-start | bytes 393224 | tf_op jit(solution)/shard_map/ppermute | solution.py:90
  29.4 9.5 %copy-start.3 = (bf16[256,1536]{1,0:T(8,128)(2,1)S(1)}, bf16[256,1536]{1,0:T(8,128)(2,1)}, u32[]{:S(2)}) copy-start(bf16[256,1536]{1,0:T(8,128)(2,1)} %param.14) | copy-start | bytes 2359300
  29.4 9.5 %copy-start.10 = (f32[1536]{0:T(1024)S(1)}, f32[1536]{0:T(1024)}, u32[]{:S(2)}) copy-start(f32[1536]{0:T(1024)} %param.15) | copy-start | bytes 18436
  31.1 31.3 %all-to-all-start = ((bf16[16,2,64,256]{3,2,1,0:T(8,128)(2,1)}), bf16[16,2,64,256]{3,2,1,0:T(8,128)(2,1)}, u32[]{:S(2)}, u32[]{:S(2)}) async-start(bf16[16,2,64,256]{3,2,1,0:T(8,128)(2,1)} %bitcast.8), calls=%async_computation | async-start | bytes 2097152 | tf_op jit(solution)/shard_map/all_to_all | solution.py:73
  38.9 112.9 %all-gather.3.cloned.1.call-start = ((), (), s32[]{:S(2)}) async-start(), calls=%async_computation.2 | async-start | bytes 7077888 | tf_op jit(solution)/shard_map/all_gather | solution.py:122
  48.4 6.8 %copy-start.4 = (bf16[1,512,256]{2,1,0:T(8,128)(2,1)S(1)}, bf16[1,512,256]{2,1,0:T(8,128)(2,1)}, u32[]{:S(2)}) copy-start(bf16[1,512,256]{2,1,0:T(8,128)(2,1)} %param.24) | copy-start | bytes 786436
  105.9 3.9 %copy-start.5 = (f32[1536]{0:T(1024)S(1)}, f32[1536]{0:T(1024)}, u32[]{:S(2)}) copy-start(f32[1536]{0:T(1024)} %param.19) | copy-start | bytes 18436
  110.9 107.2 %reduce-scatter.2.cloned.1.call-start = ((), (), s32[]{:S(2)}) async-start(), calls=%async_computation.4 | async-start | bytes 7077888 | tf_op jit(solution)/shard_map/reduce_scatter | solution.py:126
  151.8 9.5 %copy-start.8 = (bf16[2048,1536]{1,0:T(8,128)(2,1)S(1)}, bf16[2048,1536]{1,0:T(8,128)(2,1)}, u32[]{:S(2)}) copy-start(bf16[2048,1536]{1,0:T(8,128)(2,1)} %all-gather.3.cloned.1.call-done) | copy-start | bytes 18874372
  151.8 9.5 %copy-start.9 = (bf16[1536,1728]{1,0:T(8,128)(2,1)S(1)}, bf16[1536,1728]{1,0:T(8,128)(2,1)}, u32[]{:S(2)}) copy-start(bf16[1536,1728]{1,0:T(8,128)(2,1)} %all-gather.5.cloned.1.call-done) | copy-start | bytes 15925252
  176.4 43.9 %copy-start.1 = (bf16[1536,256]{1,0:T(8,128)(2,1)S(1)}, bf16[1536,256]{1,0:T(8,128)(2,1)}, u32[]{:S(2)}) copy-start(bf16[1536,256]{1,0:T(8,128)(2,1)} %param.17) | copy-start | bytes 2359300
Sparse Core Ops, SparseCore 0:
  9.5 67.5 all-gather.4
  111.0 40.7 all-gather.2
  176.6 41.5 reduce-scatter.1

commit v5 on v1

--- a/solution.py
+++ b/solution.py
@@ -61,8 +61,6 @@
     packed = lax.all_gather(
         jnp.concatenate([w_gate, w_up, w_down], 1), "req", axis=0, tiled=True
     )
-    gate_full = packed[:, :ff_cols]
-    up_full = packed[:, ff_cols : 2 * ff_cols]
     down_full = packed[:, 2 * ff_cols :]
 
     level_zero = node_parent[leaf_parent]
@@ -87,16 +85,22 @@
     new_keyval = jnp.concatenate([new_keys, new_vals], 1)
     piece = lax.all_gather(new_keyval, "mlp", axis=0, tiled=True)
 
+    sources = jnp.concatenate([levels[0], levels[1], own_prefix[0], piece], 0)
     seq_len = 3 * seg_slot + piece.shape[0]
-    seq = jnp.zeros((seq_len, piece.shape[1]), jnp.bfloat16)
-    seq = lax.dynamic_update_slice(seq, levels[0], (0, 0))
-    seq = lax.dynamic_update_slice(seq, levels[1], (len_zero, 0))
-    seq = lax.dynamic_update_slice(seq, own_prefix[0], (len_zero + len_one, 0))
-    seq = lax.dynamic_update_slice(seq, piece, (total, 0))
     span = WINDOW + tok_rows
     first = jnp.clip(total + position_group * tok_rows - WINDOW, 0, seq_len - span)
-    window = lax.dynamic_slice_in_dim(seq, first, span, 0)
     key_at = first + jnp.arange(span, dtype=jnp.int32)
+    len_cut = len_zero + len_one
+    source_row = jnp.where(
+        key_at < len_zero,
+        key_at,
+        jnp.where(
+            key_at < len_cut,
+            key_at - len_zero + seg_slot,
+            jnp.where(key_at < total, key_at - len_cut + 2 * seg_slot, key_at - total + 3 * seg_slot),
+        ),
+    )
+    window = jnp.take(sources, source_row, axis=0, mode="clip")
     spacing = query_at[:, None] - key_at[None, :]
     allowed = ((spacing >= 0) & (spacing < WINDOW))[:, None, :]
     scores = jnp.einsum(
@@ -116,8 +120,9 @@
     resid = (tokens.astype(jnp.float32) + attn_out).astype(jnp.bfloat16)
     ffn_in = rms_scale(resid, ffn_gain).astype(jnp.bfloat16)
     all_rows = lax.all_gather(ffn_in, "mlp", axis=0, tiled=True)
-    gate = jnp.dot(all_rows, gate_full, preferred_element_type=jnp.float32)
-    upward = jnp.dot(all_rows, up_full, preferred_element_type=jnp.float32)
+    gate_up = jnp.dot(all_rows, packed[:, : 2 * ff_cols], preferred_element_type=jnp.float32)
+    gate = gate_up[:, :ff_cols]
+    upward = gate_up[:, ff_cols:]
     hidden = (jax.nn.gelu(gate, approximate=True) * upward).astype(jnp.bfloat16)
     summed = lax.psum_scatter(
         lax.dot_general(

time: 226 us -> 222 us (0.982)
  other arithmetic: 10.9 us -> 15.9 us
  local copies, waits for them, and re-layouts: 26.9 us -> 23.2 us
  matrix products: 51.5 us -> 48.2 us
    dynamic_update_slice x4 -> x0, local copies, waits for them, and re-layouts: 10.1 us -> none  [the longest x1 6.18 us: body(): seq = lax.dynamic_update_slice(seq, piece, (total, 0))]
    dot_general x2 -> x1, matrix products: 17.3 us -> 11.1 us  [body(): jnp.dot(all_rows, packed[:, :2 * ff_cols], preferred_element_type=jnp.flo...]
    gather x0 -> x1, local copies, waits for them, and re-layouts: none -> 4.06 us  [body(): window = jnp.take(sources, source_row, axis=0, mode='clip')]
    concatenate x0 -> x1, local copies, waits for them, and re-layouts: none -> 2.88 us  [body(): sources = jnp.concatenate([levels[0], levels[1], own_prefix[0], piece], 0)]
    concatenate x0 -> x1, other arithmetic: none -> 2.64 us  [body(): sources = jnp.concatenate([levels[0], levels[1], own_prefix[0], piece], 0)]
    dot_general x1, matrix products: 7.2 us -> 9.57 us  [body(): lax.dot_general(hidden, down_full, (((1,), (1,)), ((), ())), preferred_el...]
    unnamed x34 -> x33, local copies, waits for them, and re-layouts: 4.56 us -> 4.84 us
  transfers between devices with their start and end apart: 5 -> 5, of which waited for: 3 -> 3; matrix products, arithmetic and copies ran while one was open for 24% -> 26% of each run, Pallas kernels for 0% -> 0%
where the time goes in v5:
time: 222 us; the launch traced here: 221 us
  waiting for transfers between devices  90.2 us (41%)
  matrix products  48.2 us (22%)
  local copies, waits for them, and re-layouts  23.2 us (10%)
  between operations  19.3 us (9%)
  other arithmetic  15.9 us (7%)
  blocking collectives  15.5 us (7%)
  starting transfers between devices  9 us (4%)
    all_gather x1, waiting for transfers between devices, body(): all_rows = lax.all_gather(ffn_in, 'mlp', axis=0, tiled=True)  42.6 us
    reduce_scatter x1, waiting for transfers between devices, body(): lax.psum_scatter(lax.dot_general(hidden, down_full, (((1,), (1,)), ((), (...  41.7 us
    all_gather x1, blocking collectives, body(): levels = lax.all_gather(my_part, 'mlp', axis=1, tiled=True)  15.5 us
    sub x1, matrix products, body(): weights = jnp.where(allowed, jnp.exp(scores - top), 0.0)  11.3 us
    dot_general x1, matrix products, body(): jnp.dot(all_rows, packed[:, :2 * ff_cols], preferred_element_type=jnp.flo...  11.1 us
    dot_general x1, matrix products, body(): lax.dot_general(hidden, down_full, (((1,), (1,)), ((), ())), preferred_el...  9.57 us
    all_to_all x1, starting transfers between devices, body(): lax.all_to_all(outgoing, 'req', split_axis=0, concat_axis=0, tiled=True)  8.65 us
    dot_general x1, matrix products, body(): jnp.einsum('thk,kd->thd', weights.astype(jnp.bfloat16), window[:, HD:], p...  6.03 us
  transfers between devices with their start and end apart: 5, of which 3 were waited for; matrix products, arithmetic and copies ran while one was open for 26% of the time, Pallas kernels for 0%

profile of v5, /device:TPU:1, one launch (start us, length us, event | category | flops | bytes accessed | tf_op | source)
XLA Modules:
  0.0 221.3 jit_solution(13196897716380005611)
XLA Ops:
  6.5 1.3 dynamic_slice.21
  9.8 1.2 dynamic_slice.22
  12.4 1.4 fusion.29
  13.7 0.0 copy-start.6
  13.7 0.0 copy-start.7
  13.8 0.0 copy-start.10
  13.8 0.0 copy-start.2
  13.8 1.8 fusion.37
  16.3 0.0 copy-done.11
  16.3 0.7 constant_dynamic-slice_fusion.2
  18.9 0.3 fusion.46
  19.3 0.7 pad_maximum_fusion.1
  19.9 0.0 all-gather.4.cloned.1.call-update
  19.9 0.0 all-gather.8.cloned.1.call-start
  20.0 0.9 concatenate.47
  20.9 0.0 all-gather.8.cloned.1.call-update
  21.0 0.7 gather_fusion
  21.7 0.1 copy.32
  21.7 0.1 reshape.414
  21.8 1.1 constant_dynamic-slice_fusion
  22.9 0.0 copy-start.3
  22.9 0.0 copy-start.13
  22.9 1.6 gather_fusion.1
  24.5 8.6 %all-to-all-start = ((bf16[16,2,64,256]{3,2,1,0:T(8,128)(2,1)}), bf16[16,2,64,256]{3,2,1,0:T(8,128)(2,1)}, u32[]{:S(2)}, u32[]{:S(2)}) async-start(bf16[16,2,64,256]{3,2,1,0:T(8,128)(2,1)} %bitcast.8), calls=%async_computation | async-start | bytes 2097152 | tf_op jit(solution)/shard_map/all_to_all | solution.py:71
  33.2 0.0 all-gather.6.cloned.1.call-start
  33.3 0.2 dynamic-slice_reduce_fusion
  33.5 0.5 fusion.57
  34.0 1.2 multiply_cosine_fusion
  35.2 4.4 %fusion.39 = f32[256,1536]{0,1:T(8,128)S(1)} fusion(bf16[1536,1536]{1,0:T(8,128)(2,1)} %param.16, bf16[256,1536]{1,0:T(8,128)(2,1)S(1)} %copy-done.3, f32[1536]{0:T(1024)S(1)} %copy-done.13, f32[256]{0:T(256)S(1)} %add_rsqrt_fusion.1), kind=kOutput, calls=%fused_computation.55 | convolution fusion | flops 1209532416 | bytes 7085056 | tf_op jit(solution)/shard_map/dot_general | solution.py:78
  39.6 0.0 copy-start.4
  39.6 1.0 fusion.64
  40.6 0.6 iota_add_fusion.1
  41.2 0.1 copy.36
  41.3 1.6 copy.40
  43.0 1.7 copy.41
  44.6 0.7 fusion.49
  45.3 3.5 %multiply_subtract_fusion = (f32[256,12,64]{2,0,1:T(8,128)}, f32[256,12,64]{2,0,1:T(8,128)}) fusion(f32[256,12,64]{2,0,1:T(8,128)} %copy.41, f32[256,12,64]{2,0,1:T(8,128)S(1)} %copy.40, f32[256,64]{1,0:T(8,128)} %get-tuple-element.17, f32[256,64]{1,0:T(8,128)S(1)} %get-tuple-element.16), kind=kLoop, calls=%fused_computation.49 | loop fusion | flops 1179648 | bytes 3276800 | tf_op jit(solution)/shard_map/sub | solution.py:27
  48.8 1.1 fusion.35
  49.9 0.0 all-to-all-done
  49.9 1.8 gather_fusion.2
  51.7 0.1 copy.33
  51.8 15.5 %all_gather.12 = bf16[2,512,256]{2,0,1:T(2,128)(2,1)S(1)} all-gather(bf16[2,64,256]{2,0,1:T(2,128)(2,1)S(1)} %copy.33), channel_id=1, replica_groups=mesh['req'=16,'mlp'=8] {'mlp'}, dimensions={1}, use_global_device_ids=true | all-gather | bytes 589824 | tf_op jit(solution)/shard_map/all_gather | solution.py:74
  67.2 0.7 fusion.65
  68.0 0.7 copy.42
  68.7 0.7 copy.43
  69.3 0.0 all-gather.4.cloned.1.call-done
  69.4 2.6 %pad_maximum_fusion = bf16[3584,256]{0,1:T(8,128)(2,1)} fusion(bf16[2048,256]{0,1:T(8,128)(2,1)} %all-gather.4.cloned.1.call-done, bf16[512,256]{0,1:T(8,128)(2,1)S(1)} %bitcast.59, bf16[512,256]{0,1:T(8,128)(2,1)S(1)} %bitcast.58, bf16[512,256]{0,1:T(8,128)(2,1)S(1)} %bitcast.57), kind=kLoop, calls=%fused_computation.38 | loop fusion | flops 7340032 | bytes 3670016 | tf_op jit(solution)/shard_map/concatenate | solution.py:88
  72.0 2.9 %copy.37 = bf16[3584,256]{1,0:T(8,128)(2,1)S(1)} copy(bf16[3584,256]{0,1:T(8,128)(2,1)} %pad_maximum_fusion) | data formatting | bytes 3670016 | tf_op jit(solution)/shard_map/concatenate | solution.py:88
  74.9 4.1 %gather_fusion.3 = bf16[1280,256]{1,0:T(8,128)(2,1)S(1)} fusion(bf16[3584,256]{1,0:T(8,128)(2,1)S(1)} %copy.37, s32[2048]{0:T(1024)S(1)} %pad_clamp_fusion), kind=kCustom, calls=%fused_computation.3 | custom fusion | bytes 1315840 | tf_op jit(solution)/shard_map/jit(_take)/gather | solution.py:103
  79.0 11.3 %fusion.66 = (f32[256,12]{0,1:T(8,128)S(1)}, bf16[256,12,1280]{2,0,1:T(8,128)(2,1)}) fusion(pred[256,1280]{1,0:T(8,128)(4,1)} %fusion.35, bf16[1280,256]{1,0:T(8,128)(2,1)S(1)} %gather_fusion.3, f32[256,12,64]{2,0,1:T(8,128)} %get-tuple-element.6, f32[256,12,64]{2,0,1:T(8,128)} %get-tuple-element.5), kind=kOutput, calls=%fused_computation.116 | convolution fusion | flops 2035287296 | bytes 15478784 | tf_op jit(solution)/shard_map/sub | solution.py:110
  90.3 6.0 %divide_convert_fusion = bf16[256,12,128]{0,2,1:T(8,128)(2,1)S(1)} fusion(bf16[256,12,1280]{2,0,1:T(8,128)(2,1)} %get-tuple-element.19, f32[256,12]{0,1:T(8,128)S(1)} %get-tuple-element.18, bf16[1280,256]{1,0:T(8,128)(2,1)S(1)} %gather_fusion.3), kind=kOutput, calls=%fused_computation.47 | convolution fusion | flops 1007419392 | bytes 8994816 | tf_op jit(solution)/shard_map/thk,kd->thd/dot_general | solution.py:112
  96.4 0.0 copy-start.8
  96.4 3.9 %multiply_reduce_fusion = (f32[256]{0:T(256)S(1)}, f32[256,1536]{1,0:T(8,128)S(1)}) fusion(bf16[256,1536]{0,1:T(8,128)(2,1)S(1)} %bitcast.55, bf16[1536,1536]{1,0:T(8,128)(2,1)} %param.18, bf16[256,1536]{1,0:T(8,128)(2,1)S(1)} %copy-done.3), kind=kOutput, calls=%fused_computation.46 | convolution fusion | flops 1210318592 | bytes 7865344 | tf_op jit(solution)/shard_map/dot_general | solution.py:119
  100.3 1.1 multiply_convert_fusion
  101.4 0.0 all-gather.6.cloned.1.call-update
  101.4 0.3 reduce-scatter.2.cloned.1.call-start
  101.7 5.8 %all-gather.8.cloned.1.call-done = bf16[1536,1728]{1,0:T(8,128)(2,1)} async-done(((bf16[96,1728]{1,0:T(8,128)(2,1)}), bf16[1536,1728]{1,0:T(8,128)(2,1)}) %all-gather.8.cloned.1.call-update) | async-done | bytes 5308432 | tf_op jit(solution)/shard_map/all_gather | solution.py:61
  107.5 42.6 %all-gather.6.cloned.1.call-done = bf16[2048,1536]{1,0:T(8,128)(2,1)} async-done(((bf16[256,1536]{1,0:T(8,128)(2,1)}), bf16[2048,1536]{1,0:T(8,128)(2,1)}) %all-gather.6.cloned.1.call-update) | async-done | bytes 6291472 | tf_op jit(solution)/shard_map/all_gather | solution.py:122
  150.1 11.1 %fusion.17 = f32[2048,1152]{0,1:T(8,128)S(1)} fusion(bf16[2048,1536]{1,0:T(8,128)(2,1)} %all-gather.6.cloned.1.call-done, bf16[1536,1728]{1,0:T(8,128)(2,1)} %all-gather.8.cloned.1.call-done), kind=kOutput, calls=%fused_computation.23 | convolution fusion | flops 7247757312 | bytes 19267584 | tf_op jit(solution)/shard_map/dot_general | solution.py:123
  161.2 9.6 %convolution_convert_fusion = bf16[2048,1536]{1,0:T(8,128)(2,1)} fusion(f32[2048,1152]{0,1:T(8,128)S(1)} %fusion.17, bf16[1536,1728]{1,0:T(8,128)(2,1)} %all-gather.8.cloned.1.call-done), kind=kOutput, calls=%fused_computation.12 | convolution fusion | flops 3638820864 | bytes 17694720 | tf_op jit(solution)/shard_map/dot_general | solution.py:128
  170.8 0.0 reduce-scatter.2.cloned.1.call-update
  170.8 0.0 copy-start.1
  170.8 41.7 %reduce-scatter.2.cloned.1.call-done = bf16[256,1536]{1,0:T(8,128)(2,1)} async-done(((bf16[2048,1536]{1,0:T(8,128)(2,1)}), bf16[256,1536]{1,0:T(8,128)(2,1)}) %reduce-scatter.2.cloned.1.call-update) | async-done | bytes 786448 | tf_op jit(solution)/shard_map/reduce_scatter | solution.py:127
  212.5 2.2 add_convert_fusion
  (32 shorter events, 0.1 us)
Async XLA Ops:
  6.5 7.2 %copy-start = (bf16[1536,256]{1,0:T(8,128)(2,1)S(1)}, bf16[1536,256]{1,0:T(8,128)(2,1)}, u32[]{:S(2)}) copy-start(bf16[1536,256]{1,0:T(8,128)(2,1)} %param.17) | copy-start | bytes 2359300
  6.5 9.8 %copy-start.11 = (s32[3,128]{1,0:T(4,128)S(1)}, s32[3,128]{1,0:T(4,128)}, u32[]{:S(2)}) copy-start(s32[3,128]{1,0:T(4,128)} %param.27) | copy-start | bytes 4612
  6.5 62.8 %all-gather.4.cloned.1.call-start = ((), (), s32[]{:S(2)}) async-start(), calls=%async_computation.2 | async-start | bytes 1179648 | tf_op jit(solution)/shard_map/all_gather | solution.py:86
  13.7 6.3 %copy-start.5 = (bf16[96,576]{1,0:T(8,128)(2,1)S(1)}, bf16[96,576]{1,0:T(8,128)(2,1)}, u32[]{:S(2)}) copy-start(bf16[96,576]{1,0:T(8,128)(2,1)} %param.20) | copy-start | bytes 331780
  13.7 6.3 %copy-start.6 = (bf16[96,576]{1,0:T(8,128)(2,1)S(1)}, bf16[96,576]{1,0:T(8,128)(2,1)}, u32[]{:S(2)}) copy-start(bf16[96,576]{1,0:T(8,128)(2,1)} %param.21) | copy-start | bytes 331780
  13.7 6.3 %copy-start.7 = (bf16[96,576]{1,0:T(8,128)(2,1)S(1)}, bf16[96,576]{1,0:T(8,128)(2,1)}, u32[]{:S(2)}) copy-start(bf16[96,576]{1,0:T(8,128)(2,1)} %param.22) | copy-start | bytes 331780
  13.8 7.1 %copy-start.10 = (s32[16]{0:T(128)S(1)}, s32[16]{0:T(128)}, u32[]{:S(2)}) copy-start(s32[16]{0:T(128)} %param.25) | copy-start | bytes 196
  13.8 7.2 %copy-start.2 = (s32[128]{0:T(128)S(1)}, s32[128]{0:T(128)}, u32[]{:S(2)}) copy-start(s32[128]{0:T(128)} %param.26) | copy-start | bytes 1540
  19.9 87.6 %all-gather.8.cloned.1.call-start = ((), (), s32[]{:S(2)}) async-start(), calls=%async_computation.4 | async-start | bytes 5849088 | tf_op jit(solution)/shard_map/all_gather | solution.py:61
  22.9 12.3 %copy-start.3 = (bf16[256,1536]{1,0:T(8,128)(2,1)S(1)}, bf16[256,1536]{1,0:T(8,128)(2,1)}, u32[]{:S(2)}) copy-start(bf16[256,1536]{1,0:T(8,128)(2,1)} %param.14) | copy-start | bytes 2359300
  22.9 12.3 %copy-start.13 = (f32[1536]{0:T(1024)S(1)}, f32[1536]{0:T(1024)}, u32[]{:S(2)}) copy-start(f32[1536]{0:T(1024)} %param.15) | copy-start | bytes 18436
  24.5 25.4 %all-to-all-start = ((bf16[16,2,64,256]{3,2,1,0:T(8,128)(2,1)}), bf16[16,2,64,256]{3,2,1,0:T(8,128)(2,1)}, u32[]{:S(2)}, u32[]{:S(2)}) async-start(bf16[16,2,64,256]{3,2,1,0:T(8,128)(2,1)} %bitcast.8), calls=%async_computation | async-start | bytes 2097152 | tf_op jit(solution)/shard_map/all_to_all | solution.py:71
  33.2 116.9 %all-gather.6.cloned.1.call-start = ((), (), s32[]{:S(2)}) async-start(), calls=%async_computation.3 | async-start | bytes 7077888 | tf_op jit(solution)/shard_map/all_gather | solution.py:122
  39.6 1.6 copy-start.4
  45.3 3.5 %copy-start.12 = (s32[256]{0:T(256)S(1)}, s32[256]{0:T(256)}, u32[]{:S(2)}) copy-start(s32[256]{0:T(256)} %iota_add_fusion.1) | copy-start | bytes 3076
  45.3 4.6 %copy-start.9 = (s32[2]{0:T(128)S(1)}, s32[2]{0:T(128)}, u32[]{:S(2)}) copy-start(s32[2]{0:T(128)} %fusion.57) | copy-start | bytes 28
  96.4 4.0 %copy-start.8 = (f32[1536]{0:T(1024)S(1)}, f32[1536]{0:T(1024)}, u32[]{:S(2)}) copy-start(f32[1536]{0:T(1024)} %param.19) | copy-start | bytes 18436
  101.4 111.1 %reduce-scatter.2.cloned.1.call-start = ((), (), s32[]{:S(2)}) async-start(), calls=%async_computation.5 | async-start | bytes 7077888 | tf_op jit(solution)/shard_map/reduce_scatter | solution.py:127
  170.8 43.9 %copy-start.1 = (bf16[1536,256]{1,0:T(8,128)(2,1)S(1)}, bf16[1536,256]{1,0:T(8,128)(2,1)}, u32[]{:S(2)}) copy-start(bf16[1536,256]{1,0:T(8,128)(2,1)} %param.17) | copy-start | bytes 2359300
Sparse Core Ops, SparseCore 0:
  20.1 26.9 all-gather.3
  49.2 58.2 all-gather.7
  109.2 40.8 all-gather.5
  170.9 41.5 reduce-scatter.1

commit v6 on v5

--- a/solution.py
+++ b/solution.py
@@ -1,6 +1,8 @@
 import jax
 import jax.numpy as jnp
 from jax import lax
+from jax.experimental import pallas as pl
+from jax.experimental.pallas import tpu as pltpu
 from jax.sharding import PartitionSpec as P
 
 HEADS = 12
@@ -25,6 +27,39 @@
     first = values[..., :half_dim]
     second = values[..., half_dim:]
     return jnp.concatenate([first * cosine - second * sine, first * sine + second * cosine], -1)
+
+
+def _attend_kernel(where_ref, q_ref, kv_ref, o_ref):
+    query = q_ref[0]
+    keys = kv_ref[:, :HD]
+    vals = kv_ref[:, HD:]
+    scores = lax.dot_general(query, keys, (((1,), (1,)), ((), ())), preferred_element_type=jnp.float32)
+    query_at = where_ref[0] + lax.broadcasted_iota(jnp.int32, scores.shape, 0)
+    key_at = where_ref[1] + lax.broadcasted_iota(jnp.int32, scores.shape, 1)
+    spacing = query_at - key_at
+    allowed = (key_at >= 0) & (spacing >= 0) & (spacing < WINDOW)
+    top = jnp.max(jnp.where(allowed, scores, -jnp.inf), axis=1, keepdims=True)
+    weights = jnp.where(allowed, jnp.exp(scores - top), 0.0)
+    denom = jnp.sum(weights, axis=1, keepdims=True)
+    mixed = jnp.dot(weights.astype(jnp.bfloat16), vals, preferred_element_type=jnp.float32)
+    o_ref[0] = (mixed / denom).astype(o_ref.dtype)
+
+def attend_window(queries_hm, window, where):
+    heads, rows, _ = queries_hm.shape
+    span = window.shape[0]
+    return pl.pallas_call(
+        _attend_kernel,
+        grid_spec=pltpu.PrefetchScalarGridSpec(
+            num_scalar_prefetch=1,
+            grid=(heads,),
+            in_specs=[
+                pl.BlockSpec((1, rows, HD), lambda h, w: (h, 0, 0)),
+                pl.BlockSpec((span, 2 * HD), lambda h, w: (0, 0)),
+            ],
+            out_specs=pl.BlockSpec((1, rows, HD), lambda h, w: (h, 0, 0)),
+        ),
+        out_shape=jax.ShapeDtypeStruct((heads, rows, HD), jnp.bfloat16),
+    )(where, queries_hm, window)
 
 
 def body(
@@ -101,21 +136,9 @@
         ),
     )
     window = jnp.take(sources, source_row, axis=0, mode="clip")
-    spacing = query_at[:, None] - key_at[None, :]
-    allowed = ((spacing >= 0) & (spacing < WINDOW))[:, None, :]
-    scores = jnp.einsum(
-        "thd,kd->thk", queries, window[:, :HD], preferred_element_type=jnp.float32
-    )
-    top = jnp.max(jnp.where(allowed, scores, -jnp.inf), axis=-1, keepdims=True)
-    weights = jnp.where(allowed, jnp.exp(scores - top), 0.0)
-    denom = jnp.sum(weights, axis=-1)
-    mixed = jnp.einsum(
-        "thk,kd->thd",
-        weights.astype(jnp.bfloat16),
-        window[:, HD:],
-        preferred_element_type=jnp.float32,
-    )
-    context = (mixed / denom[..., None]).reshape(tok_rows, HEADS * HD).astype(jnp.bfloat16)
+    where = jnp.stack([total + position_group * tok_rows, first]).astype(jnp.int32)
+    heads_first = attend_window(jnp.transpose(queries, (1, 0, 2)), window, where)
+    context = jnp.transpose(heads_first, (1, 0, 2)).reshape(tok_rows, HEADS * HD)
     attn_out = jnp.dot(context, w_out, preferred_element_type=jnp.float32)
     resid = (tokens.astype(jnp.float32) + attn_out).astype(jnp.bfloat16)
     ffn_in = rms_scale(resid, ffn_gain).astype(jnp.bfloat16)

time: 222 us -> 222 us (level)
  matrix products: 48.2 us -> 30.8 us
  Pallas kernels: 0 us -> 16.2 us
  other arithmetic: 15.9 us -> 13.4 us
    pallas_call x0 -> x1, Pallas kernels: none -> 16.2 us  [attend_window(): pl.pallas_call(_attend_kernel, grid_spec=pltpu.PrefetchScalarGridSpec(num...]
    sub x1 -> x0, matrix products: 11.3 us -> none  [body(): weights = jnp.where(allowed, jnp.exp(scores - top), 0.0)]
    dot_general x1 -> x0, matrix products: 6.03 us -> none  [body(): jnp.einsum('thk,kd->thd', weights.astype(jnp.bfloat16), window[:, HD:], p...]
    unnamed x33 -> x29, local copies, waits for them, and re-layouts: 4.84 us -> 4.81 us
  transfers between devices with their start and end apart: 5 -> 5, of which waited for: 3 -> 4; matrix products, arithmetic and copies ran while one was open for 26% -> 18% of each run, Pallas kernels for 0% -> 7%
where the time goes in v6:
time: 222 us; the launch traced here: 221 us
  waiting for transfers between devices  90.8 us (41%)
  matrix products  30.8 us (14%)
  local copies, waits for them, and re-layouts  25.2 us (11%)
  between operations  19.4 us (9%)
  blocking collectives  16.6 us (7%)
  Pallas kernels  16.2 us (7%)
  other arithmetic  13.4 us (6%)
  starting transfers between devices  9 us (4%)
    all_gather x1, waiting for transfers between devices, body(): all_rows = lax.all_gather(ffn_in, 'mlp', axis=0, tiled=True)  42.5 us
    reduce_scatter x1, waiting for transfers between devices, body(): lax.psum_scatter(lax.dot_general(hidden, down_full, (((1,), (1,)), ((), (...  41.7 us
    all_gather x1, blocking collectives, body(): levels = lax.all_gather(my_part, 'mlp', axis=1, tiled=True)  16.6 us
    pallas_call x1, Pallas kernels, attend_window(): pl.pallas_call(_attend_kernel, grid_spec=pltpu.PrefetchScalarGridSpec(num...  16.2 us
    dot_general x1, matrix products, body(): jnp.dot(all_rows, packed[:, :2 * ff_cols], preferred_element_type=jnp.flo...  11.1 us
    dot_general x1, matrix products, body(): lax.dot_general(hidden, down_full, (((1,), (1,)), ((), ())), preferred_el...  9.58 us
    all_to_all x1, starting transfers between devices, body(): lax.all_to_all(outgoing, 'req', split_axis=0, concat_axis=0, tiled=True)  8.65 us
    all_gather x1, waiting for transfers between devices, body(): lax.all_gather(jnp.concatenate([w_gate, w_up, w_down], 1), 'req', axis=0,...  5.04 us
  transfers between devices with their start and end apart: 5, of which 4 were waited for; matrix products, arithmetic and copies ran while one was open for 18% of the time, Pallas kernels for 7%

profile of v6, /device:TPU:1, one launch (start us, length us, event | category | flops | bytes accessed | tf_op | source)
XLA Modules:
  0.0 221.3 jit_solution(13357900858454506012)
XLA Ops:
  6.5 1.3 dynamic_slice.21
  9.8 1.2 dynamic_slice.22
  12.4 1.4 fusion.19
  13.7 0.0 copy-start.6
  13.7 0.0 copy-start.7
  13.8 0.0 copy-start.9
  13.8 0.0 copy-start.2
  13.8 1.8 fusion.24
  16.3 0.0 copy-done.10
  16.3 0.7 constant_dynamic-slice_fusion.2
  19.0 0.3 fusion.33
  19.3 0.7 pad_maximum_fusion.1
  20.0 0.0 all-gather.4.cloned.1.call-update
  20.0 0.0 all-gather.8.cloned.1.call-start
  20.1 0.9 concatenate.47
  21.0 0.0 all-gather.8.cloned.1.call-update
  21.0 0.7 gather_fusion
  21.7 0.1 copy.29
  21.8 0.1 reshape.382
  21.9 1.1 constant_dynamic-slice_fusion
  23.0 0.0 copy-start.3
  23.0 0.0 copy-start.11
  23.0 1.6 gather_fusion.1
  24.6 8.6 %all-to-all-start = ((bf16[16,2,64,256]{3,2,1,0:T(8,128)(2,1)}), bf16[16,2,64,256]{3,2,1,0:T(8,128)(2,1)}, u32[]{:S(2)}, u32[]{:S(2)}) async-start(bf16[16,2,64,256]{3,2,1,0:T(8,128)(2,1)} %bitcast.11), calls=%async_computation | async-start | bytes 2097152 | tf_op jit(solution)/shard_map/all_to_all | solution.py:106
  33.3 0.0 all-gather.6.cloned.1.call-start
  33.3 0.7 fusion.36
  34.1 4.4 %fusion.26 = f32[256,1536]{0,1:T(8,128)S(1)} fusion(bf16[1536,1536]{1,0:T(8,128)(2,1)} %param.16, bf16[256,1536]{1,0:T(8,128)(2,1)S(1)} %copy-done.3, f32[1536]{0:T(1024)S(1)} %copy-done.11, f32[256]{0:T(256)S(1)} %add_rsqrt_fusion.1), kind=kOutput, calls=%fused_computation.40 | convolution fusion | flops 1209532416 | bytes 7085056 | tf_op jit(solution)/shard_map/dot_general | solution.py:113
  38.4 0.0 copy-start.4
  38.4 1.0 fusion.49
  39.5 0.6 pad_add_fusion.1.where_ref
  40.0 0.2 dynamic-slice_reduce_fusion
  40.2 0.1 copy.33
  40.4 1.6 copy.37
  42.0 1.7 copy.38
  43.6 0.5 multiply_cosine_fusion
  44.2 1.9 multiply_subtract_fusion
  46.1 1.4 fusion.23.q_ref
  47.4 1.4 all-to-all-done
  48.8 1.8 gather_fusion.2
  50.6 0.1 copy.30
  50.7 16.6 %all_gather.12 = bf16[2,512,256]{2,0,1:T(2,128)(2,1)S(1)} all-gather(bf16[2,64,256]{2,0,1:T(2,128)(2,1)S(1)} %copy.30), channel_id=1, replica_groups=mesh['req'=16,'mlp'=8] {'mlp'}, dimensions={1}, use_global_device_ids=true | all-gather | bytes 589824 | tf_op jit(solution)/shard_map/all_gather | solution.py:109
  67.3 0.7 fusion.50
  68.1 0.7 copy.39
  68.7 0.7 copy.40
  69.4 0.0 all-gather.4.cloned.1.call-done
  69.5 2.6 %pad_maximum_fusion = bf16[3584,256]{0,1:T(8,128)(2,1)} fusion(bf16[2048,256]{0,1:T(8,128)(2,1)} %all-gather.4.cloned.1.call-done, bf16[512,256]{0,1:T(8,128)(2,1)S(1)} %bitcast.48, bf16[512,256]{0,1:T(8,128)(2,1)S(1)} %bitcast.47, bf16[512,256]{0,1:T(8,128)(2,1)S(1)} %bitcast.46), kind=kLoop, calls=%fused_computation.27 | loop fusion | flops 7340032 | bytes 3670016 | tf_op jit(solution)/shard_map/concatenate | solution.py:123
  72.1 2.9 %copy.34 = bf16[3584,256]{1,0:T(8,128)(2,1)S(1)} copy(bf16[3584,256]{0,1:T(8,128)(2,1)} %pad_maximum_fusion) | data formatting | bytes 3670016 | tf_op jit(solution)/shard_map/concatenate | solution.py:123
  75.0 4.7 %gather_fusion.3 = bf16[1280,256]{1,0:T(8,128)(2,1)} fusion(bf16[3584,256]{1,0:T(8,128)(2,1)S(1)} %copy.34, s32[2048]{0:T(1024)S(1)} %pad_clamp_fusion), kind=kCustom, calls=%fused_computation.3 | custom fusion | bytes 1315840 | tf_op jit(solution)/shard_map/jit(_take)/gather | solution.py:138
  79.6 16.2 %shard_map.136 = bf16[12,256,128]{2,1,0:T(8,128)(2,1)} custom-call(s32[2]{0:T(128)} %pad_add_fusion.1.where_ref, bf16[12,256,128]{2,1,0:T(8,128)(2,1)} %fusion.23.q_ref, bf16[1280,256]{1,0:T(8,128)(2,1)} %gather_fusion.3), custom_call_target="tpu_custom_call" | custom-call | tf_op jit(solution)/shard_map/pallas_call | solution.py:50
  95.9 1.4 copy.35
  97.3 0.0 copy-start.8
  97.3 3.9 %multiply_reduce_fusion = (f32[256]{0:T(256)S(1)}, f32[256,1536]{1,0:T(8,128)S(1)}) fusion(bf16[256,1536]{0,1:T(8,128)(2,1)S(1)} %bitcast.43, bf16[1536,1536]{1,0:T(8,128)(2,1)} %param.18, bf16[256,1536]{1,0:T(8,128)(2,1)S(1)} %copy-done.3), kind=kOutput, calls=%fused_computation.35 | convolution fusion | flops 1210318592 | bytes 7865344 | tf_op jit(solution)/shard_map/dot_general | solution.py:142
  101.2 1.1 multiply_convert_fusion
  102.3 0.0 all-gather.6.cloned.1.call-update
  102.3 0.3 reduce-scatter.2.cloned.1.call-start
  102.6 5.0 %all-gather.8.cloned.1.call-done = bf16[1536,1728]{1,0:T(8,128)(2,1)} async-done(((bf16[96,1728]{1,0:T(8,128)(2,1)}), bf16[1536,1728]{1,0:T(8,128)(2,1)}) %all-gather.8.cloned.1.call-update) | async-done | bytes 5308432 | tf_op jit(solution)/shard_map/all_gather | solution.py:96
  107.7 42.5 %all-gather.6.cloned.1.call-done = bf16[2048,1536]{1,0:T(8,128)(2,1)} async-done(((bf16[256,1536]{1,0:T(8,128)(2,1)}), bf16[2048,1536]{1,0:T(8,128)(2,1)}) %all-gather.6.cloned.1.call-update) | async-done | bytes 6291472 | tf_op jit(solution)/shard_map/all_gather | solution.py:145
  150.2 11.1 %fusion.9 = f32[2048,1152]{0,1:T(8,128)S(1)} fusion(bf16[2048,1536]{1,0:T(8,128)(2,1)} %all-gather.6.cloned.1.call-done, bf16[1536,1728]{1,0:T(8,128)(2,1)} %all-gather.8.cloned.1.call-done), kind=kOutput, calls=%fused_computation.15 | convolution fusion | flops 7247757312 | bytes 19267584 | tf_op jit(solution)/shard_map/dot_general | solution.py:146
  161.3 9.6 %convolution_convert_fusion = bf16[2048,1536]{1,0:T(8,128)(2,1)} fusion(f32[2048,1152]{0,1:T(8,128)S(1)} %fusion.9, bf16[1536,1728]{1,0:T(8,128)(2,1)} %all-gather.8.cloned.1.call-done), kind=kOutput, calls=%fused_computation.4 | convolution fusion | flops 3638820864 | bytes 17694720 | tf_op jit(solution)/shard_map/dot_general | solution.py:151
  170.9 0.0 reduce-scatter.2.cloned.1.call-update
  170.9 0.0 copy-start.1
  170.9 41.7 %reduce-scatter.2.cloned.1.call-done = bf16[256,1536]{1,0:T(8,128)(2,1)} async-done(((bf16[2048,1536]{1,0:T(8,128)(2,1)}), bf16[256,1536]{1,0:T(8,128)(2,1)}) %reduce-scatter.2.cloned.1.call-update) | async-done | bytes 786448 | tf_op jit(solution)/shard_map/reduce_scatter | solution.py:150
  212.6 2.2 add_convert_fusion
  214.8 0.0 copy-done.1
  (27 shorter events, 0.1 us)
Async XLA Ops:
  6.5 7.2 %copy-start = (bf16[1536,256]{1,0:T(8,128)(2,1)S(1)}, bf16[1536,256]{1,0:T(8,128)(2,1)}, u32[]{:S(2)}) copy-start(bf16[1536,256]{1,0:T(8,128)(2,1)} %param.17) | copy-start | bytes 2359300
  6.5 9.8 %copy-start.10 = (s32[3,128]{1,0:T(4,128)S(1)}, s32[3,128]{1,0:T(4,128)}, u32[]{:S(2)}) copy-start(s32[3,128]{1,0:T(4,128)} %param.27) | copy-start | bytes 4612
  6.5 62.9 %all-gather.4.cloned.1.call-start = ((), (), s32[]{:S(2)}) async-start(), calls=%async_computation.2 | async-start | bytes 1179648 | tf_op jit(solution)/shard_map/all_gather | solution.py:121
  13.7 6.4 %copy-start.5 = (bf16[96,576]{1,0:T(8,128)(2,1)S(1)}, bf16[96,576]{1,0:T(8,128)(2,1)}, u32[]{:S(2)}) copy-start(bf16[96,576]{1,0:T(8,128)(2,1)} %param.20) | copy-start | bytes 331780
  13.7 6.4 %copy-start.6 = (bf16[96,576]{1,0:T(8,128)(2,1)S(1)}, bf16[96,576]{1,0:T(8,128)(2,1)}, u32[]{:S(2)}) copy-start(bf16[96,576]{1,0:T(8,128)(2,1)} %param.21) | copy-start | bytes 331780
  13.7 6.4 %copy-start.7 = (bf16[96,576]{1,0:T(8,128)(2,1)S(1)}, bf16[96,576]{1,0:T(8,128)(2,1)}, u32[]{:S(2)}) copy-start(bf16[96,576]{1,0:T(8,128)(2,1)} %param.22) | copy-start | bytes 331780
  13.8 7.2 %copy-start.9 = (s32[16]{0:T(128)S(1)}, s32[16]{0:T(128)}, u32[]{:S(2)}) copy-start(s32[16]{0:T(128)} %param.25) | copy-start | bytes 196
  13.8 7.3 %copy-start.2 = (s32[128]{0:T(128)S(1)}, s32[128]{0:T(128)}, u32[]{:S(2)}) copy-start(s32[128]{0:T(128)} %param.26) | copy-start | bytes 1540
  20.0 87.6 %all-gather.8.cloned.1.call-start = ((), (), s32[]{:S(2)}) async-start(), calls=%async_computation.4 | async-start | bytes 5849088 | tf_op jit(solution)/shard_map/all_gather | solution.py:96
  23.0 11.0 %copy-start.3 = (bf16[256,1536]{1,0:T(8,128)(2,1)S(1)}, bf16[256,1536]{1,0:T(8,128)(2,1)}, u32[]{:S(2)}) copy-start(bf16[256,1536]{1,0:T(8,128)(2,1)} %param.14) | copy-start | bytes 2359300
  23.0 11.0 %copy-start.11 = (f32[1536]{0:T(1024)S(1)}, f32[1536]{0:T(1024)}, u32[]{:S(2)}) copy-start(f32[1536]{0:T(1024)} %param.15) | copy-start | bytes 18436
  24.6 24.2 %all-to-all-start = ((bf16[16,2,64,256]{3,2,1,0:T(8,128)(2,1)}), bf16[16,2,64,256]{3,2,1,0:T(8,128)(2,1)}, u32[]{:S(2)}, u32[]{:S(2)}) async-start(bf16[16,2,64,256]{3,2,1,0:T(8,128)(2,1)} %bitcast.11), calls=%async_computation | async-start | bytes 2097152 | tf_op jit(solution)/shard_map/all_to_all | solution.py:106
  33.3 116.9 %all-gather.6.cloned.1.call-start = ((), (), s32[]{:S(2)}) async-start(), calls=%async_computation.3 | async-start | bytes 7077888 | tf_op jit(solution)/shard_map/all_gather | solution.py:145
  38.4 1.8 copy-start.4
  97.3 3.9 %copy-start.8 = (f32[1536]{0:T(1024)S(1)}, f32[1536]{0:T(1024)}, u32[]{:S(2)}) copy-start(f32[1536]{0:T(1024)} %param.19) | copy-start | bytes 18436
  102.3 110.3 %reduce-scatter.2.cloned.1.call-start = ((), (), s32[]{:S(2)}) async-start(), calls=%async_computation.5 | async-start | bytes 7077888 | tf_op jit(solution)/shard_map/reduce_scatter | solution.py:150
  170.9 43.9 %copy-start.1 = (bf16[1536,256]{1,0:T(8,128)(2,1)S(1)}, bf16[1536,256]{1,0:T(8,128)(2,1)}, u32[]{:S(2)}) copy-start(bf16[1536,256]{1,0:T(8,128)(2,1)} %param.17) | copy-start | bytes 2359300
Sparse Core Ops, SparseCore 0:
  20.1 26.9 all-gather.3
  49.3 58.3 all-gather.7
  109.3 40.7 all-gather.5
  171.0 41.5 reduce-scatter.1

commit v7 on v5

--- a/solution.py
+++ b/solution.py
@@ -1,6 +1,8 @@
 import jax
 import jax.numpy as jnp
 from jax import lax
+from jax.experimental import pallas as pl
+from jax.experimental.pallas import tpu as pltpu
 from jax.sharding import PartitionSpec as P
 
 HEADS = 12
@@ -25,6 +27,38 @@
     first = values[..., :half_dim]
     second = values[..., half_dim:]
     return jnp.concatenate([first * cosine - second * sine, first * sine + second * cosine], -1)
+
+
+def _attend_kernel(bias_ref, q_ref, kv_ref, o_ref):
+    keys = kv_ref[:, :HD]
+    vals = kv_ref[:, HD:]
+    bias = bias_ref[...]
+    for head in range(q_ref.shape[0]):
+        scores = lax.dot_general(
+            q_ref[head], keys, (((1,), (1,)), ((), ())), preferred_element_type=jnp.float32
+        )
+        scores = scores + bias
+        top = jnp.max(scores, axis=1, keepdims=True)
+        weights = jnp.exp(scores - top)
+        denom = jnp.sum(weights, axis=1, keepdims=True)
+        mixed = jnp.dot(weights.astype(jnp.bfloat16), vals, preferred_element_type=jnp.float32)
+        o_ref[head] = (mixed / denom).astype(o_ref.dtype)
+
+
+def attend_window(queries_hm, window, bias, heads_per_step=4):
+    heads, rows, _ = queries_hm.shape
+    span = window.shape[0]
+    return pl.pallas_call(
+        _attend_kernel,
+        grid=(heads // heads_per_step,),
+        in_specs=[
+            pl.BlockSpec((rows, span), lambda h: (0, 0)),
+            pl.BlockSpec((heads_per_step, rows, HD), lambda h: (h, 0, 0)),
+            pl.BlockSpec((span, 2 * HD), lambda h: (0, 0)),
+        ],
+        out_specs=pl.BlockSpec((heads_per_step, rows, HD), lambda h: (h, 0, 0)),
+        out_shape=jax.ShapeDtypeStruct((heads, rows, HD), jnp.bfloat16),
+    )(bias, queries_hm, window)
 
 
 def body(
@@ -102,20 +136,10 @@
     )
     window = jnp.take(sources, source_row, axis=0, mode="clip")
     spacing = query_at[:, None] - key_at[None, :]
-    allowed = ((spacing >= 0) & (spacing < WINDOW))[:, None, :]
-    scores = jnp.einsum(
-        "thd,kd->thk", queries, window[:, :HD], preferred_element_type=jnp.float32
-    )
-    top = jnp.max(jnp.where(allowed, scores, -jnp.inf), axis=-1, keepdims=True)
-    weights = jnp.where(allowed, jnp.exp(scores - top), 0.0)
-    denom = jnp.sum(weights, axis=-1)
-    mixed = jnp.einsum(
-        "thk,kd->thd",
-        weights.astype(jnp.bfloat16),
-        window[:, HD:],
-        preferred_element_type=jnp.float32,
-    )
-    context = (mixed / denom[..., None]).reshape(tok_rows, HEADS * HD).astype(jnp.bfloat16)
+    allowed = (key_at[None, :] >= 0) & (spacing >= 0) & (spacing < WINDOW)
+    bias = jnp.where(allowed, 0.0, -jnp.inf).astype(jnp.float32)
+    heads_first = attend_window(jnp.transpose(queries, (1, 0, 2)), window, bias)
+    context = jnp.transpose(heads_first, (1, 0, 2)).reshape(tok_rows, HEADS * HD)
     attn_out = jnp.dot(context, w_out, preferred_element_type=jnp.float32)
     resid = (tokens.astype(jnp.float32) + attn_out).astype(jnp.bfloat16)
     ffn_in = rms_scale(resid, ffn_gain).astype(jnp.bfloat16)

time: 222 us -> 222 us (level)
  matrix products: 48.2 us -> 30.8 us
  Pallas kernels: 0 us -> 10.1 us
  waiting for transfers between devices: 90.2 us -> 94.4 us
    sub x1 -> x0, matrix products: 11.3 us -> none  [body(): weights = jnp.where(allowed, jnp.exp(scores - top), 0.0)]
    pallas_call x0 -> x1, Pallas kernels: none -> 10.1 us  [attend_window(): pl.pallas_call(_attend_kernel, grid=(heads // heads_per_step,), in_specs=...]
    dot_general x1 -> x0, matrix products: 6.03 us -> none  [body(): jnp.einsum('thk,kd->thd', weights.astype(jnp.bfloat16), window[:, HD:], p...]
    all_gather x1, waiting for transfers between devices: 5.82 us -> 10.1 us  [body(): lax.all_gather(jnp.concatenate([w_gate, w_up, w_down], 1), 'req', axis=0,...]
    transpose x0 -> x1, other arithmetic: none -> 3.24 us  [body(): heads_first = attend_window(jnp.transpose(queries, (1, 0, 2)), window, bias)]
    unnamed x33 -> x29, local copies, waits for them, and re-layouts: 4.84 us -> 4.79 us
  transfers between devices with their start and end apart: 5 -> 5, of which waited for: 3 -> 3; matrix products, arithmetic and copies ran while one was open for 26% -> 20% of each run, Pallas kernels for 0% -> 5%
where the time goes in v7:
time: 222 us; the launch traced here: 221 us
  waiting for transfers between devices  94.4 us (43%)
  matrix products  30.8 us (14%)
  local copies, waits for them, and re-layouts  25.2 us (11%)
  between operations  19.4 us (9%)
  other arithmetic  17.8 us (8%)
  blocking collectives  14.4 us (6%)
  Pallas kernels  10.1 us (5%)
  starting transfers between devices  9 us (4%)
    all_gather x1, waiting for transfers between devices, body(): all_rows = lax.all_gather(ffn_in, 'mlp', axis=0, tiled=True)  42.6 us
    reduce_scatter x1, waiting for transfers between devices, body(): lax.psum_scatter(lax.dot_general(hidden, down_full, (((1,), (1,)), ((), (...  41.6 us
    all_gather x1, blocking collectives, body(): levels = lax.all_gather(my_part, 'mlp', axis=1, tiled=True)  14.4 us
    dot_general x1, matrix products, body(): jnp.dot(all_rows, packed[:, :2 * ff_cols], preferred_element_type=jnp.flo...  11.1 us
    all_gather x1, waiting for transfers between devices, body(): lax.all_gather(jnp.concatenate([w_gate, w_up, w_down], 1), 'req', axis=0,...  10.1 us
    pallas_call x1, Pallas kernels, attend_window(): pl.pallas_call(_attend_kernel, grid=(heads // heads_per_step,), in_specs=...  10.1 us
    dot_general x1, matrix products, body(): lax.dot_general(hidden, down_full, (((1,), (1,)), ((), ())), preferred_el...  9.57 us
    all_to_all x1, starting transfers between devices, body(): lax.all_to_all(outgoing, 'req', split_axis=0, concat_axis=0, tiled=True)  8.65 us
  transfers between devices with their start and end apart: 5, of which 3 were waited for; matrix products, arithmetic and copies ran while one was open for 20% of the time, Pallas kernels for 5%

profile of v7, /device:TPU:1, one launch (start us, length us, event | category | flops | bytes accessed | tf_op | source)
XLA Modules:
  0.0 221.2 jit_solution(2815701066328586911)
XLA Ops:
  6.5 1.3 dynamic_slice.21
  9.8 1.2 dynamic_slice.22
  12.4 1.4 fusion.19
  13.7 0.0 copy-start.6
  13.7 0.0 copy-start.7
  13.8 0.0 copy-done
  13.8 0.0 copy-start.9
  13.8 0.0 copy-start.2
  13.8 1.8 fusion.27
  16.3 0.0 copy-done.10
  16.3 0.7 constant_dynamic-slice_fusion.2
  19.0 0.3 fusion.36
  19.3 0.7 pad_maximum_fusion.1
  20.0 0.0 all-gather.4.cloned.1.call-update
  20.0 0.0 all-gather.8.cloned.1.call-start
  20.1 0.9 concatenate.47
  21.0 0.0 all-gather.8.cloned.1.call-update
  21.0 0.7 gather_fusion
  21.7 0.1 copy.29
  21.8 0.1 reshape.392
  21.9 1.1 constant_dynamic-slice_fusion
  23.0 0.0 copy-start.3
  23.0 0.0 copy-start.11
  23.0 1.6 gather_fusion.1
  24.7 8.6 %all-to-all-start = ((bf16[16,2,64,256]{3,2,1,0:T(8,128)(2,1)}), bf16[16,2,64,256]{3,2,1,0:T(8,128)(2,1)}, u32[]{:S(2)}, u32[]{:S(2)}) async-start(bf16[16,2,64,256]{3,2,1,0:T(8,128)(2,1)} %bitcast.9), calls=%async_computation | async-start | bytes 2097152 | tf_op jit(solution)/shard_map/all_to_all | solution.py:105
  33.3 0.0 all-gather.6.cloned.1.call-start
  33.4 4.4 %fusion.29 = f32[256,1536]{0,1:T(8,128)S(1)} fusion(bf16[1536,1536]{1,0:T(8,128)(2,1)} %param.16, bf16[256,1536]{1,0:T(8,128)(2,1)S(1)} %copy-done.3, f32[1536]{0:T(1024)S(1)} %copy-done.11, f32[256]{0:T(256)S(1)} %add_rsqrt_fusion.1), kind=kOutput, calls=%fused_computation.45 | convolution fusion | flops 1209532416 | bytes 7085056 | tf_op jit(solution)/shard_map/dot_general | solution.py:112
  37.8 1.0 fusion.53
  38.8 1.6 copy.37
  40.4 1.6 copy.38
  42.1 0.5 multiply_cosine_fusion
  42.6 0.0 copy-start.4
  42.6 3.5 %multiply_subtract_fusion = (f32[256,12,64]{2,0,1:T(8,128)}, f32[256,12,64]{2,0,1:T(8,128)}) fusion(f32[256,12,64]{2,0,1:T(8,128)} %copy.38, f32[256,12,64]{2,0,1:T(8,128)S(1)} %copy.37, f32[256,64]{1,0:T(8,128)S(1)} %get-tuple-element.17, f32[256,64]{1,0:T(8,128)S(1)} %get-tuple-element.16), kind=kLoop, calls=%fused_computation.39 | loop fusion | flops 1179648 | bytes 3276800 | tf_op jit(solution)/shard_map/sub | solution.py:29
  46.2 0.2 dynamic-slice_reduce_fusion
  46.4 0.1 copy.33
  46.5 0.6 fusion.39
  47.2 3.2 %fusion.26.q_ref = bf16[12,256,128]{2,1,0:T(8,128)(2,1)} fusion(f32[256,12,64]{2,0,1:T(8,128)} %get-tuple-element.6, f32[256,12,64]{2,0,1:T(8,128)} %get-tuple-element.5), kind=kLoop, calls=%fused_computation.43 | loop fusion | flops 1179648 | bytes 2359296 | tf_op jit(solution)/shard_map/transpose | solution.py:141
  50.4 1.5 fusion.25.bias_ref
  51.9 0.0 all-to-all-done
  51.9 1.8 gather_fusion.2
  53.7 0.1 copy.30
  53.8 14.4 %all_gather.12 = bf16[2,512,256]{2,0,1:T(2,128)(2,1)S(1)} all-gather(bf16[2,64,256]{2,0,1:T(2,128)(2,1)S(1)} %copy.30), channel_id=1, replica_groups=mesh['req'=16,'mlp'=8] {'mlp'}, dimensions={1}, use_global_device_ids=true | all-gather | bytes 589824 | tf_op jit(solution)/shard_map/all_gather | solution.py:108
  68.2 0.7 fusion.54
  69.0 0.7 copy.39
  69.7 0.7 copy.40
  70.3 0.0 all-gather.4.cloned.1.call-done
  70.4 2.6 %pad_maximum_fusion = bf16[3584,256]{0,1:T(8,128)(2,1)} fusion(bf16[2048,256]{0,1:T(8,128)(2,1)} %all-gather.4.cloned.1.call-done, bf16[512,256]{0,1:T(8,128)(2,1)S(1)} %bitcast.46, bf16[512,256]{0,1:T(8,128)(2,1)S(1)} %bitcast.45, bf16[512,256]{0,1:T(8,128)(2,1)S(1)} %bitcast.44), kind=kLoop, calls=%fused_computation.29 | loop fusion | flops 7340032 | bytes 3670016 | tf_op jit(solution)/shard_map/concatenate | solution.py:122
  73.0 2.9 %copy.34 = bf16[3584,256]{1,0:T(8,128)(2,1)S(1)} copy(bf16[3584,256]{0,1:T(8,128)(2,1)} %pad_maximum_fusion) | data formatting | bytes 3670016 | tf_op jit(solution)/shard_map/concatenate | solution.py:122
  75.9 4.7 %gather_fusion.3 = bf16[1280,256]{1,0:T(8,128)(2,1)} fusion(bf16[3584,256]{1,0:T(8,128)(2,1)S(1)} %copy.34, s32[2048]{0:T(1024)S(1)} %pad_clamp_fusion), kind=kCustom, calls=%fused_computation.3 | custom fusion | bytes 1315840 | tf_op jit(solution)/shard_map/jit(_take)/gather | solution.py:137
  80.6 10.1 %shard_map.136 = bf16[12,256,128]{2,1,0:T(8,128)(2,1)} custom-call(f32[256,1280]{1,0:T(8,128)} %fusion.25.bias_ref, bf16[12,256,128]{2,1,0:T(8,128)(2,1)} %fusion.26.q_ref, bf16[1280,256]{1,0:T(8,128)(2,1)} %gather_fusion.3), custom_call_target="tpu_custom_call" | custom-call | tf_op jit(solution)/shard_map/pallas_call | solution.py:51
  90.7 1.4 copy.35
  92.1 0.0 copy-start.8
  92.1 3.9 %multiply_reduce_fusion = (f32[256]{0:T(256)S(1)}, f32[256,1536]{1,0:T(8,128)S(1)}) fusion(bf16[256,1536]{0,1:T(8,128)(2,1)S(1)} %bitcast.41, bf16[1536,1536]{1,0:T(8,128)(2,1)} %param.18, bf16[256,1536]{1,0:T(8,128)(2,1)S(1)} %copy-done.3), kind=kOutput, calls=%fused_computation.37 | convolution fusion | flops 1210318592 | bytes 7865344 | tf_op jit(solution)/shard_map/dot_general | solution.py:143
  96.1 1.1 multiply_convert_fusion
  97.1 0.0 all-gather.6.cloned.1.call-update
  97.2 0.3 reduce-scatter.2.cloned.1.call-start
  97.4 10.1 %all-gather.8.cloned.1.call-done = bf16[1536,1728]{1,0:T(8,128)(2,1)} async-done(((bf16[96,1728]{1,0:T(8,128)(2,1)}), bf16[1536,1728]{1,0:T(8,128)(2,1)}) %all-gather.8.cloned.1.call-update) | async-done | bytes 5308432 | tf_op jit(solution)/shard_map/all_gather | solution.py:95
  107.6 42.6 %all-gather.6.cloned.1.call-done = bf16[2048,1536]{1,0:T(8,128)(2,1)} async-done(((bf16[256,1536]{1,0:T(8,128)(2,1)}), bf16[2048,1536]{1,0:T(8,128)(2,1)}) %all-gather.6.cloned.1.call-update) | async-done | bytes 6291472 | tf_op jit(solution)/shard_map/all_gather | solution.py:146
  150.2 11.1 %fusion.9 = f32[2048,1152]{0,1:T(8,128)S(1)} fusion(bf16[2048,1536]{1,0:T(8,128)(2,1)} %all-gather.6.cloned.1.call-done, bf16[1536,1728]{1,0:T(8,128)(2,1)} %all-gather.8.cloned.1.call-done), kind=kOutput, calls=%fused_computation.15 | convolution fusion | flops 7247757312 | bytes 19267584 | tf_op jit(solution)/shard_map/dot_general | solution.py:147
  161.3 9.6 %convolution_convert_fusion = bf16[2048,1536]{1,0:T(8,128)(2,1)} fusion(f32[2048,1152]{0,1:T(8,128)S(1)} %fusion.9, bf16[1536,1728]{1,0:T(8,128)(2,1)} %all-gather.8.cloned.1.call-done), kind=kOutput, calls=%fused_computation.4 | convolution fusion | flops 3638820864 | bytes 17694720 | tf_op jit(solution)/shard_map/dot_general | solution.py:152
  170.9 0.0 reduce-scatter.2.cloned.1.call-update
  170.9 0.0 copy-start.1
  170.9 41.6 %reduce-scatter.2.cloned.1.call-done = bf16[256,1536]{1,0:T(8,128)(2,1)} async-done(((bf16[2048,1536]{1,0:T(8,128)(2,1)}), bf16[256,1536]{1,0:T(8,128)(2,1)}) %reduce-scatter.2.cloned.1.call-update) | async-done | bytes 786448 | tf_op jit(solution)/shard_map/reduce_scatter | solution.py:151
  212.4 2.2 add_convert_fusion
  (30 shorter events, 0.2 us)
Async XLA Ops:
  6.5 7.2 %copy-start = (bf16[1536,256]{1,0:T(8,128)(2,1)S(1)}, bf16[1536,256]{1,0:T(8,128)(2,1)}, u32[]{:S(2)}) copy-start(bf16[1536,256]{1,0:T(8,128)(2,1)} %param.17) | copy-start | bytes 2359300
  6.5 9.8 %copy-start.10 = (s32[3,128]{1,0:T(4,128)S(1)}, s32[3,128]{1,0:T(4,128)}, u32[]{:S(2)}) copy-start(s32[3,128]{1,0:T(4,128)} %param.27) | copy-start | bytes 4612
  6.5 63.8 %all-gather.4.cloned.1.call-start = ((), (), s32[]{:S(2)}) async-start(), calls=%async_computation.2 | async-start | bytes 1179648 | tf_op jit(solution)/shard_map/all_gather | solution.py:120
  13.7 6.3 %copy-start.5 = (bf16[96,576]{1,0:T(8,128)(2,1)S(1)}, bf16[96,576]{1,0:T(8,128)(2,1)}, u32[]{:S(2)}) copy-start(bf16[96,576]{1,0:T(8,128)(2,1)} %param.20) | copy-start | bytes 331780
  13.7 6.3 %copy-start.6 = (bf16[96,576]{1,0:T(8,128)(2,1)S(1)}, bf16[96,576]{1,0:T(8,128)(2,1)}, u32[]{:S(2)}) copy-start(bf16[96,576]{1,0:T(8,128)(2,1)} %param.21) | copy-start | bytes 331780
  13.7 6.3 %copy-start.7 = (bf16[96,576]{1,0:T(8,128)(2,1)S(1)}, bf16[96,576]{1,0:T(8,128)(2,1)}, u32[]{:S(2)}) copy-start(bf16[96,576]{1,0:T(8,128)(2,1)} %param.22) | copy-start | bytes 331780
  13.8 7.2 %copy-start.9 = (s32[16]{0:T(128)S(1)}, s32[16]{0:T(128)}, u32[]{:S(2)}) copy-start(s32[16]{0:T(128)} %param.25) | copy-start | bytes 196
  13.8 7.2 %copy-start.2 = (s32[128]{0:T(128)S(1)}, s32[128]{0:T(128)}, u32[]{:S(2)}) copy-start(s32[128]{0:T(128)} %param.26) | copy-start | bytes 1540
  20.0 87.6 %all-gather.8.cloned.1.call-start = ((), (), s32[]{:S(2)}) async-start(), calls=%async_computation.4 | async-start | bytes 5849088 | tf_op jit(solution)/shard_map/all_gather | solution.py:95
  23.0 10.4 %copy-start.3 = (bf16[256,1536]{1,0:T(8,128)(2,1)S(1)}, bf16[256,1536]{1,0:T(8,128)(2,1)}, u32[]{:S(2)}) copy-start(bf16[256,1536]{1,0:T(8,128)(2,1)} %param.14) | copy-start | bytes 2359300
  23.0 10.4 %copy-start.11 = (f32[1536]{0:T(1024)S(1)}, f32[1536]{0:T(1024)}, u32[]{:S(2)}) copy-start(f32[1536]{0:T(1024)} %param.15) | copy-start | bytes 18436
  24.7 27.3 %all-to-all-start = ((bf16[16,2,64,256]{3,2,1,0:T(8,128)(2,1)}), bf16[16,2,64,256]{3,2,1,0:T(8,128)(2,1)}, u32[]{:S(2)}, u32[]{:S(2)}) async-start(bf16[16,2,64,256]{3,2,1,0:T(8,128)(2,1)} %bitcast.9), calls=%async_computation | async-start | bytes 2097152 | tf_op jit(solution)/shard_map/all_to_all | solution.py:105
  33.3 116.9 %all-gather.6.cloned.1.call-start = ((), (), s32[]{:S(2)}) async-start(), calls=%async_computation.3 | async-start | bytes 7077888 | tf_op jit(solution)/shard_map/all_gather | solution.py:146
  42.6 3.8 %copy-start.4 = (bf16[1,512,256]{2,1,0:T(8,128)(2,1)S(1)}, bf16[1,512,256]{2,1,0:T(8,128)(2,1)}, u32[]{:S(2)}) copy-start(bf16[1,512,256]{2,1,0:T(8,128)(2,1)} %param.24) | copy-start | bytes 786436
  92.1 4.0 %copy-start.8 = (f32[1536]{0:T(1024)S(1)}, f32[1536]{0:T(1024)}, u32[]{:S(2)}) copy-start(f32[1536]{0:T(1024)} %param.19) | copy-start | bytes 18436
  97.2 115.3 %reduce-scatter.2.cloned.1.call-start = ((), (), s32[]{:S(2)}) async-start(), calls=%async_computation.5 | async-start | bytes 7077888 | tf_op jit(solution)/shard_map/reduce_scatter | solution.py:151
  170.9 43.8 %copy-start.1 = (bf16[1536,256]{1,0:T(8,128)(2,1)S(1)}, bf16[1536,256]{1,0:T(8,128)(2,1)}, u32[]{:S(2)}) copy-start(bf16[1536,256]{1,0:T(8,128)(2,1)} %param.17) | copy-start | bytes 2359300
Sparse Core Ops, SparseCore 0:
  20.1 26.9 all-gather.3
  49.3 58.2 all-gather.7
  109.3 40.8 all-gather.5
  171.0 41.3 reduce-scatter.1

commit v8 on v7

--- a/solution.py
+++ b/solution.py
@@ -117,13 +117,16 @@
     new_keys = rotate(keyval_full[:, None, :HD], query_at)[:, 0].astype(jnp.bfloat16)
     new_vals = keyval_full[:, HD:].astype(jnp.bfloat16)
     new_keyval = jnp.concatenate([new_keys, new_vals], 1)
-    piece = lax.all_gather(new_keyval, "mlp", axis=0, tiled=True)
-
-    sources = jnp.concatenate([levels[0], levels[1], own_prefix[0], piece], 0)
-    seq_len = 3 * seg_slot + piece.shape[0]
-    span = WINDOW + tok_rows
-    first = jnp.clip(total + position_group * tok_rows - WINDOW, 0, seq_len - span)
-    key_at = first + jnp.arange(span, dtype=jnp.int32)
+    back = WINDOW // tok_rows
+    blocks = [
+        lax.ppermute(new_keyval, "mlp", [(i, (i + shift) % n_mlp) for i in range(n_mlp)])
+        for shift in range(back, 0, -1)
+    ]
+    sources = jnp.concatenate([levels[0], levels[1], own_prefix[0]] + blocks + [new_keyval], 0)
+    span = (back + 1) * tok_rows
+    first = total + position_group * tok_rows - WINDOW
+    row = jnp.arange(span, dtype=jnp.int32)
+    key_at = first + row
     len_cut = len_zero + len_one
     source_row = jnp.where(
         key_at < len_zero,
@@ -131,7 +134,7 @@
         jnp.where(
             key_at < len_cut,
             key_at - len_zero + seg_slot,
-            jnp.where(key_at < total, key_at - len_cut + 2 * seg_slot, key_at - total + 3 * seg_slot),
+            jnp.where(key_at < total, key_at - len_cut + 2 * seg_slot, row + 3 * seg_slot),
         ),
     )
     window = jnp.take(sources, source_row, axis=0, mode="clip")

time: 222 us -> 208 us (0.937)
  waiting for transfers between devices: 94.4 us -> 82.6 us
  other arithmetic: 17.8 us -> 11.1 us
  starting transfers between devices: 9 us -> 13.8 us
    all_gather x1, waiting for transfers between devices: 10.1 us -> 0.02 us  [body(): lax.all_gather(jnp.concatenate([w_gate, w_up, w_down], 1), 'req', axis=0,...]
    ppermute x0 -> x4, starting transfers between devices: none -> 5.94 us  [body(): lax.ppermute(new_keyval, 'mlp', [(i, (i + shift) % n_mlp) for i in range(...]
    ppermute x0 -> x4, local copies, waits for them, and re-layouts: none -> 3.11 us  [body(): lax.ppermute(new_keyval, 'mlp', [(i, (i + shift) % n_mlp) for i in range(...]
    concatenate x1 -> x2, local copies, waits for them, and re-layouts: 2.88 us -> 0.11 us  [the longest x1 0.1 us: body(): new_keyval = jnp.concatenate([new_keys, new_vals], 1)]
    concatenate x1 -> x0, other arithmetic: 2.63 us -> none  [body(): sources = jnp.concatenate([levels[0], levels[1], own_prefix[0], piece], 0)]
    unnamed x29 -> x27, local copies, waits for them, and re-layouts: 4.79 us -> 4.35 us
  transfers between devices with their start and end apart: 5 -> 8, of which waited for: 3 -> 2; matrix products, arithmetic and copies ran while one was open for 20% -> 20% of each run, Pallas kernels for 5% -> 5%
where the time goes in v8:
time: 208 us; the launch traced here: 207 us
  waiting for transfers between devices  82.6 us (40%)
  matrix products  29.3 us (14%)
  local copies, waits for them, and re-layouts  25.8 us (12%)
  between operations  19.3 us (9%)
  blocking collectives  14.7 us (7%)
  starting transfers between devices  13.8 us (7%)
  other arithmetic  11.1 us (5%)
  Pallas kernels  10.1 us (5%)
    reduce_scatter x1, waiting for transfers between devices, body(): lax.psum_scatter(lax.dot_general(hidden, down_full, (((1,), (1,)), ((), (...  41.7 us
    all_gather x1, waiting for transfers between devices, body(): all_rows = lax.all_gather(ffn_in, 'mlp', axis=0, tiled=True)  40.8 us
    all_gather x1, blocking collectives, body(): levels = lax.all_gather(my_part, 'mlp', axis=1, tiled=True)  14.7 us
    dot_general x1, matrix products, body(): jnp.dot(all_rows, packed[:, :2 * ff_cols], preferred_element_type=jnp.flo...  11.1 us
    pallas_call x1, Pallas kernels, attend_window(): pl.pallas_call(_attend_kernel, grid=(heads // heads_per_step,), in_specs=...  10.1 us
    dot_general x1, matrix products, body(): lax.dot_general(hidden, down_full, (((1,), (1,)), ((), ())), preferred_el...  9.43 us
    all_to_all x1, starting transfers between devices, body(): lax.all_to_all(outgoing, 'req', split_axis=0, concat_axis=0, tiled=True)  7.82 us
    ppermute x4, starting transfers between devices, body(): lax.ppermute(new_keyval, 'mlp', [(i, (i + shift) % n_mlp) for i in range(...  5.94 us
  transfers between devices with their start and end apart: 8, of which 2 were waited for; matrix products, arithmetic and copies ran while one was open for 20% of the time, Pallas kernels for 5%

profile of v8, /device:TPU:1, one launch (start us, length us, event | category | flops | bytes accessed | tf_op | source)
XLA Modules:
  0.0 206.7 jit_solution(15703755610811772376)
XLA Ops:
  6.5 2.0 concatenate.47
  8.6 0.0 all-gather.5.cloned.1.call-update
  8.6 0.0 copy-start.7
  8.6 1.2 dynamic_slice.21
  11.8 1.2 dynamic_slice.22
  14.3 0.0 copy-done.3
  14.3 0.2 fusion.19
  14.6 0.0 copy-start.6
  14.6 0.0 copy-start.2
  14.6 0.6 fusion.29
  15.9 0.6 constant_dynamic-slice_fusion.2
  18.4 0.3 fusion.38
  18.7 2.6 %collective-permute-start.3 = (bf16[256,256]{0,1:T(8,128)(2,1)S(1)}, bf16[256,256]{0,1:T(8,128)(2,1)}, u32[]{:S(2)}, u32[]{:S(2)}) collective-permute-start(bf16[256,256]{0,1:T(8,128)(2,1)S(1)} %pad_maximum_fusion), channel_id=1, source_target_pairs={{0,1},{1,2},{2,3},{3,4},{4,5},{5,6},{6,7},{7,0},{8,9},{9,10},{10,1... | collective-permute-start | bytes 393224 | tf_op jit(solution)/shard_map/ppermute | solution.py:122
  21.3 1.2 collective-permute-start.2
  22.6 1.6 collective-permute-start.1
  24.1 0.5 collective-permute-start
  24.7 0.7 gather_fusion
  25.4 0.1 copy.24
  25.5 0.1 reshape.392
  25.6 0.0 copy-done.5
  25.6 1.1 constant_dynamic-slice_fusion
  26.7 1.6 gather_fusion.1
  28.3 7.8 %all-to-all-start = ((bf16[16,2,64,256]{3,2,1,0:T(8,128)(2,1)}), bf16[16,2,64,256]{3,2,1,0:T(8,128)(2,1)}, u32[]{:S(2)}, u32[]{:S(2)}) async-start(bf16[16,2,64,256]{3,2,1,0:T(8,128)(2,1)} %bitcast.9), calls=%async_computation | async-start | bytes 2097152 | tf_op jit(solution)/shard_map/all_to_all | solution.py:105
  36.1 0.0 all-gather.3.cloned.1.call-start
  36.1 0.1 copy.29
  36.3 0.8 dynamic-slice_reduce_fusion
  37.0 4.3 %fusion.31 = f32[256,1536]{0,1:T(8,128)S(1)} fusion(bf16[1536,1536]{1,0:T(8,128)(2,1)} %param.16, bf16[256,1536]{1,0:T(8,128)(2,1)S(1)} %copy-done.3, f32[1536]{0:T(1024)S(1)} %copy-done.8, f32[256]{0:T(256)S(1)} %add_rsqrt_fusion.1), kind=kOutput, calls=%fused_computation.49 | convolution fusion | flops 1209532416 | bytes 7085056 | tf_op jit(solution)/shard_map/dot_general | solution.py:112
  41.4 1.0 fusion.55
  42.4 1.6 copy.32
  44.0 1.7 copy.33
  45.7 0.7 fusion.41
  46.4 0.7 fusion.49
  47.1 1.1 multiply_cosine_fusion
  48.2 1.9 multiply_subtract_fusion
  50.1 1.5 fusion.25.bias_ref
  51.6 1.4 fusion.26.q_ref
  52.9 0.0 collective-permute-done.3
  52.9 1.0 copy.28
  54.0 0.0 collective-permute-done.2
  54.0 1.0 copy.27
  55.0 0.0 collective-permute-done.1
  55.0 1.0 copy.26
  56.0 0.0 collective-permute-done
  56.0 0.1 copy.25
  56.1 0.0 all-to-all-done
  56.1 1.8 gather_fusion.2
  57.9 14.7 %all_gather.9 = bf16[2,512,256]{2,1,0:T(8,128)(2,1)S(1)} all-gather(bf16[2,64,256]{2,1,0:T(8,128)(2,1)S(1)} %gather_fusion.2), channel_id=1, replica_groups=mesh['req'=16,'mlp'=8] {'mlp'}, dimensions={1}, use_global_device_ids=true | all-gather | bytes 589824 | tf_op jit(solution)/shard_map/all_gather | solution.py:108
  72.6 1.0 bitcast_dynamic-update-slice_fusion
  73.7 4.7 %gather_fusion.3 = bf16[1280,256]{1,0:T(8,128)(2,1)} fusion(bf16[2816,256]{1,0:T(8,128)(2,1)S(1)} %constant_dynamic-update-slice_fusion, s32[2048]{0:T(1024)S(1)} %pad_clamp_fusion), kind=kCustom, calls=%fused_computation.3 | custom fusion | bytes 1315840 | tf_op jit(solution)/shard_map/jit(_take)/gather | solution.py:140
  78.3 10.1 %shard_map.136 = bf16[12,256,128]{2,1,0:T(8,128)(2,1)} custom-call(f32[256,1280]{1,0:T(8,128)} %fusion.25.bias_ref, bf16[12,256,128]{2,1,0:T(8,128)(2,1)} %fusion.26.q_ref, bf16[1280,256]{1,0:T(8,128)(2,1)} %gather_fusion.3), custom_call_target="tpu_custom_call" | custom-call | tf_op jit(solution)/shard_map/pallas_call | solution.py:51
  88.4 1.4 copy.30
  89.8 0.0 copy-start.4
  89.8 3.8 %multiply_reduce_fusion = (f32[256]{0:T(256)S(1)}, f32[256,1536]{1,0:T(8,128)S(1)}) fusion(bf16[256,1536]{0,1:T(8,128)(2,1)S(1)} %bitcast.48, bf16[1536,1536]{1,0:T(8,128)(2,1)} %param.18, bf16[256,1536]{1,0:T(8,128)(2,1)S(1)} %copy-done.3), kind=kOutput, calls=%fused_computation.36 | convolution fusion | flops 1210318592 | bytes 7865344 | tf_op jit(solution)/shard_map/dot_general | solution.py:146
  93.7 1.1 multiply_convert_fusion
  94.8 0.0 all-gather.3.cloned.1.call-update
  94.8 0.0 reduce-scatter.2.cloned.1.call-start
  94.8 0.0 all-gather.5.cloned.1.call-done
  94.9 40.8 %all-gather.3.cloned.1.call-done = bf16[2048,1536]{1,0:T(8,128)(2,1)} async-done(((bf16[256,1536]{1,0:T(8,128)(2,1)}), bf16[2048,1536]{1,0:T(8,128)(2,1)}) %all-gather.3.cloned.1.call-update) | async-done | bytes 6291472 | tf_op jit(solution)/shard_map/all_gather | solution.py:149
  135.7 11.1 %fusion.9 = f32[2048,1152]{0,1:T(8,128)S(1)} fusion(bf16[2048,1536]{1,0:T(8,128)(2,1)} %all-gather.3.cloned.1.call-done, bf16[1536,1728]{1,0:T(8,128)(2,1)} %all-gather.5.cloned.1.call-done), kind=kOutput, calls=%fused_computation.15 | convolution fusion | flops 7247757312 | bytes 19267584 | tf_op jit(solution)/shard_map/dot_general | solution.py:150
  146.8 9.4 %convolution_convert_fusion = bf16[2048,1536]{1,0:T(8,128)(2,1)} fusion(f32[2048,1152]{0,1:T(8,128)S(1)} %fusion.9, bf16[1536,1728]{1,0:T(8,128)(2,1)} %all-gather.5.cloned.1.call-done), kind=kOutput, calls=%fused_computation.4 | convolution fusion | flops 3638820864 | bytes 17694720 | tf_op jit(solution)/shard_map/dot_general | solution.py:155
  156.2 0.0 reduce-scatter.2.cloned.1.call-update
  156.2 0.0 copy-start.1
  156.2 41.7 %reduce-scatter.2.cloned.1.call-done = bf16[256,1536]{1,0:T(8,128)(2,1)} async-done(((bf16[2048,1536]{1,0:T(8,128)(2,1)}), bf16[256,1536]{1,0:T(8,128)(2,1)}) %reduce-scatter.2.cloned.1.call-update) | async-done | bytes 786448 | tf_op jit(solution)/shard_map/reduce_scatter | solution.py:154
  198.0 2.2 %add_convert_fusion = bf16[256,1536]{1,0:T(8,128)(2,1)} fusion(f32[256,1536]{1,0:T(8,128)S(1)} %get-tuple-element.17, bf16[256,1536]{1,0:T(8,128)(2,1)} %reduce-scatter.2.cloned.1.call-done), kind=kLoop, calls=%fused_computation.34 | loop fusion | flops 1179648 | bytes 3145728 | tf_op jit(solution)/shard_map/convert_element_type | solution.py:162
  (34 shorter events, 0.3 us)
Async XLA Ops:
  6.5 8.0 %copy-start = (bf16[1536,256]{1,0:T(8,128)(2,1)S(1)}, bf16[1536,256]{1,0:T(8,128)(2,1)}, u32[]{:S(2)}) copy-start(bf16[1536,256]{1,0:T(8,128)(2,1)} %param.17) | copy-start | bytes 2359300
  6.5 7.8 %copy-start.3 = (bf16[256,1536]{1,0:T(8,128)(2,1)S(1)}, bf16[256,1536]{1,0:T(8,128)(2,1)}, u32[]{:S(2)}) copy-start(bf16[256,1536]{1,0:T(8,128)(2,1)} %param.14) | copy-start | bytes 2359300
  6.5 8.0 %copy-start.8 = (f32[1536]{0:T(1024)S(1)}, f32[1536]{0:T(1024)}, u32[]{:S(2)}) copy-start(f32[1536]{0:T(1024)} %param.15) | copy-start | bytes 18436
  6.5 88.3 %all-gather.5.cloned.1.call-start = ((), (), s32[]{:S(2)}) async-start(), calls=%async_computation.3 | async-start | bytes 5849088 | tf_op jit(solution)/shard_map/all_gather | solution.py:95
  8.6 7.3 %copy-start.7 = (s32[3,128]{1,0:T(4,128)S(1)}, s32[3,128]{1,0:T(4,128)}, u32[]{:S(2)}) copy-start(s32[3,128]{1,0:T(4,128)} %param.27) | copy-start | bytes 4612
  14.6 10.1 %copy-start.6 = (s32[16]{0:T(128)S(1)}, s32[16]{0:T(128)}, u32[]{:S(2)}) copy-start(s32[16]{0:T(128)} %param.25) | copy-start | bytes 196
  14.6 10.1 %copy-start.2 = (s32[128]{0:T(128)S(1)}, s32[128]{0:T(128)}, u32[]{:S(2)}) copy-start(s32[128]{0:T(128)} %param.26) | copy-start | bytes 1540
  18.3 7.2 %copy-start.5 = (f32[64]{0:T(128)}, f32[64]{0:T(128)S(1)}, u32[]{:S(2)}) copy-start(f32[64]{0:T(128)S(1)} %multiply_power_fusion) | copy-start | bytes 772
  18.7 34.2 %collective-permute-start.3 = (bf16[256,256]{0,1:T(8,128)(2,1)S(1)}, bf16[256,256]{0,1:T(8,128)(2,1)}, u32[]{:S(2)}, u32[]{:S(2)}) collective-permute-start(bf16[256,256]{0,1:T(8,128)(2,1)S(1)} %pad_maximum_fusion), channel_id=1, source_target_pairs={{0,1},{1,2},{2,3},{3,4},{4,5},{5,6},{6,7},{7,0},{8,9},{9,10},{10,1... | collective-permute-start | bytes 393224 | tf_op jit(solution)/shard_map/ppermute | solution.py:122
  21.3 32.6 %collective-permute-start.2 = (bf16[256,256]{0,1:T(8,128)(2,1)S(1)}, bf16[256,256]{0,1:T(8,128)(2,1)}, u32[]{:S(2)}, u32[]{:S(2)}) collective-permute-start(bf16[256,256]{0,1:T(8,128)(2,1)S(1)} %pad_maximum_fusion), channel_id=1, source_target_pairs={{0,2},{1,3},{2,4},{3,5},{4,6},{5,7},{6,0},{7,1},{8,10},{9,11},{10,... | collective-permute-start | bytes 393224 | tf_op jit(solution)/shard_map/ppermute | solution.py:122
  22.6 32.4 %collective-permute-start.1 = (bf16[256,256]{0,1:T(8,128)(2,1)S(1)}, bf16[256,256]{0,1:T(8,128)(2,1)}, u32[]{:S(2)}, u32[]{:S(2)}) collective-permute-start(bf16[256,256]{0,1:T(8,128)(2,1)S(1)} %pad_maximum_fusion), channel_id=1, source_target_pairs={{0,3},{1,4},{2,5},{3,6},{4,7},{5,0},{6,1},{7,2},{8,11},{9,12},{10,... | collective-permute-start | bytes 393224 | tf_op jit(solution)/shard_map/ppermute | solution.py:122
  24.1 31.9 %collective-permute-start = (bf16[256,256]{0,1:T(8,128)(2,1)S(1)}, bf16[256,256]{0,1:T(8,128)(2,1)S(1)}, u32[]{:S(2)}, u32[]{:S(2)}) collective-permute-start(bf16[256,256]{0,1:T(8,128)(2,1)S(1)} %pad_maximum_fusion), channel_id=1, source_target_pairs={{0,4},{1,5},{2,6},{3,7},{4,0},{5,1},{6,2},{7,3},{8,12},{9,13},{10,... | collective-permute-start | bytes 393224 | tf_op jit(solution)/shard_map/ppermute | solution.py:122
  28.3 27.8 %all-to-all-start = ((bf16[16,2,64,256]{3,2,1,0:T(8,128)(2,1)}), bf16[16,2,64,256]{3,2,1,0:T(8,128)(2,1)}, u32[]{:S(2)}, u32[]{:S(2)}) async-start(bf16[16,2,64,256]{3,2,1,0:T(8,128)(2,1)} %bitcast.9), calls=%async_computation | async-start | bytes 2097152 | tf_op jit(solution)/shard_map/all_to_all | solution.py:105
  36.1 99.6 %all-gather.3.cloned.1.call-start = ((), (), s32[]{:S(2)}) async-start(), calls=%async_computation.2 | async-start | bytes 7077888 | tf_op jit(solution)/shard_map/all_gather | solution.py:149
  89.8 3.9 %copy-start.4 = (f32[1536]{0:T(1024)S(1)}, f32[1536]{0:T(1024)}, u32[]{:S(2)}) copy-start(f32[1536]{0:T(1024)} %param.19) | copy-start | bytes 18436
  94.8 103.2 %reduce-scatter.2.cloned.1.call-start = ((), (), s32[]{:S(2)}) async-start(), calls=%async_computation.4 | async-start | bytes 7077888 | tf_op jit(solution)/shard_map/reduce_scatter | solution.py:154
  156.2 44.0 %copy-start.1 = (bf16[1536,256]{1,0:T(8,128)(2,1)S(1)}, bf16[1536,256]{1,0:T(8,128)(2,1)}, u32[]{:S(2)}) copy-start(bf16[1536,256]{1,0:T(8,128)(2,1)} %param.17) | copy-start | bytes 2359300
Sparse Core Ops, SparseCore 0:
  9.5 65.5 all-gather.4
  94.9 40.7 all-gather.2
  156.3 41.5 reduce-scatter.1

commit v9 on v8

--- a/solution.py
+++ b/solution.py
@@ -22,43 +22,53 @@
     half_dim = values.shape[-1] // 2
     freqs = 10000.0 ** (-jnp.arange(half_dim, dtype=jnp.float32) / half_dim)
     angles = where_at.astype(jnp.float32)[:, None] * freqs[None, :]
-    cosine = jnp.cos(angles)[:, None, :]
-    sine = jnp.sin(angles)[:, None, :]
-    first = values[..., :half_dim]
-    second = values[..., half_dim:]
-    return jnp.concatenate([first * cosine - second * sine, first * sine + second * cosine], -1)
+    cosine = jnp.cos(angles)
+    sine = jnp.sin(angles)
+    cos_both = jnp.concatenate([cosine, cosine], -1)[:, None, :]
+    sin_signed = jnp.concatenate([-sine, sine], -1)[:, None, :]
+    swapped = jnp.concatenate([values[..., half_dim:], values[..., :half_dim]], -1)
+    return values * cos_both + swapped * sin_signed
 
 
-def _attend_kernel(bias_ref, q_ref, kv_ref, o_ref):
+def _attend_kernel(where_ref, q_ref, kv_ref, o_ref):
     keys = kv_ref[:, :HD]
     vals = kv_ref[:, HD:]
-    bias = bias_ref[...]
-    for head in range(q_ref.shape[0]):
+    shape = (q_ref.shape[0], kv_ref.shape[0])
+    query_at = where_ref[0] + lax.broadcasted_iota(jnp.int32, shape, 0)
+    key_at = where_ref[1] + lax.broadcasted_iota(jnp.int32, shape, 1)
+    spacing = query_at - key_at
+    allowed = (key_at >= 0) & (spacing >= 0) & (spacing < WINDOW)
+    bias = jnp.where(allowed, 0.0, -jnp.inf).astype(jnp.float32)
+    for head in range(q_ref.shape[1] // HD):
+        cols = pl.ds(head * HD, HD)
         scores = lax.dot_general(
-            q_ref[head], keys, (((1,), (1,)), ((), ())), preferred_element_type=jnp.float32
+            q_ref[:, cols], keys, (((1,), (1,)), ((), ())), preferred_element_type=jnp.float32
         )
         scores = scores + bias
         top = jnp.max(scores, axis=1, keepdims=True)
         weights = jnp.exp(scores - top)
         denom = jnp.sum(weights, axis=1, keepdims=True)
         mixed = jnp.dot(weights.astype(jnp.bfloat16), vals, preferred_element_type=jnp.float32)
-        o_ref[head] = (mixed / denom).astype(o_ref.dtype)
+        o_ref[:, cols] = (mixed / denom).astype(o_ref.dtype)
 
 
-def attend_window(queries_hm, window, bias, heads_per_step=4):
-    heads, rows, _ = queries_hm.shape
+def attend_window(queries, window, where, heads_per_step=4):
+    rows, width = queries.shape
     span = window.shape[0]
+    step_cols = heads_per_step * HD
     return pl.pallas_call(
         _attend_kernel,
-        grid=(heads // heads_per_step,),
-        in_specs=[
-            pl.BlockSpec((rows, span), lambda h: (0, 0)),
-            pl.BlockSpec((heads_per_step, rows, HD), lambda h: (h, 0, 0)),
-            pl.BlockSpec((span, 2 * HD), lambda h: (0, 0)),
-        ],
-        out_specs=pl.BlockSpec((heads_per_step, rows, HD), lambda h: (h, 0, 0)),
-        out_shape=jax.ShapeDtypeStruct((heads, rows, HD), jnp.bfloat16),
-    )(bias, queries_hm, window)
+        grid_spec=pltpu.PrefetchScalarGridSpec(
+            num_scalar_prefetch=1,
+            grid=(width // step_cols,),
+            in_specs=[
+                pl.BlockSpec((rows, step_cols), lambda h, w: (0, h)),
+                pl.BlockSpec((span, 2 * HD), lambda h, w: (0, 0)),
+            ],
+            out_specs=pl.BlockSpec((rows, step_cols), lambda h, w: (0, h)),
+        ),
+        out_shape=jax.ShapeDtypeStruct((rows, width), jnp.bfloat16),
+    )(where, queries, window)
 
 
 def body(
@@ -138,11 +148,8 @@
         ),
     )
     window = jnp.take(sources, source_row, axis=0, mode="clip")
-    spacing = query_at[:, None] - key_at[None, :]
-    allowed = (key_at[None, :] >= 0) & (spacing >= 0) & (spacing < WINDOW)
-    bias = jnp.where(allowed, 0.0, -jnp.inf).astype(jnp.float32)
-    heads_first = attend_window(jnp.transpose(queries, (1, 0, 2)), window, bias)
-    context = jnp.transpose(heads_first, (1, 0, 2)).reshape(tok_rows, HEADS * HD)
+    where = jnp.stack([total + position_group * tok_rows, first]).astype(jnp.int32)
+    context = attend_window(queries.reshape(tok_rows, HEADS * HD), window, where)
     attn_out = jnp.dot(context, w_out, preferred_element_type=jnp.float32)
     resid = (tokens.astype(jnp.float32) + attn_out).astype(jnp.bfloat16)
     ffn_in = rms_scale(resid, ffn_gain).astype(jnp.bfloat16)

time: 208 us -> 204 us (0.981)
  other arithmetic: 11.1 us -> 8.74 us
  local copies, waits for them, and re-layouts: 25.8 us -> 23.6 us
    unnamed x27 -> x29, local copies, waits for them, and re-layouts: 4.35 us -> 0.15 us
    convert_element_type x0 -> x2, other arithmetic: none -> 3.47 us  [the longest x1 3.46 us: body(): queries = (rotate(query_full, query_at) * HD ** (-0.5)).astype(jnp.bfloat16)]
    mul x0 -> x3, local copies, waits for them, and re-layouts: none -> 3.39 us  [rotate(): return values * cos_both + swapped * sin_signed]
  transfers between devices with their start and end apart: 8 -> 8, of which waited for: 2 -> 2; matrix products, arithmetic and copies ran while one was open for 20% -> 18% of each run, Pallas kernels for 5% -> 5%
where the time goes in v9:
time: 204 us
  waiting for transfers between devices  81.6 us (40%)
  matrix products  29.1 us (14%)
  local copies, waits for them, and re-layouts  23.6 us (12%)
  between operations  19.3 us (9%)
  blocking collectives  16.4 us (8%)
  starting transfers between devices  14.2 us (7%)
  Pallas kernels  10.7 us (5%)
  other arithmetic  8.74 us (4%)
    reduce_scatter x1, waiting for transfers between devices, body(): lax.psum_scatter(lax.dot_general(hidden, down_full, (((1,), (1,)), ((), (...  41.6 us
    all_gather x1, waiting for transfers between devices, body(): all_rows = lax.all_gather(ffn_in, 'mlp', axis=0, tiled=True)  39.9 us
    all_gather x1, blocking collectives, body(): levels = lax.all_gather(my_part, 'mlp', axis=1, tiled=True)  16.4 us
    dot_general x1, matrix products, body(): jnp.dot(all_rows, packed[:, :2 * ff_cols], preferred_element_type=jnp.flo...  11.1 us
    pallas_call x1, Pallas kernels, attend_window(): pl.pallas_call(_attend_kernel, grid_spec=pltpu.PrefetchScalarGridSpec(num...  10.7 us
    dot_general x1, matrix products, body(): lax.dot_general(hidden, down_full, (((1,), (1,)), ((), ())), preferred_el...  9.58 us
    all_to_all x1, starting transfers between devices, body(): lax.all_to_all(outgoing, 'req', split_axis=0, concat_axis=0, tiled=True)  7.96 us
    ppermute x4, starting transfers between devices, body(): lax.ppermute(new_keyval, 'mlp', [(i, (i + shift) % n_mlp) for i in range(...  5.94 us
  transfers between devices with their start and end apart: 8, of which 2 were waited for; matrix products, arithmetic and copies ran while one was open for 18% of the time, Pallas kernels for 5%

profile of v9, /device:TPU:1, one launch (start us, length us, event | category | flops | bytes accessed | tf_op | source)
XLA Modules:
  0.0 203.6 jit_solution(16137533958926137430)
XLA Ops:
  6.5 0.0 copy-start
  6.5 0.0 all-gather.5.cloned.1.call-start
  6.5 2.0 concatenate.63
  8.5 0.0 all-gather.5.cloned.1.call-update
  8.6 0.0 copy-start.9
  8.6 1.2 dynamic_slice.21
  11.8 1.2 dynamic_slice.22
  14.3 0.0 copy-done.3
  14.3 0.2 fusion.19
  14.6 0.0 copy-done
  14.6 0.0 copy-done.10
  14.6 0.0 copy-start.8
  14.6 0.0 copy-start.2
  14.6 0.6 fusion.24
  15.9 0.7 constant_dynamic-slice_fusion.2
  18.5 0.3 multiply_cosine_fusion
  18.9 2.6 %collective-permute-start.3 = (bf16[256,256]{0,1:T(8,128)(2,1)S(1)}, bf16[256,256]{0,1:T(8,128)(2,1)}, u32[]{:S(2)}, u32[]{:S(2)}) collective-permute-start(bf16[256,256]{0,1:T(8,128)(2,1)S(1)} %pad_maximum_fusion.2), channel_id=1, source_target_pairs={{0,1},{1,2},{2,3},{3,4},{4,5},{5,6},{6,7},{7,0},{8,9},{9,10},{10,1... | collective-permute-start | bytes 393224 | tf_op jit(solution)/shard_map/ppermute | solution.py:132
  21.5 1.2 collective-permute-start.2
  22.7 1.6 collective-permute-start.1
  24.3 0.5 collective-permute-start
  24.9 0.7 gather_fusion
  25.6 0.1 copy.26
  25.7 0.1 reshape.297
  25.7 1.1 constant_dynamic-slice_fusion
  26.8 1.6 gather_fusion.1
  28.4 8.0 %all-to-all-start = ((bf16[16,2,64,256]{3,2,1,0:T(8,128)(2,1)}), bf16[16,2,64,256]{3,2,1,0:T(8,128)(2,1)}, u32[]{:S(2)}, u32[]{:S(2)}) async-start(bf16[16,2,64,256]{3,2,1,0:T(8,128)(2,1)} %bitcast.12), calls=%async_computation | async-start | bytes 2097152 | tf_op jit(solution)/shard_map/all_to_all | solution.py:115
  36.4 0.0 all-gather.3.cloned.1.call-start
  36.5 0.2 dynamic-slice_reduce_fusion
  36.7 3.8 %fusion.26 = f32[256,1536]{1,0:T(8,128)S(1)} fusion(bf16[1536,1536]{1,0:T(8,128)(2,1)} %param.16, bf16[256,1536]{1,0:T(8,128)(2,1)S(1)} %copy-done.4, f32[1536]{0:T(1024)S(1)} %copy-done.10, f32[256]{0:T(256)S(1)} %add_rsqrt_fusion.1), kind=kOutput, calls=%fused_computation.41 | convolution fusion | flops 1209532416 | bytes 7085056 | tf_op jit(solution)/shard_map/dot_general | solution.py:122
  40.4 0.5 copy.24
  40.9 0.1 fusion.44
  41.0 0.1 maximum_multiply_fusion
  41.1 1.6 copy.25
  42.8 0.1 mul.137
  42.9 1.6 copy.23
  44.6 3.5 %multiply_convert_fusion.1.q_ref = bf16[256,1536]{1,0:T(8,128)(2,1)} fusion(f32[256,1536]{1,0:T(8,128)} %copy.25, f32[256,1536]{1,0:T(8,128)S(1)} %fusion.26, f32[256,1536]{1,0:T(8,128)} %copy.23), kind=kLoop, calls=%fused_computation.34 | loop fusion | flops 1572864 | bytes 5505024 | tf_op jit(solution)/shard_map/convert_element_type | solution.py:125
  48.0 0.6 pad_add_fusion.1.where_ref
  48.6 0.1 copy.31
  48.7 0.6 fusion.31
  49.3 0.0 collective-permute-done.3
  49.4 1.0 copy.30
  50.4 0.0 collective-permute-done.2
  50.4 1.0 copy.29
  51.4 0.0 collective-permute-done.1
  51.4 1.0 copy.28
  52.4 0.0 collective-permute-done
  52.4 1.0 copy.27
  53.4 0.0 all-to-all-done
  53.4 1.8 gather_fusion.2
  55.3 16.4 %all_gather.9 = bf16[2,512,256]{2,1,0:T(8,128)(2,1)S(1)} all-gather(bf16[2,64,256]{2,1,0:T(8,128)(2,1)S(1)} %gather_fusion.2), channel_id=1, replica_groups=mesh['req'=16,'mlp'=8] {'mlp'}, dimensions={1}, use_global_device_ids=true | all-gather | bytes 589824 | tf_op jit(solution)/shard_map/all_gather | solution.py:118
  71.9 4.7 %gather_fusion.3 = bf16[1280,256]{1,0:T(8,128)(2,1)} fusion(bf16[2816,256]{1,0:T(8,128)(2,1)S(1)} %constant_dynamic-update-slice_fusion, s32[2048]{0:T(1024)S(1)} %pad_clamp_fusion), kind=kCustom, calls=%fused_computation.3 | custom fusion | bytes 1315840 | tf_op jit(solution)/shard_map/jit(_take)/gather | solution.py:150
  76.6 10.7 %shard_map.136 = bf16[256,1536]{1,0:T(8,128)(2,1)} custom-call(s32[2]{0:T(128)} %pad_add_fusion.1.where_ref, bf16[256,1536]{1,0:T(8,128)(2,1)} %multiply_convert_fusion.1.q_ref, bf16[1280,256]{1,0:T(8,128)(2,1)} %gather_fusion.3), custom_call_target="tpu_custom_call" | custom-call | tf_op jit(solution)/shard_map/pallas_call | solution.py:59
  87.2 4.1 %multiply_reduce_fusion = (f32[256]{0:T(256)S(1)}, f32[256,1536]{1,0:T(8,128)S(1)}) fusion(bf16[256,1536]{1,0:T(8,128)(2,1)} %shard_map.136, bf16[1536,1536]{1,0:T(8,128)(2,1)} %param.18, bf16[256,1536]{1,0:T(8,128)(2,1)S(1)} %copy-done.5), kind=kOutput, calls=%fused_computation.33 | convolution fusion | flops 1210318592 | bytes 7865344 | tf_op jit(solution)/shard_map/dot_general | solution.py:153
  91.3 1.1 multiply_convert_fusion
  92.4 0.0 all-gather.3.cloned.1.call-update
  92.4 0.2 reduce-scatter.2.cloned.1.call-start
  92.7 0.0 all-gather.5.cloned.1.call-done
  92.7 39.9 %all-gather.3.cloned.1.call-done = bf16[2048,1536]{1,0:T(8,128)(2,1)} async-done(((bf16[256,1536]{1,0:T(8,128)(2,1)}), bf16[2048,1536]{1,0:T(8,128)(2,1)}) %all-gather.3.cloned.1.call-update) | async-done | bytes 6291472 | tf_op jit(solution)/shard_map/all_gather | solution.py:156
  132.6 11.1 %fusion.9 = f32[2048,1152]{0,1:T(8,128)S(1)} fusion(bf16[2048,1536]{1,0:T(8,128)(2,1)} %all-gather.3.cloned.1.call-done, bf16[1536,1728]{1,0:T(8,128)(2,1)} %all-gather.5.cloned.1.call-done), kind=kOutput, calls=%fused_computation.15 | convolution fusion | flops 7247757312 | bytes 19267584 | tf_op jit(solution)/shard_map/dot_general | solution.py:157
  143.7 9.6 %convolution_convert_fusion = bf16[2048,1536]{1,0:T(8,128)(2,1)} fusion(f32[2048,1152]{0,1:T(8,128)S(1)} %fusion.9, bf16[1536,1728]{1,0:T(8,128)(2,1)} %all-gather.5.cloned.1.call-done), kind=kOutput, calls=%fused_computation.4 | convolution fusion | flops 3638820864 | bytes 17694720 | tf_op jit(solution)/shard_map/dot_general | solution.py:162
  153.3 0.0 reduce-scatter.2.cloned.1.call-update
  153.3 0.0 copy-start.1
  153.4 41.6 %reduce-scatter.2.cloned.1.call-done = bf16[256,1536]{1,0:T(8,128)(2,1)} async-done(((bf16[2048,1536]{1,0:T(8,128)(2,1)}), bf16[256,1536]{1,0:T(8,128)(2,1)}) %reduce-scatter.2.cloned.1.call-update) | async-done | bytes 786448 | tf_op jit(solution)/shard_map/reduce_scatter | solution.py:161
  194.9 2.2 %add_convert_fusion = bf16[256,1536]{1,0:T(8,128)(2,1)} fusion(f32[256,1536]{1,0:T(8,128)S(1)} %get-tuple-element.19, bf16[256,1536]{1,0:T(8,128)(2,1)} %reduce-scatter.2.cloned.1.call-done), kind=kLoop, calls=%fused_computation.31 | loop fusion | flops 1179648 | bytes 3145728 | tf_op jit(solution)/shard_map/convert_element_type | solution.py:169
  (37 shorter events, 0.3 us)
Async XLA Ops:
  6.5 8.0 %copy-start = (bf16[1536,256]{1,0:T(8,128)(2,1)S(1)}, bf16[1536,256]{1,0:T(8,128)(2,1)}, u32[]{:S(2)}) copy-start(bf16[1536,256]{1,0:T(8,128)(2,1)} %param.17) | copy-start | bytes 2359300
  6.5 7.8 %copy-start.3 = (bf16[256,1536]{1,0:T(8,128)(2,1)S(1)}, bf16[256,1536]{1,0:T(8,128)(2,1)}, u32[]{:S(2)}) copy-start(bf16[256,1536]{1,0:T(8,128)(2,1)} %param.14) | copy-start | bytes 2359300
  6.5 8.0 %copy-start.10 = (f32[1536]{0:T(1024)S(1)}, f32[1536]{0:T(1024)}, u32[]{:S(2)}) copy-start(f32[1536]{0:T(1024)} %param.15) | copy-start | bytes 18436
  6.5 86.1 %all-gather.5.cloned.1.call-start = ((), (), s32[]{:S(2)}) async-start(), calls=%async_computation.3 | async-start | bytes 5849088 | tf_op jit(solution)/shard_map/all_gather | solution.py:105
  8.6 7.3 %copy-start.9 = (s32[3,128]{1,0:T(4,128)S(1)}, s32[3,128]{1,0:T(4,128)}, u32[]{:S(2)}) copy-start(s32[3,128]{1,0:T(4,128)} %param.27) | copy-start | bytes 4612
  14.6 10.3 %copy-start.8 = (s32[16]{0:T(128)S(1)}, s32[16]{0:T(128)}, u32[]{:S(2)}) copy-start(s32[16]{0:T(128)} %param.25) | copy-start | bytes 196
  14.6 10.3 %copy-start.2 = (s32[128]{0:T(128)S(1)}, s32[128]{0:T(128)}, u32[]{:S(2)}) copy-start(s32[128]{0:T(128)} %param.26) | copy-start | bytes 1540
  18.9 30.4 %collective-permute-start.3 = (bf16[256,256]{0,1:T(8,128)(2,1)S(1)}, bf16[256,256]{0,1:T(8,128)(2,1)}, u32[]{:S(2)}, u32[]{:S(2)}) collective-permute-start(bf16[256,256]{0,1:T(8,128)(2,1)S(1)} %pad_maximum_fusion.2), channel_id=1, source_target_pairs={{0,1},{1,2},{2,3},{3,4},{4,5},{5,6},{6,7},{7,0},{8,9},{9,10},{10,1... | collective-permute-start | bytes 393224 | tf_op jit(solution)/shard_map/ppermute | solution.py:132
  21.5 28.8 %collective-permute-start.2 = (bf16[256,256]{0,1:T(8,128)(2,1)S(1)}, bf16[256,256]{0,1:T(8,128)(2,1)}, u32[]{:S(2)}, u32[]{:S(2)}) collective-permute-start(bf16[256,256]{0,1:T(8,128)(2,1)S(1)} %pad_maximum_fusion.2), channel_id=1, source_target_pairs={{0,2},{1,3},{2,4},{3,5},{4,6},{5,7},{6,0},{7,1},{8,10},{9,11},{10,... | collective-permute-start | bytes 393224 | tf_op jit(solution)/shard_map/ppermute | solution.py:132
  22.7 28.7 %collective-permute-start.1 = (bf16[256,256]{0,1:T(8,128)(2,1)S(1)}, bf16[256,256]{0,1:T(8,128)(2,1)}, u32[]{:S(2)}, u32[]{:S(2)}) collective-permute-start(bf16[256,256]{0,1:T(8,128)(2,1)S(1)} %pad_maximum_fusion.2), channel_id=1, source_target_pairs={{0,3},{1,4},{2,5},{3,6},{4,7},{5,0},{6,1},{7,2},{8,11},{9,12},{10,... | collective-permute-start | bytes 393224 | tf_op jit(solution)/shard_map/ppermute | solution.py:132
  24.3 28.1 %collective-permute-start = (bf16[256,256]{0,1:T(8,128)(2,1)S(1)}, bf16[256,256]{0,1:T(8,128)(2,1)}, u32[]{:S(2)}, u32[]{:S(2)}) collective-permute-start(bf16[256,256]{0,1:T(8,128)(2,1)S(1)} %pad_maximum_fusion.2), channel_id=1, source_target_pairs={{0,4},{1,5},{2,6},{3,7},{4,0},{5,1},{6,2},{7,3},{8,12},{9,13},{10,... | collective-permute-start | bytes 393224 | tf_op jit(solution)/shard_map/ppermute | solution.py:132
  28.4 8.2 %copy-start.4 = (bf16[256,1536]{1,0:T(8,128)(2,1)S(1)}, bf16[256,1536]{1,0:T(8,128)(2,1)}, u32[]{:S(2)}) copy-start(bf16[256,1536]{1,0:T(8,128)(2,1)} %param.14) | copy-start | bytes 2359300
  28.4 25.0 %all-to-all-start = ((bf16[16,2,64,256]{3,2,1,0:T(8,128)(2,1)}), bf16[16,2,64,256]{3,2,1,0:T(8,128)(2,1)}, u32[]{:S(2)}, u32[]{:S(2)}) async-start(bf16[16,2,64,256]{3,2,1,0:T(8,128)(2,1)} %bitcast.12), calls=%async_computation | async-start | bytes 2097152 | tf_op jit(solution)/shard_map/all_to_all | solution.py:115
  36.4 96.2 %all-gather.3.cloned.1.call-start = ((), (), s32[]{:S(2)}) async-start(), calls=%async_computation.2 | async-start | bytes 7077888 | tf_op jit(solution)/shard_map/all_gather | solution.py:156
  48.0 23.7 %copy-start.6 = (bf16[1,512,256]{2,1,0:T(8,128)(2,1)S(1)}, bf16[1,512,256]{2,1,0:T(8,128)(2,1)}, u32[]{:S(2)}) copy-start(bf16[1,512,256]{2,1,0:T(8,128)(2,1)} %param.24) | copy-start | bytes 786436
  76.6 10.7 %copy-start.5 = (bf16[256,1536]{1,0:T(8,128)(2,1)S(1)}, bf16[256,1536]{1,0:T(8,128)(2,1)}, u32[]{:S(2)}) copy-start(bf16[256,1536]{1,0:T(8,128)(2,1)} %param.14) | copy-start | bytes 2359300
  87.2 4.1 %copy-start.7 = (f32[1536]{0:T(1024)S(1)}, f32[1536]{0:T(1024)}, u32[]{:S(2)}) copy-start(f32[1536]{0:T(1024)} %param.19) | copy-start | bytes 18436
  92.4 102.5 %reduce-scatter.2.cloned.1.call-start = ((), (), s32[]{:S(2)}) async-start(), calls=%async_computation.4 | async-start | bytes 7077888 | tf_op jit(solution)/shard_map/reduce_scatter | solution.py:161
  153.3 43.8 %copy-start.1 = (bf16[1536,256]{1,0:T(8,128)(2,1)S(1)}, bf16[1536,256]{1,0:T(8,128)(2,1)}, u32[]{:S(2)}) copy-start(bf16[1536,256]{1,0:T(8,128)(2,1)} %param.17) | copy-start | bytes 2359300
Sparse Core Ops, SparseCore 0:
  9.5 65.8 all-gather.4
  92.6 40.0 all-gather.2
  153.5 41.3 reduce-scatter.1

commit v10 on v9

--- a/solution.py
+++ b/solution.py
@@ -69,6 +69,32 @@
         ),
         out_shape=jax.ShapeDtypeStruct((rows, width), jnp.bfloat16),
     )(where, queries, window)
+
+
+def _ffn_kernel(x_ref, w_ref, o_ref):
+    rows = x_ref[...]
+    width = w_ref.shape[1] // 3
+    gate = jnp.dot(rows, w_ref[:, :width], preferred_element_type=jnp.float32)
+    upward = jnp.dot(rows, w_ref[:, width : 2 * width], preferred_element_type=jnp.float32)
+    hidden = (jax.nn.gelu(gate, approximate=True) * upward).astype(jnp.bfloat16)
+    partial_down = lax.dot_general(
+        hidden, w_ref[:, 2 * width :], (((1,), (1,)), ((), ())), preferred_element_type=jnp.float32
+    )
+    o_ref[...] = partial_down.astype(o_ref.dtype)
+
+
+def ffn_block(all_rows, packed, block_rows=512):
+    rows, model = all_rows.shape
+    return pl.pallas_call(
+        _ffn_kernel,
+        grid=(rows // block_rows,),
+        in_specs=[
+            pl.BlockSpec((block_rows, model), lambda i: (i, 0)),
+            pl.BlockSpec(packed.shape, lambda i: (0, 0)),
+        ],
+        out_specs=pl.BlockSpec((block_rows, model), lambda i: (i, 0)),
+        out_shape=jax.ShapeDtypeStruct((rows, model), jnp.bfloat16),
+    )(all_rows, packed)
 
 
 def body(
@@ -102,10 +128,9 @@
     total = len_zero + len_one + len_two
 
     ff_cols = w_gate.shape[1]
-    packed = lax.all_gather(
-        jnp.concatenate([w_gate, w_up, w_down], 1), "req", axis=0, tiled=True
-    )
-    down_full = packed[:, 2 * ff_cols :]
+    lanes = -(-ff_cols // 128) * 128
+    padded = [jnp.pad(part, ((0, 0), (0, lanes - ff_cols))) for part in (w_gate, w_up, w_down)]
+    packed = lax.all_gather(jnp.concatenate(padded, 1), "req", axis=0, tiled=True)
 
     level_zero = node_parent[leaf_parent]
     wanted = jnp.stack([level_zero, leaf_parent], 1)
@@ -154,17 +179,9 @@
     resid = (tokens.astype(jnp.float32) + attn_out).astype(jnp.bfloat16)
     ffn_in = rms_scale(resid, ffn_gain).astype(jnp.bfloat16)
     all_rows = lax.all_gather(ffn_in, "mlp", axis=0, tiled=True)
-    gate_up = jnp.dot(all_rows, packed[:, : 2 * ff_cols], preferred_element_type=jnp.float32)
-    gate = gate_up[:, :ff_cols]
-    upward = gate_up[:, ff_cols:]
-    hidden = (jax.nn.gelu(gate, approximate=True) * upward).astype(jnp.bfloat16)
+    partial_down = ffn_block(all_rows, packed)
     summed = lax.psum_scatter(
-        lax.dot_general(
-            hidden, down_full, (((1,), (1,)), ((), ())), preferred_element_type=jnp.float32
-        ).astype(jnp.bfloat16),
-        "mlp",
-        scatter_dimension=0,
-        tiled=True,
+        partial_down, "mlp", scatter_dimension=0, tiled=True
     ).astype(jnp.float32)
     return (resid.astype(jnp.float32) + summed).astype(jnp.bfloat16)
 

time: 204 us -> 206 us (level)
  Pallas kernels: 10.7 us -> 30.3 us
  matrix products: 29.1 us -> 9.58 us
  other arithmetic: 8.74 us -> 11.7 us
    dot_general x2 -> x0, matrix products: 20.7 us -> none  [the longest x1 11.1 us: body(): jnp.dot(all_rows, packed[:, :2 * ff_cols], preferred_element_type=jnp.flo...]
    pallas_call x0 -> x1, Pallas kernels: none -> 19.7 us  [ffn_block(): pl.pallas_call(_ffn_kernel, grid=(rows // block_rows,), in_specs=[pl.Bloc...]
  transfers between devices with their start and end apart: 8 -> 8, of which waited for: 2 -> 2; matrix products, arithmetic and copies ran while one was open for 18% -> 19% of each run, Pallas kernels for 5% -> 5%
where the time goes in v10:
time: 206 us; the launch traced here: 205 us
  waiting for transfers between devices  82.6 us (40%)
  Pallas kernels  30.3 us (15%)
  local copies, waits for them, and re-layouts  23.4 us (11%)
  between operations  19.3 us (9%)
  blocking collectives  14.5 us (7%)
  starting transfers between devices  14 us (7%)
  other arithmetic  11.7 us (6%)
  matrix products  9.58 us (5%)
    reduce_scatter x1, waiting for transfers between devices, body(): lax.psum_scatter(partial_down, 'mlp', scatter_dimension=0, tiled=True)  41.7 us
    all_gather x1, waiting for transfers between devices, body(): all_rows = lax.all_gather(ffn_in, 'mlp', axis=0, tiled=True)  40.8 us
    pallas_call x1, Pallas kernels, ffn_block(): pl.pallas_call(_ffn_kernel, grid=(rows // block_rows,), in_specs=[pl.Bloc...  19.7 us
    all_gather x1, blocking collectives, body(): levels = lax.all_gather(my_part, 'mlp', axis=1, tiled=True)  14.5 us
    pallas_call x1, Pallas kernels, attend_window(): pl.pallas_call(_attend_kernel, grid_spec=pltpu.PrefetchScalarGridSpec(num...  10.7 us
    all_to_all x1, starting transfers between devices, body(): lax.all_to_all(outgoing, 'req', split_axis=0, concat_axis=0, tiled=True)  7.77 us
    ppermute x4, starting transfers between devices, body(): lax.ppermute(new_keyval, 'mlp', [(i, (i + shift) % n_mlp) for i in range(...  5.94 us
    dot_general x1, matrix products, body(): jnp.dot(normed, w_query, preferred_element_type=jnp.float32)  4.95 us
  transfers between devices with their start and end apart: 8, of which 2 were waited for; matrix products, arithmetic and copies ran while one was open for 19% of the time, Pallas kernels for 5%

profile of v10, /device:TPU:1, one launch (start us, length us, event | category | flops | bytes accessed | tf_op | source)
XLA Modules:
  0.0 205.4 jit_solution(6172052956771683427)
XLA Ops:
  6.5 0.0 copy-start
  6.5 0.0 all-gather.5.cloned.1.call-start
  6.5 1.9 fusion.10
  8.5 0.0 all-gather.5.cloned.1.call-update
  8.5 0.0 copy-start.8
  8.5 1.2 dynamic_slice.21
  11.7 1.2 dynamic_slice.22
  14.2 0.0 copy-done.2
  14.3 0.2 fusion.2
  14.5 0.0 copy-done
  14.5 0.0 copy-start.7
  14.5 0.0 copy-start.1
  14.5 0.6 fusion.13
  15.8 0.6 constant_dynamic-slice_fusion.2
  18.4 0.3 multiply_cosine_fusion
  18.7 0.7 fusion.18
  19.4 2.6 %collective-permute-start.3 = (bf16[256,256]{0,1:T(8,128)(2,1)S(1)}, bf16[256,256]{0,1:T(8,128)(2,1)}, u32[]{:S(2)}, u32[]{:S(2)}) collective-permute-start(bf16[256,256]{0,1:T(8,128)(2,1)S(1)} %pad_maximum_fusion.2), channel_id=1, source_target_pairs={{0,1},{1,2},{2,3},{3,4},{4,5},{5,6},{6,7},{7,0},{8,9},{9,10},{10,1... | collective-permute-start | bytes 393224 | tf_op jit(solution)/shard_map/ppermute | solution.py:157
  22.0 1.2 collective-permute-start.2
  23.3 1.6 collective-permute-start.1
  24.9 0.5 collective-permute-start
  25.4 0.7 gather_fusion
  26.1 0.1 copy.26
  26.2 0.1 reshape.297
  26.3 1.1 constant_dynamic-slice_fusion
  27.4 1.6 gather_fusion.1
  29.0 7.8 %all-to-all-start = ((bf16[16,2,64,256]{3,2,1,0:T(8,128)(2,1)}), bf16[16,2,64,256]{3,2,1,0:T(8,128)(2,1)S(1)}, u32[]{:S(2)}, u32[]{:S(2)}) async-start(bf16[16,2,64,256]{3,2,1,0:T(8,128)(2,1)} %bitcast.12), calls=%async_computation | async-start | bytes 2097152 | tf_op jit(solution)/shard_map/all_to_all | solution.py:140
  36.8 0.0 all-gather.3.cloned.1.call-start
  36.8 0.2 dynamic-slice_reduce_fusion
  37.0 5.0 %fusion.15 = f32[256,1536]{1,0:T(8,128)} fusion(bf16[1536,1536]{1,0:T(8,128)(2,1)} %param.16, bf16[256,1536]{1,0:T(8,128)(2,1)S(1)} %copy-done.2, f32[1536]{0:T(1024)S(1)} %copy-done.9, f32[256]{0:T(256)S(1)} %add_rsqrt_fusion.1), kind=kOutput, calls=%fused_computation.33 | convolution fusion | flops 1209532416 | bytes 7085056 | tf_op jit(solution)/shard_map/dot_general | solution.py:147
  42.0 1.9 copy.24
  43.8 0.0 copy-start.4
  43.9 0.1 fusion.29
  44.0 0.8 copy-done.4
  44.8 0.1 maximum_multiply_fusion
  44.9 1.6 copy.25
  46.5 1.0 mul.113
  47.5 1.6 copy.23
  49.2 3.7 %multiply_convert_fusion.1.q_ref = bf16[256,1536]{1,0:T(8,128)(2,1)} fusion(f32[256,1536]{1,0:T(8,128)} %copy.25, f32[256,1536]{1,0:T(8,128)} %fusion.15, f32[256,1536]{1,0:T(8,128)} %copy.23), kind=kLoop, calls=%fused_computation.16 | loop fusion | flops 1572864 | bytes 5505024 | tf_op jit(solution)/shard_map/convert_element_type | solution.py:150
  52.9 0.7 pad_add_fusion.1.where_ref
  53.6 0.1 copy.31
  53.7 0.7 fusion.20
  54.4 0.0 collective-permute-done.3
  54.4 1.0 copy.30
  55.4 0.0 collective-permute-done.2
  55.4 1.0 copy.29
  56.4 0.0 collective-permute-done.1
  56.4 1.0 copy.28
  57.4 0.0 collective-permute-done
  57.4 1.0 copy.27
  58.4 0.0 all-to-all-done
  58.5 0.6 gather_fusion.2
  59.0 14.5 %all_gather.9 = bf16[2,512,256]{2,1,0:T(8,128)(2,1)S(1)} all-gather(bf16[2,64,256]{2,1,0:T(8,128)(2,1)S(1)} %gather_fusion.2), channel_id=1, replica_groups=mesh['req'=16,'mlp'=8] {'mlp'}, dimensions={1}, use_global_device_ids=true | all-gather | bytes 589824 | tf_op jit(solution)/shard_map/all_gather | solution.py:143
  73.7 4.7 %gather_fusion.3 = bf16[1280,256]{1,0:T(8,128)(2,1)} fusion(bf16[2816,256]{1,0:T(8,128)(2,1)S(1)} %constant_dynamic-update-slice_fusion, s32[2048]{0:T(1024)S(1)} %pad_clamp_fusion), kind=kCustom, calls=%fused_computation.3 | custom fusion | bytes 1315840 | tf_op jit(solution)/shard_map/jit(_take)/gather | solution.py:175
  78.3 10.7 %shard_map.136 = bf16[256,1536]{1,0:T(8,128)(2,1)} custom-call(s32[2]{0:T(128)} %pad_add_fusion.1.where_ref, bf16[256,1536]{1,0:T(8,128)(2,1)} %multiply_convert_fusion.1.q_ref, bf16[1280,256]{1,0:T(8,128)(2,1)} %gather_fusion.3), custom_call_target="tpu_custom_call" | custom-call | tf_op jit(solution)/shard_map/pallas_call | solution.py:59
  89.0 4.1 %multiply_reduce_fusion = (f32[256]{0:T(256)S(1)}, f32[256,1536]{1,0:T(8,128)S(1)}) fusion(bf16[256,1536]{1,0:T(8,128)(2,1)} %shard_map.136, bf16[1536,1536]{1,0:T(8,128)(2,1)} %param.18, bf16[256,1536]{1,0:T(8,128)(2,1)S(1)} %copy-done.3), kind=kOutput, calls=%fused_computation.15 | convolution fusion | flops 1210318592 | bytes 7865344 | tf_op jit(solution)/shard_map/dot_general | solution.py:178
  93.1 1.1 multiply_convert_fusion
  94.2 0.0 all-gather.3.cloned.1.call-update
  94.2 0.2 reduce-scatter.2.cloned.1.call-start
  94.4 0.0 all-gather.5.cloned.1.call-done.w_ref
  94.4 40.8 %all-gather.3.cloned.1.call-done.x_ref = bf16[2048,1536]{1,0:T(8,128)(2,1)} async-done(((bf16[256,1536]{1,0:T(8,128)(2,1)}), bf16[2048,1536]{1,0:T(8,128)(2,1)}) %all-gather.3.cloned.1.call-update) | async-done | bytes 6291472 | tf_op jit(solution)/shard_map/all_gather | solution.py:181
  135.2 19.7 %shard_map.137 = bf16[2048,1536]{1,0:T(8,128)(2,1)} custom-call(bf16[2048,1536]{1,0:T(8,128)(2,1)} %all-gather.3.cloned.1.call-done.x_ref, bf16[1536,1920]{1,0:T(8,128)(2,1)} %all-gather.5.cloned.1.call-done.w_ref), custom_call_target="tpu_custom_call" | custom-call | tf_op jit(solution)/shard_map/pallas_call | solution.py:88
  154.9 0.0 reduce-scatter.2.cloned.1.call-update
  154.9 41.7 %reduce-scatter.2.cloned.1.call-done = bf16[256,1536]{1,0:T(8,128)(2,1)} async-done(((bf16[2048,1536]{1,0:T(8,128)(2,1)}), bf16[256,1536]{1,0:T(8,128)(2,1)}) %reduce-scatter.2.cloned.1.call-update) | async-done | bytes 786448 | tf_op jit(solution)/shard_map/reduce_scatter | solution.py:183
  196.6 2.2 %add_convert_fusion = bf16[256,1536]{1,0:T(8,128)(2,1)} fusion(f32[256,1536]{1,0:T(8,128)S(1)} %get-tuple-element.19, bf16[256,1536]{1,0:T(8,128)(2,1)} %reduce-scatter.2.cloned.1.call-done), kind=kLoop, calls=%fused_computation.13 | loop fusion | flops 1179648 | bytes 3145728 | tf_op jit(solution)/shard_map/convert_element_type | solution.py:186
  (34 shorter events, 0.3 us)
Async XLA Ops:
  6.5 8.0 %copy-start = (bf16[1536,256]{1,0:T(8,128)(2,1)S(1)}, bf16[1536,256]{1,0:T(8,128)(2,1)}, u32[]{:S(2)}) copy-start(bf16[1536,256]{1,0:T(8,128)(2,1)} %param.17) | copy-start | bytes 2359300
  6.5 7.7 %copy-start.2 = (bf16[256,1536]{1,0:T(8,128)(2,1)S(1)}, bf16[256,1536]{1,0:T(8,128)(2,1)}, u32[]{:S(2)}) copy-start(bf16[256,1536]{1,0:T(8,128)(2,1)} %param.14) | copy-start | bytes 2359300
  6.5 8.0 %copy-start.9 = (f32[1536]{0:T(1024)S(1)}, f32[1536]{0:T(1024)}, u32[]{:S(2)}) copy-start(f32[1536]{0:T(1024)} %param.15) | copy-start | bytes 18436
  6.5 87.9 %all-gather.5.cloned.1.call-start = ((), (), s32[]{:S(2)}) async-start(), calls=%async_computation.3 | async-start | bytes 6266880 | tf_op jit(solution)/shard_map/all_gather | solution.py:133
  8.5 7.3 %copy-start.8 = (s32[3,128]{1,0:T(4,128)S(1)}, s32[3,128]{1,0:T(4,128)}, u32[]{:S(2)}) copy-start(s32[3,128]{1,0:T(4,128)} %param.27) | copy-start | bytes 4612
  14.5 10.9 %copy-start.7 = (s32[16]{0:T(128)S(1)}, s32[16]{0:T(128)}, u32[]{:S(2)}) copy-start(s32[16]{0:T(128)} %param.25) | copy-start | bytes 196
  14.5 10.9 %copy-start.1 = (s32[128]{0:T(128)S(1)}, s32[128]{0:T(128)}, u32[]{:S(2)}) copy-start(s32[128]{0:T(128)} %param.26) | copy-start | bytes 1540
  19.4 34.9 %collective-permute-start.3 = (bf16[256,256]{0,1:T(8,128)(2,1)S(1)}, bf16[256,256]{0,1:T(8,128)(2,1)}, u32[]{:S(2)}, u32[]{:S(2)}) collective-permute-start(bf16[256,256]{0,1:T(8,128)(2,1)S(1)} %pad_maximum_fusion.2), channel_id=1, source_target_pairs={{0,1},{1,2},{2,3},{3,4},{4,5},{5,6},{6,7},{7,0},{8,9},{9,10},{10,1... | collective-permute-start | bytes 393224 | tf_op jit(solution)/shard_map/ppermute | solution.py:157
  22.0 33.3 %collective-permute-start.2 = (bf16[256,256]{0,1:T(8,128)(2,1)S(1)}, bf16[256,256]{0,1:T(8,128)(2,1)}, u32[]{:S(2)}, u32[]{:S(2)}) collective-permute-start(bf16[256,256]{0,1:T(8,128)(2,1)S(1)} %pad_maximum_fusion.2), channel_id=1, source_target_pairs={{0,2},{1,3},{2,4},{3,5},{4,6},{5,7},{6,0},{7,1},{8,10},{9,11},{10,... | collective-permute-start | bytes 393224 | tf_op jit(solution)/shard_map/ppermute | solution.py:157
  23.3 33.2 %collective-permute-start.1 = (bf16[256,256]{0,1:T(8,128)(2,1)S(1)}, bf16[256,256]{0,1:T(8,128)(2,1)}, u32[]{:S(2)}, u32[]{:S(2)}) collective-permute-start(bf16[256,256]{0,1:T(8,128)(2,1)S(1)} %pad_maximum_fusion.2), channel_id=1, source_target_pairs={{0,3},{1,4},{2,5},{3,6},{4,7},{5,0},{6,1},{7,2},{8,11},{9,12},{10,... | collective-permute-start | bytes 393224 | tf_op jit(solution)/shard_map/ppermute | solution.py:157
  24.9 32.6 %collective-permute-start = (bf16[256,256]{0,1:T(8,128)(2,1)S(1)}, bf16[256,256]{0,1:T(8,128)(2,1)}, u32[]{:S(2)}, u32[]{:S(2)}) collective-permute-start(bf16[256,256]{0,1:T(8,128)(2,1)S(1)} %pad_maximum_fusion.2), channel_id=1, source_target_pairs={{0,4},{1,5},{2,6},{3,7},{4,0},{5,1},{6,2},{7,3},{8,12},{9,13},{10,... | collective-permute-start | bytes 393224 | tf_op jit(solution)/shard_map/ppermute | solution.py:157
  29.0 29.5 %all-to-all-start = ((bf16[16,2,64,256]{3,2,1,0:T(8,128)(2,1)}), bf16[16,2,64,256]{3,2,1,0:T(8,128)(2,1)S(1)}, u32[]{:S(2)}, u32[]{:S(2)}) async-start(bf16[16,2,64,256]{3,2,1,0:T(8,128)(2,1)} %bitcast.12), calls=%async_computation | async-start | bytes 2097152 | tf_op jit(solution)/shard_map/all_to_all | solution.py:140
  36.8 98.4 %all-gather.3.cloned.1.call-start = ((), (), s32[]{:S(2)}) async-start(), calls=%async_computation.2 | async-start | bytes 7077888 | tf_op jit(solution)/shard_map/all_gather | solution.py:181
  43.8 0.9 copy-start.4
  52.9 20.6 %copy-start.5 = (bf16[1,512,256]{2,1,0:T(8,128)(2,1)S(1)}, bf16[1,512,256]{2,1,0:T(8,128)(2,1)}, u32[]{:S(2)}) copy-start(bf16[1,512,256]{2,1,0:T(8,128)(2,1)} %param.24) | copy-start | bytes 786436
  78.3 10.7 %copy-start.3 = (bf16[256,1536]{1,0:T(8,128)(2,1)S(1)}, bf16[256,1536]{1,0:T(8,128)(2,1)}, u32[]{:S(2)}) copy-start(bf16[256,1536]{1,0:T(8,128)(2,1)} %param.14) | copy-start | bytes 2359300
  89.0 4.1 %copy-start.6 = (f32[1536]{0:T(1024)S(1)}, f32[1536]{0:T(1024)}, u32[]{:S(2)}) copy-start(f32[1536]{0:T(1024)} %param.19) | copy-start | bytes 18436
  94.2 102.4 %reduce-scatter.2.cloned.1.call-start = ((), (), s32[]{:S(2)}) async-start(), calls=%async_computation.4 | async-start | bytes 7077888 | tf_op jit(solution)/shard_map/reduce_scatter | solution.py:183
Sparse Core Ops, SparseCore 0:
  9.5 67.7 all-gather.4
  94.3 40.8 all-gather.2
  155.0 41.5 reduce-scatter.1

commit v11 on v9

--- a/solution.py
+++ b/solution.py
@@ -94,12 +94,15 @@
     node_dev = prefix_kv.shape[1]
     seg_slot = prefix_kv.shape[2]
     share = seg_slot // n_mlp
-    leaf = leaf_parent[mine]
-    upper = node_parent[leaf]
-    len_zero = seg_lengths[0, upper]
-    len_one = seg_lengths[1, leaf]
-    len_two = seg_lengths[2, mine]
-    total = len_zero + len_one + len_two
+    level_zero = node_parent[leaf_parent]
+    n_requests = leaf_parent.shape[0]
+    all_lengths = jnp.stack(
+        [seg_lengths[0][level_zero], seg_lengths[1][leaf_parent], seg_lengths[2, :n_requests]]
+    )
+    my_lengths = lax.dynamic_index_in_dim(all_lengths, mine, 1, keepdims=False)
+    len_zero = my_lengths[0]
+    len_one = my_lengths[1]
+    total = len_zero + len_one + my_lengths[2]
 
     ff_cols = w_gate.shape[1]
     packed = lax.all_gather(
@@ -107,7 +110,6 @@
     )
     down_full = packed[:, 2 * ff_cols :]
 
-    level_zero = node_parent[leaf_parent]
     wanted = jnp.stack([level_zero, leaf_parent], 1)
     local_slot = wanted % node_dev
     my_rows = lax.dynamic_slice_in_dim(prefix_kv, position_group * share, share, 2)

time: 204 us -> 200 us (0.980)
  between operations: 19.3 us -> 15.4 us
    dynamic_slice x3 -> x1, local copies, waits for them, and re-layouts: 3.16 us -> 0.08 us  [body(): my_lengths = lax.dynamic_index_in_dim(all_lengths, mine, 1, keepdims=False)]
  transfers between devices with their start and end apart: 8 -> 8, of which waited for: 2 -> 2; matrix products, arithmetic and copies ran while one was open for 18% -> 19% of each run, Pallas kernels for 5% -> 5%
where the time goes in v11:
time: 200 us; the launch traced here: 199 us
  waiting for transfers between devices  81.9 us (41%)
  matrix products  29.1 us (15%)
  local copies, waits for them, and re-layouts  23.9 us (12%)
  between operations  15.4 us (8%)
  blocking collectives  15.2 us (8%)
  starting transfers between devices  14 us (7%)
  Pallas kernels  10.7 us (5%)
  other arithmetic  9.22 us (5%)
    reduce_scatter x1, waiting for transfers between devices, body(): lax.psum_scatter(lax.dot_general(hidden, down_full, (((1,), (1,)), ((), (...  41.6 us
    all_gather x1, waiting for transfers between devices, body(): all_rows = lax.all_gather(ffn_in, 'mlp', axis=0, tiled=True)  40.3 us
    all_gather x1, blocking collectives, body(): levels = lax.all_gather(my_part, 'mlp', axis=1, tiled=True)  15.2 us
    dot_general x1, matrix products, body(): jnp.dot(all_rows, packed[:, :2 * ff_cols], preferred_element_type=jnp.flo...  11.1 us
    pallas_call x1, Pallas kernels, attend_window(): pl.pallas_call(_attend_kernel, grid_spec=pltpu.PrefetchScalarGridSpec(num...  10.7 us
    dot_general x1, matrix products, body(): lax.dot_general(hidden, down_full, (((1,), (1,)), ((), ())), preferred_el...  9.58 us
    all_to_all x1, starting transfers between devices, body(): lax.all_to_all(outgoing, 'req', split_axis=0, concat_axis=0, tiled=True)  7.94 us
    ppermute x4, starting transfers between devices, body(): lax.ppermute(new_keyval, 'mlp', [(i, (i + shift) % n_mlp) for i in range(...  5.94 us
  transfers between devices with their start and end apart: 8, of which 2 were waited for; matrix products, arithmetic and copies ran while one was open for 19% of the time, Pallas kernels for 5%

profile of v11, /device:TPU:1, one launch (start us, length us, event | category | flops | bytes accessed | tf_op | source)
XLA Modules:
  0.0 199.4 jit_solution(10577530033101393675)
XLA Ops:
  6.5 0.0 copy-start
  6.5 0.0 all-gather.5.cloned.1.call-start
  6.6 2.0 concatenate.63
  8.6 0.0 all-gather.5.cloned.1.call-update
  8.6 0.7 slice.60
  9.3 0.7 compare_select_fusion.8
  10.0 0.8 slice_bitcast_fusion.6
  10.7 0.7 gather_fusion.2
  11.4 0.7 gather_fusion
  12.0 0.0 copy-done.3
  12.1 0.2 fusion.19
  12.3 0.6 fusion.24
  12.9 0.0 copy-start.8
  13.0 0.7 gather_fusion.1
  13.6 0.1 constant_dynamic-slice_fusion.1
  13.7 0.6 fusion.46
  16.3 0.3 multiply_cosine_fusion
  16.7 2.6 %collective-permute-start.3 = (bf16[256,256]{0,1:T(8,128)(2,1)S(1)}, bf16[256,256]{0,1:T(8,128)(2,1)}, u32[]{:S(2)}, u32[]{:S(2)}) collective-permute-start(bf16[256,256]{0,1:T(8,128)(2,1)S(1)} %pad_maximum_fusion.2), channel_id=1, source_target_pairs={{0,1},{1,2},{2,3},{3,4},{4,5},{5,6},{6,7},{7,0},{8,9},{9,10},{10,1... | collective-permute-start | bytes 393224 | tf_op jit(solution)/shard_map/ppermute | solution.py:134
  19.3 1.2 collective-permute-start.2
  20.5 1.6 collective-permute-start.1
  22.1 0.5 collective-permute-start
  22.6 0.1 copy.26
  22.7 0.1 reshape.332
  22.8 1.1 constant_dynamic-slice_fusion
  23.9 1.6 gather_fusion.3
  25.5 7.9 %all-to-all-start = ((bf16[16,2,64,256]{3,2,1,0:T(8,128)(2,1)}), bf16[16,2,64,256]{3,2,1,0:T(8,128)(2,1)}, u32[]{:S(2)}, u32[]{:S(2)}) async-start(bf16[16,2,64,256]{3,2,1,0:T(8,128)(2,1)} %bitcast.16), calls=%async_computation | async-start | bytes 2097152 | tf_op jit(solution)/shard_map/all_to_all | solution.py:117
  33.5 0.0 all-gather.3.cloned.1.call-start
  33.5 0.2 dynamic-slice_reduce_fusion
  33.7 3.8 %fusion.26 = f32[256,1536]{1,0:T(8,128)S(1)} fusion(bf16[1536,1536]{1,0:T(8,128)(2,1)} %param.16, bf16[256,1536]{1,0:T(8,128)(2,1)S(1)} %copy-done.4, f32[1536]{0:T(1024)S(1)} %copy-done.9, f32[256]{0:T(256)S(1)} %add_rsqrt_fusion.1), kind=kOutput, calls=%fused_computation.43 | convolution fusion | flops 1209532416 | bytes 7085056 | tf_op jit(solution)/shard_map/dot_general | solution.py:124
  37.5 0.5 copy.24
  38.0 0.1 fusion.45
  38.1 0.1 maximum_multiply_fusion
  38.2 1.6 copy.25
  39.9 0.1 mul.137
  40.0 1.6 copy.23
  41.6 3.3 %multiply_convert_fusion.1.q_ref = bf16[256,1536]{1,0:T(8,128)(2,1)} fusion(f32[256,1536]{1,0:T(8,128)} %copy.25, f32[256,1536]{1,0:T(8,128)S(1)} %fusion.26, f32[256,1536]{1,0:T(8,128)} %copy.23), kind=kLoop, calls=%fused_computation.36 | loop fusion | flops 1572864 | bytes 5505024 | tf_op jit(solution)/shard_map/convert_element_type | solution.py:127
  44.9 0.6 pad_add_fusion.2.where_ref
  45.5 0.1 copy.31
  45.6 0.6 fusion.31
  46.2 0.0 collective-permute-done.3
  46.2 1.0 copy.30
  47.2 0.0 collective-permute-done.2
  47.3 1.0 copy.29
  48.3 0.0 collective-permute-done.1
  48.3 1.0 copy.28
  49.3 0.0 collective-permute-done
  49.3 1.0 copy.27
  50.3 0.0 all-to-all-done
  50.3 1.8 gather_fusion.4
  52.1 15.2 %all_gather.9 = bf16[2,512,256]{2,1,0:T(8,128)(2,1)S(1)} all-gather(bf16[2,64,256]{2,1,0:T(8,128)(2,1)S(1)} %gather_fusion.4), channel_id=1, replica_groups=mesh['req'=16,'mlp'=8] {'mlp'}, dimensions={1}, use_global_device_ids=true | all-gather | bytes 589824 | tf_op jit(solution)/shard_map/all_gather | solution.py:120
  67.5 4.7 %gather_fusion.5 = bf16[1280,256]{1,0:T(8,128)(2,1)} fusion(bf16[2816,256]{1,0:T(8,128)(2,1)S(1)} %constant_dynamic-update-slice_fusion, s32[2048]{0:T(1024)S(1)} %pad_clamp_fusion), kind=kCustom, calls=%fused_computation.5 | custom fusion | bytes 1315840 | tf_op jit(solution)/shard_map/jit(_take)/gather | solution.py:152
  72.1 10.7 %shard_map.136 = bf16[256,1536]{1,0:T(8,128)(2,1)} custom-call(s32[2]{0:T(128)} %pad_add_fusion.2.where_ref, bf16[256,1536]{1,0:T(8,128)(2,1)} %multiply_convert_fusion.1.q_ref, bf16[1280,256]{1,0:T(8,128)(2,1)} %gather_fusion.5), custom_call_target="tpu_custom_call" | custom-call | tf_op jit(solution)/shard_map/pallas_call | solution.py:59
  82.8 4.1 %multiply_reduce_fusion = (f32[256]{0:T(256)S(1)}, f32[256,1536]{1,0:T(8,128)S(1)}) fusion(bf16[256,1536]{1,0:T(8,128)(2,1)} %shard_map.136, bf16[1536,1536]{1,0:T(8,128)(2,1)} %param.18, bf16[256,1536]{1,0:T(8,128)(2,1)S(1)} %copy-done.5), kind=kOutput, calls=%fused_computation.35 | convolution fusion | flops 1210318592 | bytes 7865344 | tf_op jit(solution)/shard_map/dot_general | solution.py:155
  86.9 1.1 multiply_convert_fusion
  88.0 0.0 all-gather.3.cloned.1.call-update
  88.0 0.0 reduce-scatter.2.cloned.1.call-start
  88.1 0.0 all-gather.5.cloned.1.call-done
  88.1 40.3 %all-gather.3.cloned.1.call-done = bf16[2048,1536]{1,0:T(8,128)(2,1)} async-done(((bf16[256,1536]{1,0:T(8,128)(2,1)}), bf16[2048,1536]{1,0:T(8,128)(2,1)}) %all-gather.3.cloned.1.call-update) | async-done | bytes 6291472 | tf_op jit(solution)/shard_map/all_gather | solution.py:158
  128.4 11.1 %fusion.9 = f32[2048,1152]{0,1:T(8,128)S(1)} fusion(bf16[2048,1536]{1,0:T(8,128)(2,1)} %all-gather.3.cloned.1.call-done, bf16[1536,1728]{1,0:T(8,128)(2,1)} %all-gather.5.cloned.1.call-done), kind=kOutput, calls=%fused_computation.17 | convolution fusion | flops 7247757312 | bytes 19267584 | tf_op jit(solution)/shard_map/dot_general | solution.py:159
  139.5 9.6 %convolution_convert_fusion = bf16[2048,1536]{1,0:T(8,128)(2,1)} fusion(f32[2048,1152]{0,1:T(8,128)S(1)} %fusion.9, bf16[1536,1728]{1,0:T(8,128)(2,1)} %all-gather.5.cloned.1.call-done), kind=kOutput, calls=%fused_computation.6 | convolution fusion | flops 3638820864 | bytes 17694720 | tf_op jit(solution)/shard_map/dot_general | solution.py:164
  149.1 0.0 reduce-scatter.2.cloned.1.call-update
  149.1 0.0 copy-start.1
  149.1 41.6 %reduce-scatter.2.cloned.1.call-done = bf16[256,1536]{1,0:T(8,128)(2,1)} async-done(((bf16[2048,1536]{1,0:T(8,128)(2,1)}), bf16[256,1536]{1,0:T(8,128)(2,1)}) %reduce-scatter.2.cloned.1.call-update) | async-done | bytes 786448 | tf_op jit(solution)/shard_map/reduce_scatter | solution.py:163
  190.7 2.2 %add_convert_fusion = bf16[256,1536]{1,0:T(8,128)(2,1)} fusion(f32[256,1536]{1,0:T(8,128)S(1)} %get-tuple-element.21, bf16[256,1536]{1,0:T(8,128)(2,1)} %reduce-scatter.2.cloned.1.call-done), kind=kLoop, calls=%fused_computation.33 | loop fusion | flops 1179648 | bytes 3145728 | tf_op jit(solution)/shard_map/convert_element_type | solution.py:171
  (41 shorter events, 0.3 us)
Async XLA Ops:
  6.5 5.8 %copy-start = (bf16[1536,256]{1,0:T(8,128)(2,1)S(1)}, bf16[1536,256]{1,0:T(8,128)(2,1)}, u32[]{:S(2)}) copy-start(bf16[1536,256]{1,0:T(8,128)(2,1)} %param.17) | copy-start | bytes 2359300
  6.5 4.8 %copy-start.2 = (s32[128]{0:T(128)S(1)}, s32[128]{0:T(128)}, u32[]{:S(2)}) copy-start(s32[128]{0:T(128)} %param.26) | copy-start | bytes 1540
  6.5 5.5 %copy-start.3 = (bf16[256,1536]{1,0:T(8,128)(2,1)S(1)}, bf16[256,1536]{1,0:T(8,128)(2,1)}, u32[]{:S(2)}) copy-start(bf16[256,1536]{1,0:T(8,128)(2,1)} %param.14) | copy-start | bytes 2359300
  6.5 5.8 %copy-start.9 = (f32[1536]{0:T(1024)S(1)}, f32[1536]{0:T(1024)}, u32[]{:S(2)}) copy-start(f32[1536]{0:T(1024)} %param.15) | copy-start | bytes 18436
  6.5 81.5 %all-gather.5.cloned.1.call-start = ((), (), s32[]{:S(2)}) async-start(), calls=%async_computation.3 | async-start | bytes 5849088 | tf_op jit(solution)/shard_map/all_gather | solution.py:108
  12.9 9.7 %copy-start.8 = (s32[16]{0:T(128)S(1)}, s32[16]{0:T(128)}, u32[]{:S(2)}) copy-start(s32[16]{0:T(128)} %param.25) | copy-start | bytes 196
  16.7 29.6 %collective-permute-start.3 = (bf16[256,256]{0,1:T(8,128)(2,1)S(1)}, bf16[256,256]{0,1:T(8,128)(2,1)}, u32[]{:S(2)}, u32[]{:S(2)}) collective-permute-start(bf16[256,256]{0,1:T(8,128)(2,1)S(1)} %pad_maximum_fusion.2), channel_id=1, source_target_pairs={{0,1},{1,2},{2,3},{3,4},{4,5},{5,6},{6,7},{7,0},{8,9},{9,10},{10,1... | collective-permute-start | bytes 393224 | tf_op jit(solution)/shard_map/ppermute | solution.py:134
  19.3 28.0 %collective-permute-start.2 = (bf16[256,256]{0,1:T(8,128)(2,1)S(1)}, bf16[256,256]{0,1:T(8,128)(2,1)}, u32[]{:S(2)}, u32[]{:S(2)}) collective-permute-start(bf16[256,256]{0,1:T(8,128)(2,1)S(1)} %pad_maximum_fusion.2), channel_id=1, source_target_pairs={{0,2},{1,3},{2,4},{3,5},{4,6},{5,7},{6,0},{7,1},{8,10},{9,11},{10,... | collective-permute-start | bytes 393224 | tf_op jit(solution)/shard_map/ppermute | solution.py:134
  20.5 27.8 %collective-permute-start.1 = (bf16[256,256]{0,1:T(8,128)(2,1)S(1)}, bf16[256,256]{0,1:T(8,128)(2,1)}, u32[]{:S(2)}, u32[]{:S(2)}) collective-permute-start(bf16[256,256]{0,1:T(8,128)(2,1)S(1)} %pad_maximum_fusion.2), channel_id=1, source_target_pairs={{0,3},{1,4},{2,5},{3,6},{4,7},{5,0},{6,1},{7,2},{8,11},{9,12},{10,... | collective-permute-start | bytes 393224 | tf_op jit(solution)/shard_map/ppermute | solution.py:134
  22.1 27.2 %collective-permute-start = (bf16[256,256]{0,1:T(8,128)(2,1)S(1)}, bf16[256,256]{0,1:T(8,128)(2,1)}, u32[]{:S(2)}, u32[]{:S(2)}) collective-permute-start(bf16[256,256]{0,1:T(8,128)(2,1)S(1)} %pad_maximum_fusion.2), channel_id=1, source_target_pairs={{0,4},{1,5},{2,6},{3,7},{4,0},{5,1},{6,2},{7,3},{8,12},{9,13},{10,... | collective-permute-start | bytes 393224 | tf_op jit(solution)/shard_map/ppermute | solution.py:134
  25.5 8.2 %copy-start.4 = (bf16[256,1536]{1,0:T(8,128)(2,1)S(1)}, bf16[256,1536]{1,0:T(8,128)(2,1)}, u32[]{:S(2)}) copy-start(bf16[256,1536]{1,0:T(8,128)(2,1)} %param.14) | copy-start | bytes 2359300
  25.5 24.8 %all-to-all-start = ((bf16[16,2,64,256]{3,2,1,0:T(8,128)(2,1)}), bf16[16,2,64,256]{3,2,1,0:T(8,128)(2,1)}, u32[]{:S(2)}, u32[]{:S(2)}) async-start(bf16[16,2,64,256]{3,2,1,0:T(8,128)(2,1)} %bitcast.16), calls=%async_computation | async-start | bytes 2097152 | tf_op jit(solution)/shard_map/all_to_all | solution.py:117
  33.5 94.9 %all-gather.3.cloned.1.call-start = ((), (), s32[]{:S(2)}) async-start(), calls=%async_computation.2 | async-start | bytes 7077888 | tf_op jit(solution)/shard_map/all_gather | solution.py:158
  44.9 22.5 %copy-start.6 = (bf16[1,512,256]{2,1,0:T(8,128)(2,1)S(1)}, bf16[1,512,256]{2,1,0:T(8,128)(2,1)}, u32[]{:S(2)}) copy-start(bf16[1,512,256]{2,1,0:T(8,128)(2,1)} %param.24) | copy-start | bytes 786436
  72.1 10.7 %copy-start.5 = (bf16[256,1536]{1,0:T(8,128)(2,1)S(1)}, bf16[256,1536]{1,0:T(8,128)(2,1)}, u32[]{:S(2)}) copy-start(bf16[256,1536]{1,0:T(8,128)(2,1)} %param.14) | copy-start | bytes 2359300
  82.8 4.1 %copy-start.7 = (f32[1536]{0:T(1024)S(1)}, f32[1536]{0:T(1024)}, u32[]{:S(2)}) copy-start(f32[1536]{0:T(1024)} %param.19) | copy-start | bytes 18436
  88.0 102.7 %reduce-scatter.2.cloned.1.call-start = ((), (), s32[]{:S(2)}) async-start(), calls=%async_computation.4 | async-start | bytes 7077888 | tf_op jit(solution)/shard_map/reduce_scatter | solution.py:163
  149.1 43.8 %copy-start.1 = (bf16[1536,256]{1,0:T(8,128)(2,1)S(1)}, bf16[1536,256]{1,0:T(8,128)(2,1)}, u32[]{:S(2)}) copy-start(bf16[1536,256]{1,0:T(8,128)(2,1)} %param.17) | copy-start | bytes 2359300
Sparse Core Ops, SparseCore 0:
  9.6 67.4 all-gather.4
  88.1 40.2 all-gather.2
  149.2 41.3 reduce-scatter.1

commit v12 on v11

--- a/solution.py
+++ b/solution.py
@@ -30,9 +30,11 @@
     return values * cos_both + swapped * sin_signed
 
 
-def _attend_kernel(where_ref, q_ref, kv_ref, o_ref):
+def _attend_kernel(where_ref, q_ref, cos_ref, sin_ref, kv_ref, o_ref):
     keys = kv_ref[:, :HD]
     vals = kv_ref[:, HD:]
+    cosine = cos_ref[...]
+    sine = sin_ref[...]
     shape = (q_ref.shape[0], kv_ref.shape[0])
     query_at = where_ref[0] + lax.broadcasted_iota(jnp.int32, shape, 0)
     key_at = where_ref[1] + lax.broadcasted_iota(jnp.int32, shape, 1)
@@ -41,8 +43,11 @@
     bias = jnp.where(allowed, 0.0, -jnp.inf).astype(jnp.float32)
     for head in range(q_ref.shape[1] // HD):
         cols = pl.ds(head * HD, HD)
+        raw = q_ref[:, cols]
+        turned = raw * cosine + pltpu.roll(raw, HD // 2, 1) * sine
+        query = (turned * HD ** (-0.5)).astype(jnp.bfloat16)
         scores = lax.dot_general(
-            q_ref[:, cols], keys, (((1,), (1,)), ((), ())), preferred_element_type=jnp.float32
+            query, keys, (((1,), (1,)), ((), ())), preferred_element_type=jnp.float32
         )
         scores = scores + bias
         top = jnp.max(scores, axis=1, keepdims=True)
@@ -52,8 +57,8 @@
         o_ref[:, cols] = (mixed / denom).astype(o_ref.dtype)
 
 
-def attend_window(queries, window, where, heads_per_step=4):
-    rows, width = queries.shape
+def attend_window(query_full, cosine, sine, window, where, heads_per_step=4):
+    rows, width = query_full.shape
     span = window.shape[0]
     step_cols = heads_per_step * HD
     return pl.pallas_call(
@@ -63,12 +68,14 @@
             grid=(width // step_cols,),
             in_specs=[
                 pl.BlockSpec((rows, step_cols), lambda h, w: (0, h)),
+                pl.BlockSpec((rows, HD), lambda h, w: (0, 0)),
+                pl.BlockSpec((rows, HD), lambda h, w: (0, 0)),
                 pl.BlockSpec((span, 2 * HD), lambda h, w: (0, 0)),
             ],
             out_specs=pl.BlockSpec((rows, step_cols), lambda h, w: (0, h)),
         ),
         out_shape=jax.ShapeDtypeStruct((rows, width), jnp.bfloat16),
-    )(where, queries, window)
+    )(where, query_full, cosine, sine, window)
 
 
 def body(
@@ -121,12 +128,16 @@
 
     query_at = total + position_group * tok_rows + jnp.arange(tok_rows, dtype=jnp.int32)
     normed = rms_scale(tokens, attn_gain).astype(jnp.bfloat16)
-    query_full = jnp.dot(normed, w_query, preferred_element_type=jnp.float32).reshape(
-        tok_rows, HEADS, HD
-    )
-    queries = (rotate(query_full, query_at) * HD ** (-0.5)).astype(jnp.bfloat16)
+    query_full = jnp.dot(normed, w_query, preferred_element_type=jnp.float32)
     keyval_full = jnp.dot(normed, w_keyval, preferred_element_type=jnp.float32)
-    new_keys = rotate(keyval_full[:, None, :HD], query_at)[:, 0].astype(jnp.bfloat16)
+    half_dim = HD // 2
+    freqs = 10000.0 ** (-jnp.arange(half_dim, dtype=jnp.float32) / half_dim)
+    angles = query_at.astype(jnp.float32)[:, None] * jnp.concatenate([freqs, freqs])[None, :]
+    cosine = jnp.cos(angles)
+    sine = jnp.sin(angles) * jnp.where(jnp.arange(HD) < half_dim, -1.0, 1.0)
+    raw_keys = keyval_full[:, :HD]
+    swapped = jnp.concatenate([raw_keys[:, half_dim:], raw_keys[:, :half_dim]], 1)
+    new_keys = (raw_keys * cosine + swapped * sine).astype(jnp.bfloat16)
     new_vals = keyval_full[:, HD:].astype(jnp.bfloat16)
     new_keyval = jnp.concatenate([new_keys, new_vals], 1)
     back = WINDOW // tok_rows
@@ -151,7 +162,7 @@
     )
     window = jnp.take(sources, source_row, axis=0, mode="clip")
     where = jnp.stack([total + position_group * tok_rows, first]).astype(jnp.int32)
-    context = attend_window(queries.reshape(tok_rows, HEADS * HD), window, where)
+    context = attend_window(query_full, cosine, sine, window, where)
     attn_out = jnp.dot(context, w_out, preferred_element_type=jnp.float32)
     resid = (tokens.astype(jnp.float32) + attn_out).astype(jnp.bfloat16)
     ffn_in = rms_scale(resid, ffn_gain).astype(jnp.bfloat16)

time: 200 us -> 201 us (level)
  waiting for transfers between devices: 81.9 us -> 89 us
  local copies, waits for them, and re-layouts: 23.9 us -> 17.3 us
    all_to_all x1, waiting for transfers between devices: 0.01 us -> 8.81 us  [body(): lax.all_to_all(outgoing, 'req', split_axis=0, concat_axis=0, tiled=True)]
    ppermute x4 -> x0, local copies, waits for them, and re-layouts: 4.02 us -> none  [body(): lax.ppermute(new_keyval, 'mlp', [(i, (i + shift) % n_mlp) for i in range(...]
    mul x3 -> x0, local copies, waits for them, and re-layouts: 3.39 us -> none  [rotate(): return values * cos_both + swapped * sin_signed]
    unnamed x27 -> x21, local copies, waits for them, and re-layouts: 0.14 us -> 2.85 us
    convert_element_type x3 -> x2, other arithmetic: 3.31 us -> 1.29 us  [the longest x1 1.29 us: body(): new_keys = (raw_keys * cosine + swapped * sine).astype(jnp.bfloat16)]
  transfers between devices with their start and end apart: 8 -> 8, of which waited for: 2 -> 3; matrix products, arithmetic and copies ran while one was open for 19% -> 15% of each run, Pallas kernels for 5% -> 5%
where the time goes in v12:
time: 201 us; the launch traced here: 200 us
  waiting for transfers between devices  89 us (44%)
  matrix products  30.1 us (15%)
  local copies, waits for them, and re-layouts  17.3 us (9%)
  blocking collectives  16.6 us (8%)
  between operations  15.2 us (8%)
  starting transfers between devices  14 us (7%)
  Pallas kernels  10.7 us (5%)
  other arithmetic  7.59 us (4%)
    reduce_scatter x1, waiting for transfers between devices, body(): lax.psum_scatter(lax.dot_general(hidden, down_full, (((1,), (1,)), ((), (...  41.6 us
    all_gather x1, waiting for transfers between devices, body(): all_rows = lax.all_gather(ffn_in, 'mlp', axis=0, tiled=True)  38.6 us
    all_gather x1, blocking collectives, body(): levels = lax.all_gather(my_part, 'mlp', axis=1, tiled=True)  16.6 us
    dot_general x1, matrix products, body(): jnp.dot(all_rows, packed[:, :2 * ff_cols], preferred_element_type=jnp.flo...  11.1 us
    pallas_call x1, Pallas kernels, attend_window(): pl.pallas_call(_attend_kernel, grid_spec=pltpu.PrefetchScalarGridSpec(num...  10.7 us
    dot_general x1, matrix products, body(): lax.dot_general(hidden, down_full, (((1,), (1,)), ((), ())), preferred_el...  9.56 us
    all_to_all x1, waiting for transfers between devices, body(): lax.all_to_all(outgoing, 'req', split_axis=0, concat_axis=0, tiled=True)  8.81 us
    all_to_all x1, starting transfers between devices, body(): lax.all_to_all(outgoing, 'req', split_axis=0, concat_axis=0, tiled=True)  7.77 us
  transfers between devices with their start and end apart: 8, of which 3 were waited for; matrix products, arithmetic and copies ran while one was open for 15% of the time, Pallas kernels for 5%

profile of v12, /device:TPU:1, one launch (start us, length us, event | category | flops | bytes accessed | tf_op | source)
XLA Modules:
  0.0 200.5 jit_solution(14259830382747444075)
XLA Ops:
  6.5 0.0 copy-start
  6.5 0.0 copy-start.1
  6.5 0.0 all-gather.5.cloned.1.call-start
  6.6 2.0 concatenate.46
  8.6 0.0 all-gather.5.cloned.1.call-update
  8.6 0.7 slice.56
  9.3 0.7 compare_select_fusion.8
  10.0 0.8 slice_bitcast_fusion.3
  10.7 0.7 gather_fusion.2
  11.4 0.0 copy-done.1
  11.4 0.7 gather_fusion
  12.1 0.0 copy-done.2
  12.1 0.2 fusion.19
  12.3 0.0 copy-done
  12.3 0.0 copy-done.6
  12.3 0.4 fusion.24
  12.8 0.0 copy-start.5
  12.8 0.7 gather_fusion.1
  13.5 0.1 constant_dynamic-slice_fusion.1
  13.6 0.6 fusion.46
  16.0 0.1 compare_select_fusion.9
  16.1 0.1 fusion.45
  16.2 1.3 fusion.30
  17.4 0.7 pad_maximum_fusion
  18.1 2.6 %collective-permute-start.3 = (bf16[256,256]{1,0:T(8,128)(2,1)}, bf16[256,256]{1,0:T(8,128)(2,1)S(1)}, u32[]{:S(2)}, u32[]{:S(2)}) collective-permute-start(bf16[256,256]{1,0:T(8,128)(2,1)} %pad_maximum_fusion), channel_id=1, source_target_pairs={{0,1},{1,2},{2,3},{3,4},{4,5},{5,6},{6,7},{7,0},{8,9},{9,10},{10,1... | collective-permute-start | bytes 393224 | tf_op jit(solution)/shard_map/ppermute | solution.py:145
  20.7 1.2 collective-permute-start.2
  21.9 1.5 collective-permute-start.1
  23.5 0.5 collective-permute-start
  24.0 0.0 copy-done.5
  24.0 0.1 copy.20
  24.1 0.1 reshape.315
  24.2 1.1 constant_dynamic-slice_fusion
  25.3 1.6 gather_fusion.3
  26.9 7.8 %all-to-all-start = ((bf16[16,2,64,256]{3,2,1,0:T(8,128)(2,1)}), bf16[16,2,64,256]{3,2,1,0:T(8,128)(2,1)S(1)}, u32[]{:S(2)}, u32[]{:S(2)}) async-start(bf16[16,2,64,256]{3,2,1,0:T(8,128)(2,1)} %bitcast.13), calls=%async_computation | async-start | bytes 2097152 | tf_op jit(solution)/shard_map/all_to_all | solution.py:124
  34.7 0.0 all-gather.3.cloned.1.call-start
  34.8 0.2 dynamic-slice_reduce_fusion
  34.9 0.6 fusion.31
  35.6 0.7 pad_add_fusion.2.where_ref
  36.2 4.9 %fusion.26.q_ref = f32[256,1536]{1,0:T(8,128)} fusion(bf16[1536,1536]{1,0:T(8,128)(2,1)} %param.16, bf16[256,1536]{1,0:T(8,128)(2,1)S(1)} %copy-done.2, f32[1536]{0:T(1024)S(1)} %copy-done.6, f32[256]{0:T(256)S(1)} %add_rsqrt_fusion.1), kind=kOutput, calls=%fused_computation.41 | convolution fusion | flops 1209532416 | bytes 7085056 | tf_op jit(solution)/shard_map/dot_general | solution.py:131
  41.2 8.8 %all-to-all-done = bf16[16,2,64,256]{3,2,1,0:T(8,128)(2,1)S(1)} async-done(((bf16[16,2,64,256]{3,2,1,0:T(8,128)(2,1)}), bf16[16,2,64,256]{3,2,1,0:T(8,128)(2,1)S(1)}, u32[]{:S(2)}, u32[]{:S(2)}) %all-to-all-start) | async-done | bytes 1048608 | tf_op jit(solution)/shard_map/all_to_all | solution.py:124
  50.0 0.6 gather_fusion.4
  50.5 16.6 %all_gather.9 = bf16[2,512,256]{2,1,0:T(8,128)(2,1)S(1)} all-gather(bf16[2,64,256]{2,1,0:T(8,128)(2,1)S(1)} %gather_fusion.4), channel_id=1, replica_groups=mesh['req'=16,'mlp'=8] {'mlp'}, dimensions={1}, use_global_device_ids=true | all-gather | bytes 589824 | tf_op jit(solution)/shard_map/all_gather | solution.py:127
  67.2 0.0 copy-done.3
  67.2 0.0 collective-permute-done
  67.2 0.9 constant_dynamic-update-slice_fusion.4
  68.1 0.0 collective-permute-done.1
  68.2 0.9 constant_dynamic-update-slice_fusion.3
  69.1 0.0 collective-permute-done.2
  69.1 0.9 constant_dynamic-update-slice_fusion.2
  70.0 0.0 collective-permute-done.3
  70.1 4.7 %gather_fusion.5 = bf16[1280,256]{1,0:T(8,128)(2,1)} fusion(bf16[2816,256]{1,0:T(8,128)(2,1)S(1)} %constant_dynamic-update-slice_fusion, s32[2048]{0:T(1024)S(1)} %pad_clamp_fusion), kind=kCustom, calls=%fused_computation.5 | custom fusion | bytes 1315840 | tf_op jit(solution)/shard_map/jit(_take)/gather | solution.py:163
  74.7 10.7 %shard_map.136 = bf16[256,1536]{1,0:T(8,128)(2,1)} custom-call(s32[2]{0:T(128)} %pad_add_fusion.2.where_ref, f32[256,1536]{1,0:T(8,128)} %fusion.26.q_ref, f32[256,128]{1,0:T(8,128)} %get-tuple-element.14.cos_ref, f32[256,128]{1,0:T(8,128)} %get-tuple-element.8.sin_ref, bf16[1280,256]{1,0:T(8,128)(2,1)} %gather_fusion.5), custom_call_target="tpu_custom_call" | custom-call | tf_op jit(solution)/shard_map/pallas_call | solution.py:64
  85.5 4.1 %multiply_reduce_fusion = (f32[256]{0:T(256)S(1)}, f32[256,1536]{1,0:T(8,128)S(1)}) fusion(bf16[256,1536]{1,0:T(8,128)(2,1)} %shard_map.136, bf16[1536,1536]{1,0:T(8,128)(2,1)} %param.18, bf16[256,1536]{1,0:T(8,128)(2,1)S(1)} %copy-done.2), kind=kOutput, calls=%fused_computation.34 | convolution fusion | flops 1210318592 | bytes 7865344 | tf_op jit(solution)/shard_map/dot_general | solution.py:166
  89.5 0.0 copy-done.4
  89.6 1.1 multiply_convert_fusion
  90.6 0.0 all-gather.3.cloned.1.call-update
  90.7 0.2 reduce-scatter.2.cloned.1.call-start
  90.9 0.0 all-gather.5.cloned.1.call-done
  90.9 38.6 %all-gather.3.cloned.1.call-done = bf16[2048,1536]{1,0:T(8,128)(2,1)} async-done(((bf16[256,1536]{1,0:T(8,128)(2,1)}), bf16[2048,1536]{1,0:T(8,128)(2,1)}) %all-gather.3.cloned.1.call-update) | async-done | bytes 6291472 | tf_op jit(solution)/shard_map/all_gather | solution.py:169
  129.5 11.1 %fusion.9 = f32[2048,1152]{0,1:T(8,128)S(1)} fusion(bf16[2048,1536]{1,0:T(8,128)(2,1)} %all-gather.3.cloned.1.call-done, bf16[1536,1728]{1,0:T(8,128)(2,1)} %all-gather.5.cloned.1.call-done), kind=kOutput, calls=%fused_computation.17 | convolution fusion | flops 7247757312 | bytes 19267584 | tf_op jit(solution)/shard_map/dot_general | solution.py:170
  140.6 9.6 %convolution_convert_fusion = bf16[2048,1536]{1,0:T(8,128)(2,1)} fusion(f32[2048,1152]{0,1:T(8,128)S(1)} %fusion.9, bf16[1536,1728]{1,0:T(8,128)(2,1)} %all-gather.5.cloned.1.call-done), kind=kOutput, calls=%fused_computation.6 | convolution fusion | flops 3638820864 | bytes 17694720 | tf_op jit(solution)/shard_map/dot_general | solution.py:175
  150.2 0.0 reduce-scatter.2.cloned.1.call-update
  150.2 41.6 %reduce-scatter.2.cloned.1.call-done = bf16[256,1536]{1,0:T(8,128)(2,1)} async-done(((bf16[2048,1536]{1,0:T(8,128)(2,1)}), bf16[256,1536]{1,0:T(8,128)(2,1)}) %reduce-scatter.2.cloned.1.call-update) | async-done | bytes 786448 | tf_op jit(solution)/shard_map/reduce_scatter | solution.py:174
  191.8 2.2 %add_convert_fusion = bf16[256,1536]{1,0:T(8,128)(2,1)} fusion(f32[256,1536]{1,0:T(8,128)S(1)} %get-tuple-element.16, bf16[256,1536]{1,0:T(8,128)(2,1)} %reduce-scatter.2.cloned.1.call-done), kind=kLoop, calls=%fused_computation.32 | loop fusion | flops 1179648 | bytes 3145728 | tf_op jit(solution)/shard_map/convert_element_type | solution.py:182
  (22 shorter events, 0.2 us)
Async XLA Ops:
  6.5 5.8 %copy-start = (bf16[1536,256]{1,0:T(8,128)(2,1)S(1)}, bf16[1536,256]{1,0:T(8,128)(2,1)}, u32[]{:S(2)}) copy-start(bf16[1536,256]{1,0:T(8,128)(2,1)} %param.17) | copy-start | bytes 2359300
  6.5 4.8 %copy-start.1 = (s32[128]{0:T(128)S(1)}, s32[128]{0:T(128)}, u32[]{:S(2)}) copy-start(s32[128]{0:T(128)} %param.26) | copy-start | bytes 1540
  6.5 5.5 %copy-start.2 = (bf16[256,1536]{1,0:T(8,128)(2,1)S(1)}, bf16[256,1536]{1,0:T(8,128)(2,1)}, u32[]{:S(2)}) copy-start(bf16[256,1536]{1,0:T(8,128)(2,1)} %param.14) | copy-start | bytes 2359300
  6.5 5.8 %copy-start.6 = (f32[1536]{0:T(1024)S(1)}, f32[1536]{0:T(1024)}, u32[]{:S(2)}) copy-start(f32[1536]{0:T(1024)} %param.15) | copy-start | bytes 18436
  6.5 84.4 %all-gather.5.cloned.1.call-start = ((), (), s32[]{:S(2)}) async-start(), calls=%async_computation.3 | async-start | bytes 5849088 | tf_op jit(solution)/shard_map/all_gather | solution.py:115
  12.8 11.3 %copy-start.5 = (s32[16]{0:T(128)S(1)}, s32[16]{0:T(128)}, u32[]{:S(2)}) copy-start(s32[16]{0:T(128)} %param.25) | copy-start | bytes 196
  18.1 51.9 %collective-permute-start.3 = (bf16[256,256]{1,0:T(8,128)(2,1)}, bf16[256,256]{1,0:T(8,128)(2,1)S(1)}, u32[]{:S(2)}, u32[]{:S(2)}) collective-permute-start(bf16[256,256]{1,0:T(8,128)(2,1)} %pad_maximum_fusion), channel_id=1, source_target_pairs={{0,1},{1,2},{2,3},{3,4},{4,5},{5,6},{6,7},{7,0},{8,9},{9,10},{10,1... | collective-permute-start | bytes 393224 | tf_op jit(solution)/shard_map/ppermute | solution.py:145
  20.7 48.4 %collective-permute-start.2 = (bf16[256,256]{1,0:T(8,128)(2,1)}, bf16[256,256]{1,0:T(8,128)(2,1)}, u32[]{:S(2)}, u32[]{:S(2)}) collective-permute-start(bf16[256,256]{1,0:T(8,128)(2,1)} %pad_maximum_fusion), channel_id=1, source_target_pairs={{0,2},{1,3},{2,4},{3,5},{4,6},{5,7},{6,0},{7,1},{8,10},{9,11},{10,... | collective-permute-start | bytes 393224 | tf_op jit(solution)/shard_map/ppermute | solution.py:145
  21.9 46.2 %collective-permute-start.1 = (bf16[256,256]{1,0:T(8,128)(2,1)}, bf16[256,256]{1,0:T(8,128)(2,1)}, u32[]{:S(2)}, u32[]{:S(2)}) collective-permute-start(bf16[256,256]{1,0:T(8,128)(2,1)} %pad_maximum_fusion), channel_id=1, source_target_pairs={{0,3},{1,4},{2,5},{3,6},{4,7},{5,0},{6,1},{7,2},{8,11},{9,12},{10,... | collective-permute-start | bytes 393224 | tf_op jit(solution)/shard_map/ppermute | solution.py:145
  23.5 43.7 %collective-permute-start = (bf16[256,256]{1,0:T(8,128)(2,1)}, bf16[256,256]{1,0:T(8,128)(2,1)}, u32[]{:S(2)}, u32[]{:S(2)}) collective-permute-start(bf16[256,256]{1,0:T(8,128)(2,1)} %pad_maximum_fusion), channel_id=1, source_target_pairs={{0,4},{1,5},{2,6},{3,7},{4,0},{5,1},{6,2},{7,3},{8,12},{9,13},{10,... | collective-permute-start | bytes 393224 | tf_op jit(solution)/shard_map/ppermute | solution.py:145
  26.9 23.1 %all-to-all-start = ((bf16[16,2,64,256]{3,2,1,0:T(8,128)(2,1)}), bf16[16,2,64,256]{3,2,1,0:T(8,128)(2,1)S(1)}, u32[]{:S(2)}, u32[]{:S(2)}) async-start(bf16[16,2,64,256]{3,2,1,0:T(8,128)(2,1)} %bitcast.13), calls=%async_computation | async-start | bytes 2097152 | tf_op jit(solution)/shard_map/all_to_all | solution.py:124
  34.7 94.8 %all-gather.3.cloned.1.call-start = ((), (), s32[]{:S(2)}) async-start(), calls=%async_computation.2 | async-start | bytes 7077888 | tf_op jit(solution)/shard_map/all_gather | solution.py:169
  41.2 26.0 %copy-start.3 = (bf16[1,512,256]{2,1,0:T(8,128)(2,1)S(1)}, bf16[1,512,256]{2,1,0:T(8,128)(2,1)}, u32[]{:S(2)}) copy-start(bf16[1,512,256]{2,1,0:T(8,128)(2,1)} %param.24) | copy-start | bytes 786436
  85.5 4.1 %copy-start.4 = (f32[1536]{0:T(1024)S(1)}, f32[1536]{0:T(1024)}, u32[]{:S(2)}) copy-start(f32[1536]{0:T(1024)} %param.19) | copy-start | bytes 18436
  90.7 101.1 %reduce-scatter.2.cloned.1.call-start = ((), (), s32[]{:S(2)}) async-start(), calls=%async_computation.4 | async-start | bytes 7077888 | tf_op jit(solution)/shard_map/reduce_scatter | solution.py:174
Sparse Core Ops, SparseCore 0:
  9.6 64.4 all-gather.4
  90.8 38.6 all-gather.2
  150.3 41.3 reduce-scatter.1

commit v13 on v12

--- a/solution.py
+++ b/solution.py
@@ -141,6 +141,7 @@
     new_vals = keyval_full[:, HD:].astype(jnp.bfloat16)
     new_keyval = jnp.concatenate([new_keys, new_vals], 1)
     back = WINDOW // tok_rows
+    new_keyval, arrived = lax.optimization_barrier((new_keyval, arrived))
     blocks = [
         lax.ppermute(new_keyval, "mlp", [(i, (i + shift) % n_mlp) for i in range(n_mlp)])
         for shift in range(back, 0, -1)

time: 201 us -> 199 us (0.990)
  waiting for transfers between devices: 89 us -> 85 us
  starting transfers between devices: 14 us -> 17.6 us
    ppermute x4, starting transfers between devices: 5.89 us -> 8.58 us  [body(): lax.ppermute(new_keyval, 'mlp', [(i, (i + shift) % n_mlp) for i in range(...]
    all_to_all x1, waiting for transfers between devices: 8.81 us -> 6.19 us  [body(): lax.all_to_all(outgoing, 'req', split_axis=0, concat_axis=0, tiled=True)]
  transfers between devices with their start and end apart: 8 -> 8, of which waited for: 3 -> 3; matrix products, arithmetic and copies ran while one was open for 15% -> 14% of each run, Pallas kernels for 5% -> 5%
where the time goes in v13:
time: 199 us
  waiting for transfers between devices  85 us (43%)
  matrix products  29.9 us (15%)
  starting transfers between devices  17.6 us (9%)
  blocking collectives  17.1 us (9%)
  local copies, waits for them, and re-layouts  16.5 us (8%)
  between operations  15.2 us (8%)
  Pallas kernels  10.8 us (5%)
  other arithmetic  6.92 us (3%)
    reduce_scatter x1, waiting for transfers between devices, body(): lax.psum_scatter(lax.dot_general(hidden, down_full, (((1,), (1,)), ((), (...  41.9 us
    all_gather x1, waiting for transfers between devices, body(): all_rows = lax.all_gather(ffn_in, 'mlp', axis=0, tiled=True)  36.8 us
    all_gather x1, blocking collectives, body(): levels = lax.all_gather(my_part, 'mlp', axis=1, tiled=True)  17.1 us
    dot_general x1, matrix products, body(): jnp.dot(all_rows, packed[:, :2 * ff_cols], preferred_element_type=jnp.flo...  11.1 us
    pallas_call x1, Pallas kernels, attend_window(): pl.pallas_call(_attend_kernel, grid_spec=pltpu.PrefetchScalarGridSpec(num...  10.8 us
    dot_general x1, matrix products, body(): lax.dot_general(hidden, down_full, (((1,), (1,)), ((), ())), preferred_el...  9.41 us
    all_to_all x1, starting transfers between devices, body(): lax.all_to_all(outgoing, 'req', split_axis=0, concat_axis=0, tiled=True)  8.73 us
    ppermute x4, starting transfers between devices, body(): lax.ppermute(new_keyval, 'mlp', [(i, (i + shift) % n_mlp) for i in range(...  8.58 us
  transfers between devices with their start and end apart: 8, of which 3 were waited for; matrix products, arithmetic and copies ran while one was open for 14% of the time, Pallas kernels for 5%

profile of v13, /device:TPU:1, one launch (start us, length us, event | category | flops | bytes accessed | tf_op | source)
XLA Modules:
  0.0 198.9 jit_solution(6532954110544037887)
XLA Ops:
  6.5 0.0 copy-start
  6.5 0.0 copy-start.4
  6.5 0.0 all-gather.5.cloned.1.call-start
  6.5 2.0 concatenate.46
  8.5 0.0 all-gather.5.cloned.1.call-update
  8.5 0.7 compare_select_fusion.8
  9.2 1.3 gather_fusion
  10.5 0.0 copy-done.4
  10.6 0.1 copy.20
  10.6 0.1 reshape.315
  10.7 1.1 constant_dynamic-slice_fusion
  11.8 1.6 gather_fusion.3
  13.4 0.0 copy-start.1
  13.4 0.0 copy-start.6
  13.4 8.7 %all-to-all-start = ((bf16[16,2,64,256]{3,2,1,0:T(8,128)(2,1)}), bf16[16,2,64,256]{3,2,1,0:T(8,128)(2,1)S(1)}, u32[]{:S(2)}, u32[]{:S(2)}) async-start(bf16[16,2,64,256]{3,2,1,0:T(8,128)(2,1)} %bitcast.13), calls=%async_computation | async-start | bytes 2097152 | tf_op jit(solution)/shard_map/all_to_all | solution.py:124
  22.2 0.0 all-gather.3.cloned.1.call-start
  22.2 0.0 copy-done.5
  22.3 0.7 gather_fusion.2
  22.9 0.0 copy-done.1
  22.9 0.2 fusion.19
  23.2 0.0 copy-done
  23.2 0.0 copy-done.6
  23.2 0.4 fusion.24
  23.7 0.2 dynamic-slice_reduce_fusion
  23.9 0.7 gather_fusion.1
  24.6 0.1 constant_dynamic-slice_fusion.1
  24.6 0.6 fusion.46
  27.0 0.6 fusion.31
  27.7 0.7 pad_add_fusion.2.where_ref
  28.3 0.1 compare_select_fusion.9
  28.4 0.1 fusion.45
  28.5 1.3 fusion.30
  29.8 4.9 %fusion.26.q_ref = f32[256,1536]{1,0:T(8,128)} fusion(bf16[1536,1536]{1,0:T(8,128)(2,1)} %param.16, bf16[256,1536]{1,0:T(8,128)(2,1)S(1)} %copy-done.1, f32[1536]{0:T(1024)S(1)} %copy-done.6, f32[256]{0:T(256)S(1)} %add_rsqrt_fusion.1), kind=kOutput, calls=%fused_computation.41 | convolution fusion | flops 1209532416 | bytes 7085056 | tf_op jit(solution)/shard_map/dot_general | solution.py:131
  34.8 0.0 copy-start.2
  34.8 6.2 %all-to-all-done = bf16[16,2,64,256]{3,2,1,0:T(8,128)(2,1)S(1)} async-done(((bf16[16,2,64,256]{3,2,1,0:T(8,128)(2,1)}), bf16[16,2,64,256]{3,2,1,0:T(8,128)(2,1)S(1)}, u32[]{:S(2)}, u32[]{:S(2)}) %all-to-all-start) | async-done | bytes 1048608 | tf_op jit(solution)/shard_map/all_to_all | solution.py:124
  41.0 5.3 %collective-permute-start.3 = (bf16[256,256]{1,0:T(8,128)(2,1)S(1)}, bf16[256,256]{1,0:T(8,128)(2,1)S(1)}, u32[]{:S(2)}, u32[]{:S(2)}) collective-permute-start(bf16[256,256]{1,0:T(8,128)(2,1)S(1)} %pad_maximum_fusion), channel_id=1, source_target_pairs={{0,1},{1,2},{2,3},{3,4},{4,5},{5,6},{6,7},{7,0},{8,9},{9,10},{10,1... | collective-permute-start | bytes 393224 | tf_op jit(solution)/shard_map/ppermute | solution.py:146
  46.3 1.2 collective-permute-start.2
  47.5 1.5 collective-permute-start.1
  49.0 0.5 collective-permute-start
  49.5 0.6 gather_fusion.4
  50.1 17.1 %all_gather.9 = bf16[2,512,256]{2,1,0:T(8,128)(2,1)S(1)} all-gather(bf16[2,64,256]{2,1,0:T(8,128)(2,1)S(1)} %gather_fusion.4), channel_id=1, replica_groups=mesh['req'=16,'mlp'=8] {'mlp'}, dimensions={1}, use_global_device_ids=true | all-gather | bytes 589824 | tf_op jit(solution)/shard_map/all_gather | solution.py:127
  67.2 0.0 copy-done.2
  67.2 0.0 collective-permute-done
  67.2 0.9 constant_dynamic-update-slice_fusion.4
  68.2 0.0 collective-permute-done.1
  68.2 0.9 constant_dynamic-update-slice_fusion.3
  69.1 0.0 collective-permute-done.2
  69.1 0.9 constant_dynamic-update-slice_fusion.2
  70.0 0.0 collective-permute-done.3
  70.1 4.7 %gather_fusion.5 = bf16[1280,256]{1,0:T(8,128)(2,1)} fusion(bf16[2816,256]{1,0:T(8,128)(2,1)S(1)} %constant_dynamic-update-slice_fusion, s32[2048]{0:T(1024)S(1)} %pad_clamp_fusion), kind=kCustom, calls=%fused_computation.5 | custom fusion | bytes 1315840 | tf_op jit(solution)/shard_map/jit(_take)/gather | solution.py:164
  74.7 10.8 %shard_map.136 = bf16[256,1536]{1,0:T(8,128)(2,1)} custom-call(s32[2]{0:T(128)} %pad_add_fusion.2.where_ref, f32[256,1536]{1,0:T(8,128)} %fusion.26.q_ref, f32[256,128]{1,0:T(8,128)} %get-tuple-element.16.cos_ref, f32[256,128]{1,0:T(8,128)} %get-tuple-element.10.sin_ref, bf16[1280,256]{1,0:T(8,128)(2,1)} %gather_fusion.5), custom_call_target="tpu_custom_call" | custom-call | tf_op jit(solution)/shard_map/pallas_call | solution.py:64
  85.5 0.0 copy-start.3
  85.5 4.1 %multiply_reduce_fusion = (f32[256]{0:T(256)S(1)}, f32[256,1536]{1,0:T(8,128)S(1)}) fusion(bf16[256,1536]{1,0:T(8,128)(2,1)} %shard_map.136, bf16[1536,1536]{1,0:T(8,128)(2,1)} %param.18, bf16[256,1536]{1,0:T(8,128)(2,1)S(1)} %copy-done.1), kind=kOutput, calls=%fused_computation.34 | convolution fusion | flops 1210318592 | bytes 7865344 | tf_op jit(solution)/shard_map/dot_general | solution.py:167
  89.6 0.0 copy-done.3
  89.6 1.1 multiply_convert_fusion
  90.7 0.0 all-gather.3.cloned.1.call-update
  90.7 0.2 reduce-scatter.2.cloned.1.call-start
  90.9 0.0 all-gather.5.cloned.1.call-done
  90.9 36.8 %all-gather.3.cloned.1.call-done = bf16[2048,1536]{1,0:T(8,128)(2,1)} async-done(((bf16[256,1536]{1,0:T(8,128)(2,1)}), bf16[2048,1536]{1,0:T(8,128)(2,1)}) %all-gather.3.cloned.1.call-update) | async-done | bytes 6291472 | tf_op jit(solution)/shard_map/all_gather | solution.py:170
  127.8 11.1 %fusion.9 = f32[2048,1152]{0,1:T(8,128)S(1)} fusion(bf16[2048,1536]{1,0:T(8,128)(2,1)} %all-gather.3.cloned.1.call-done, bf16[1536,1728]{1,0:T(8,128)(2,1)} %all-gather.5.cloned.1.call-done), kind=kOutput, calls=%fused_computation.17 | convolution fusion | flops 7247757312 | bytes 19267584 | tf_op jit(solution)/shard_map/dot_general | solution.py:171
  138.9 9.4 %convolution_convert_fusion = bf16[2048,1536]{1,0:T(8,128)(2,1)} fusion(f32[2048,1152]{0,1:T(8,128)S(1)} %fusion.9, bf16[1536,1728]{1,0:T(8,128)(2,1)} %all-gather.5.cloned.1.call-done), kind=kOutput, calls=%fused_computation.6 | convolution fusion | flops 3638820864 | bytes 17694720 | tf_op jit(solution)/shard_map/dot_general | solution.py:176
  148.3 0.0 reduce-scatter.2.cloned.1.call-update
  148.3 41.9 %reduce-scatter.2.cloned.1.call-done = bf16[256,1536]{1,0:T(8,128)(2,1)} async-done(((bf16[2048,1536]{1,0:T(8,128)(2,1)}), bf16[256,1536]{1,0:T(8,128)(2,1)}) %reduce-scatter.2.cloned.1.call-update) | async-done | bytes 786448 | tf_op jit(solution)/shard_map/reduce_scatter | solution.py:175
  190.2 2.2 %add_convert_fusion = bf16[256,1536]{1,0:T(8,128)(2,1)} fusion(f32[256,1536]{1,0:T(8,128)S(1)} %get-tuple-element.18, bf16[256,1536]{1,0:T(8,128)(2,1)} %reduce-scatter.2.cloned.1.call-done), kind=kLoop, calls=%fused_computation.32 | loop fusion | flops 1179648 | bytes 3145728 | tf_op jit(solution)/shard_map/convert_element_type | solution.py:183
  (22 shorter events, 0.2 us)
Async XLA Ops:
  6.5 16.7 %copy-start = (bf16[1536,256]{1,0:T(8,128)(2,1)S(1)}, bf16[1536,256]{1,0:T(8,128)(2,1)}, u32[]{:S(2)}) copy-start(bf16[1536,256]{1,0:T(8,128)(2,1)} %param.17) | copy-start | bytes 2359300
  6.5 4.0 %copy-start.4 = (s32[16]{0:T(128)S(1)}, s32[16]{0:T(128)}, u32[]{:S(2)}) copy-start(s32[16]{0:T(128)} %param.25) | copy-start | bytes 196
  6.5 84.4 %all-gather.5.cloned.1.call-start = ((), (), s32[]{:S(2)}) async-start(), calls=%async_computation.3 | async-start | bytes 5849088 | tf_op jit(solution)/shard_map/all_gather | solution.py:115
  13.4 8.8 %copy-start.5 = (s32[3,128]{1,0:T(4,128)S(1)}, s32[3,128]{1,0:T(4,128)}, u32[]{:S(2)}) copy-start(s32[3,128]{1,0:T(4,128)} %param.27) | copy-start | bytes 4612
  13.4 9.5 %copy-start.1 = (bf16[256,1536]{1,0:T(8,128)(2,1)S(1)}, bf16[256,1536]{1,0:T(8,128)(2,1)}, u32[]{:S(2)}) copy-start(bf16[256,1536]{1,0:T(8,128)(2,1)} %param.14) | copy-start | bytes 2359300
  13.4 9.8 %copy-start.6 = (f32[1536]{0:T(1024)S(1)}, f32[1536]{0:T(1024)}, u32[]{:S(2)}) copy-start(f32[1536]{0:T(1024)} %param.15) | copy-start | bytes 18436
  13.4 27.5 %all-to-all-start = ((bf16[16,2,64,256]{3,2,1,0:T(8,128)(2,1)}), bf16[16,2,64,256]{3,2,1,0:T(8,128)(2,1)S(1)}, u32[]{:S(2)}, u32[]{:S(2)}) async-start(bf16[16,2,64,256]{3,2,1,0:T(8,128)(2,1)} %bitcast.13), calls=%async_computation | async-start | bytes 2097152 | tf_op jit(solution)/shard_map/all_to_all | solution.py:124
  22.2 105.6 %all-gather.3.cloned.1.call-start = ((), (), s32[]{:S(2)}) async-start(), calls=%async_computation.2 | async-start | bytes 7077888 | tf_op jit(solution)/shard_map/all_gather | solution.py:170
  34.8 32.4 %copy-start.2 = (bf16[1,512,256]{2,1,0:T(8,128)(2,1)S(1)}, bf16[1,512,256]{2,1,0:T(8,128)(2,1)}, u32[]{:S(2)}) copy-start(bf16[1,512,256]{2,1,0:T(8,128)(2,1)} %param.24) | copy-start | bytes 786436
  41.0 29.1 %collective-permute-start.3 = (bf16[256,256]{1,0:T(8,128)(2,1)S(1)}, bf16[256,256]{1,0:T(8,128)(2,1)S(1)}, u32[]{:S(2)}, u32[]{:S(2)}) collective-permute-start(bf16[256,256]{1,0:T(8,128)(2,1)S(1)} %pad_maximum_fusion), channel_id=1, source_target_pairs={{0,1},{1,2},{2,3},{3,4},{4,5},{5,6},{6,7},{7,0},{8,9},{9,10},{10,1... | collective-permute-start | bytes 393224 | tf_op jit(solution)/shard_map/ppermute | solution.py:146
  46.3 22.8 %collective-permute-start.2 = (bf16[256,256]{1,0:T(8,128)(2,1)S(1)}, bf16[256,256]{1,0:T(8,128)(2,1)}, u32[]{:S(2)}, u32[]{:S(2)}) collective-permute-start(bf16[256,256]{1,0:T(8,128)(2,1)S(1)} %pad_maximum_fusion), channel_id=1, source_target_pairs={{0,2},{1,3},{2,4},{3,5},{4,6},{5,7},{6,0},{7,1},{8,10},{9,11},{10,... | collective-permute-start | bytes 393224 | tf_op jit(solution)/shard_map/ppermute | solution.py:146
  47.5 20.7 %collective-permute-start.1 = (bf16[256,256]{1,0:T(8,128)(2,1)S(1)}, bf16[256,256]{1,0:T(8,128)(2,1)}, u32[]{:S(2)}, u32[]{:S(2)}) collective-permute-start(bf16[256,256]{1,0:T(8,128)(2,1)S(1)} %pad_maximum_fusion), channel_id=1, source_target_pairs={{0,3},{1,4},{2,5},{3,6},{4,7},{5,0},{6,1},{7,2},{8,11},{9,12},{10,... | collective-permute-start | bytes 393224 | tf_op jit(solution)/shard_map/ppermute | solution.py:146
  49.0 18.2 %collective-permute-start = (bf16[256,256]{1,0:T(8,128)(2,1)S(1)}, bf16[256,256]{1,0:T(8,128)(2,1)}, u32[]{:S(2)}, u32[]{:S(2)}) collective-permute-start(bf16[256,256]{1,0:T(8,128)(2,1)S(1)} %pad_maximum_fusion), channel_id=1, source_target_pairs={{0,4},{1,5},{2,6},{3,7},{4,0},{5,1},{6,2},{7,3},{8,12},{9,13},{10,... | collective-permute-start | bytes 393224 | tf_op jit(solution)/shard_map/ppermute | solution.py:146
  85.5 4.1 %copy-start.3 = (f32[1536]{0:T(1024)S(1)}, f32[1536]{0:T(1024)}, u32[]{:S(2)}) copy-start(f32[1536]{0:T(1024)} %param.19) | copy-start | bytes 18436
  90.7 99.5 %reduce-scatter.2.cloned.1.call-start = ((), (), s32[]{:S(2)}) async-start(), calls=%async_computation.4 | async-start | bytes 7077888 | tf_op jit(solution)/shard_map/reduce_scatter | solution.py:175
Sparse Core Ops, SparseCore 0:
  9.5 69.3 all-gather.4
  90.8 36.9 all-gather.2
  148.4 41.7 reduce-scatter.1

commit v14 on v13

--- a/solution.py
+++ b/solution.py
@@ -124,7 +124,9 @@
     arrived = lax.all_to_all(outgoing, "req", split_axis=0, concat_axis=0, tiled=True)
     owners = wanted[mine] // node_dev
     my_part = arrived[owners, jnp.arange(2)]
-    levels = lax.all_gather(my_part, "mlp", axis=1, tiled=True)
+    fanned = jnp.broadcast_to(my_part[None], (n_mlp,) + my_part.shape)
+    levels = lax.all_to_all(fanned, "mlp", split_axis=0, concat_axis=0, tiled=True)
+    levels = jnp.swapaxes(levels, 0, 1).reshape(2, seg_slot, my_part.shape[-1])
 
     query_at = total + position_group * tok_rows + jnp.arange(tok_rows, dtype=jnp.int32)
     normed = rms_scale(tokens, attn_gain).astype(jnp.bfloat16)

time: 199 us -> 203 us (1.020)
  blocking collectives: 17.1 us -> 0 us
  waiting for transfers between devices: 85 us -> 99 us
  starting transfers between devices: 17.6 us -> 22.5 us
    all_gather x1 -> x0, blocking collectives: 17.1 us -> none  [body(): levels = lax.all_gather(my_part, 'mlp', axis=1, tiled=True)]
    ppermute x4, waiting for transfers between devices: 0.01 us -> 9.74 us  [body(): lax.ppermute(new_keyval, 'mlp', [(i, (i + shift) % n_mlp) for i in range(...]
    all_to_all x0 -> x1, starting transfers between devices: none -> 8.52 us  [body(): lax.all_to_all(fanned, 'mlp', split_axis=0, concat_axis=0, tiled=True)]
    all_to_all x1, waiting for transfers between devices: 6.19 us -> 11 us  [body(): lax.all_to_all(outgoing, 'req', split_axis=0, concat_axis=0, tiled=True)]
    ppermute x4, starting transfers between devices: 8.58 us -> 5.03 us  [body(): lax.ppermute(new_keyval, 'mlp', [(i, (i + shift) % n_mlp) for i in range(...]
  transfers between devices with their start and end apart: 8 -> 9, of which waited for: 3 -> 4; matrix products, arithmetic and copies ran while one was open for 14% -> 15% of each run, Pallas kernels for 5% -> 5%
where the time goes in v14:
time: 203 us; the launch traced here: 202 us
  waiting for transfers between devices  99 us (49%)
  matrix products  30 us (15%)
  starting transfers between devices  22.5 us (11%)
  local copies, waits for them, and re-layouts  17.4 us (9%)
  between operations  15.4 us (8%)
  Pallas kernels  10.8 us (5%)
  other arithmetic  6.92 us (3%)
    reduce_scatter x1, waiting for transfers between devices, body(): lax.psum_scatter(lax.dot_general(hidden, down_full, (((1,), (1,)), ((), (...  41.8 us
    all_gather x1, waiting for transfers between devices, body(): all_rows = lax.all_gather(ffn_in, 'mlp', axis=0, tiled=True)  36.4 us
    dot_general x1, matrix products, body(): jnp.dot(all_rows, packed[:, :2 * ff_cols], preferred_element_type=jnp.flo...  11.1 us
    all_to_all x1, waiting for transfers between devices, body(): lax.all_to_all(outgoing, 'req', split_axis=0, concat_axis=0, tiled=True)  11 us
    pallas_call x1, Pallas kernels, attend_window(): pl.pallas_call(_attend_kernel, grid_spec=pltpu.PrefetchScalarGridSpec(num...  10.8 us
    ppermute x4, waiting for transfers between devices, body(): lax.ppermute(new_keyval, 'mlp', [(i, (i + shift) % n_mlp) for i in range(...  9.74 us
    dot_general x1, matrix products, body(): lax.dot_general(hidden, down_full, (((1,), (1,)), ((), ())), preferred_el...  9.43 us
    all_to_all x1, starting transfers between devices, body(): lax.all_to_all(outgoing, 'req', split_axis=0, concat_axis=0, tiled=True)  8.73 us
  transfers between devices with their start and end apart: 9, of which 4 were waited for; matrix products, arithmetic and copies ran while one was open for 15% of the time, Pallas kernels for 5%

profile of v14, /device:TPU:1, one launch (start us, length us, event | category | flops | bytes accessed | tf_op | source)
XLA Modules:
  0.0 201.9 jit_solution(13093991014384199766)
XLA Ops:
  6.5 0.0 copy-start
  6.5 0.0 copy-start.4
  6.5 0.0 all-gather.5.cloned.1.call-start
  6.5 2.0 concatenate.46
  8.5 0.0 all-gather.5.cloned.1.call-update
  8.5 0.7 compare_select_fusion.8
  9.2 1.3 gather_fusion
  10.5 0.0 copy-done.4
  10.6 0.1 copy.25
  10.6 0.1 reshape.321
  10.7 1.1 constant_dynamic-slice_fusion
  11.8 1.6 gather_fusion.3
  13.4 0.0 copy-start.5
  13.4 0.0 copy-start.1
  13.4 8.7 %all-to-all-start = ((bf16[16,2,64,256]{3,2,1,0:T(8,128)(2,1)}), bf16[16,2,64,256]{3,2,1,0:T(8,128)(2,1)S(1)}, u32[]{:S(2)}, u32[]{:S(2)}) async-start(bf16[16,2,64,256]{3,2,1,0:T(8,128)(2,1)} %bitcast.13), calls=%async_computation | async-start | bytes 2097152 | tf_op jit(solution)/shard_map/all_to_all | solution.py:124
  22.2 0.0 copy-done.5
  22.2 0.7 gather_fusion.2
  22.9 0.0 copy-done.1
  22.9 0.2 fusion.19
  23.1 0.0 copy-done
  23.1 0.0 copy-done.6
  23.1 0.4 fusion.22
  23.6 0.2 dynamic-slice_reduce_fusion
  23.8 0.7 gather_fusion.1
  24.5 0.1 constant_dynamic-slice_fusion.1
  24.6 0.6 fusion.45
  27.1 0.7 fusion.29
  27.8 0.1 compare_select_fusion.9
  27.9 0.6 pad_add_fusion.2.where_ref
  28.5 0.1 fusion.44
  28.6 1.3 fusion.28
  29.9 11.0 %all-to-all-done = bf16[16,2,64,256]{3,2,1,0:T(8,128)(2,1)S(1)} async-done(((bf16[16,2,64,256]{3,2,1,0:T(8,128)(2,1)}), bf16[16,2,64,256]{3,2,1,0:T(8,128)(2,1)S(1)}, u32[]{:S(2)}, u32[]{:S(2)}) %all-to-all-start) | async-done | bytes 1048608 | tf_op jit(solution)/shard_map/all_to_all | solution.py:124
  40.9 0.6 gather_fusion.4
  41.5 0.8 broadcast_in_dim.17
  42.3 8.5 %all-to-all-start.1 = ((bf16[8,2,64,256]{3,2,1,0:T(8,128)(2,1)}), bf16[8,2,64,256]{3,2,1,0:T(8,128)(2,1)S(1)}, u32[]{:S(2)}, u32[]{:S(2)}) async-start(bf16[8,2,64,256]{3,2,1,0:T(8,128)(2,1)} %broadcast_in_dim.17), calls=%async_computation.1 | async-start | bytes 1048576 | tf_op jit(solution)/shard_map/all_to_all | solution.py:128
  50.9 0.0 all-gather.3.cloned.1.call-start
  50.9 4.9 %fusion.24.q_ref = f32[256,1536]{1,0:T(8,128)} fusion(bf16[1536,1536]{1,0:T(8,128)(2,1)} %param.16, bf16[256,1536]{1,0:T(8,128)(2,1)S(1)} %copy-done.1, f32[1536]{0:T(1024)S(1)} %copy-done.6, f32[256]{0:T(256)S(1)} %add_rsqrt_fusion.1), kind=kOutput, calls=%fused_computation.37 | convolution fusion | flops 1209532416 | bytes 7085056 | tf_op jit(solution)/shard_map/dot_general | solution.py:133
  55.8 1.6 collective-permute-start.3
  57.4 1.2 collective-permute-start.2
  58.6 1.6 collective-permute-start.1
  60.3 0.6 collective-permute-start
  60.8 0.0 all-to-all-done.1
  60.9 0.0 copy-done.2
  61.0 9.7 %collective-permute-done = bf16[256,256]{1,0:T(8,128)(2,1)} collective-permute-done((bf16[256,256]{1,0:T(8,128)(2,1)S(1)}, bf16[256,256]{1,0:T(8,128)(2,1)}, u32[]{:S(2)}, u32[]{:S(2)}) %collective-permute-start) | collective-permute-done | bytes 131104 | tf_op jit(solution)/shard_map/ppermute | solution.py:148
  70.7 0.9 constant_dynamic-update-slice_fusion.4
  71.6 0.0 collective-permute-done.1
  71.6 0.9 constant_dynamic-update-slice_fusion.3
  72.6 0.0 collective-permute-done.2
  72.6 0.9 constant_dynamic-update-slice_fusion.2
  73.5 0.0 collective-permute-done.3
  73.5 4.7 %gather_fusion.5 = bf16[1280,256]{1,0:T(8,128)(2,1)} fusion(bf16[2816,256]{1,0:T(8,128)(2,1)S(1)} %constant_dynamic-update-slice_fusion, s32[2048]{0:T(1024)S(1)} %pad_clamp_fusion), kind=kCustom, calls=%fused_computation.5 | custom fusion | bytes 1315840 | tf_op jit(solution)/shard_map/jit(_take)/gather | solution.py:166
  78.2 10.8 %shard_map.136 = bf16[256,1536]{1,0:T(8,128)(2,1)} custom-call(s32[2]{0:T(128)} %pad_add_fusion.2.where_ref, f32[256,1536]{1,0:T(8,128)} %fusion.24.q_ref, f32[256,128]{1,0:T(8,128)} %get-tuple-element.18.cos_ref, f32[256,128]{1,0:T(8,128)} %get-tuple-element.12.sin_ref, bf16[1280,256]{1,0:T(8,128)(2,1)} %gather_fusion.5), custom_call_target="tpu_custom_call" | custom-call | tf_op jit(solution)/shard_map/pallas_call | solution.py:64
  89.0 4.1 %multiply_reduce_fusion = (f32[256]{0:T(256)S(1)}, f32[256,1536]{1,0:T(8,128)S(1)}) fusion(bf16[256,1536]{1,0:T(8,128)(2,1)} %shard_map.136, bf16[1536,1536]{1,0:T(8,128)(2,1)} %param.18, bf16[256,1536]{1,0:T(8,128)(2,1)S(1)} %copy-done.1), kind=kOutput, calls=%fused_computation.34 | convolution fusion | flops 1210318592 | bytes 7865344 | tf_op jit(solution)/shard_map/dot_general | solution.py:169
  93.1 0.0 copy-done.3
  93.1 1.1 multiply_convert_fusion
  94.1 0.0 all-gather.3.cloned.1.call-update
  94.2 0.2 reduce-scatter.2.cloned.1.call-start
  94.4 0.0 all-gather.5.cloned.1.call-done
  94.4 36.4 %all-gather.3.cloned.1.call-done = bf16[2048,1536]{1,0:T(8,128)(2,1)} async-done(((bf16[256,1536]{1,0:T(8,128)(2,1)}), bf16[2048,1536]{1,0:T(8,128)(2,1)}) %all-gather.3.cloned.1.call-update) | async-done | bytes 6291472 | tf_op jit(solution)/shard_map/all_gather | solution.py:172
  130.9 11.1 %fusion.9 = f32[2048,1152]{0,1:T(8,128)S(1)} fusion(bf16[2048,1536]{1,0:T(8,128)(2,1)} %all-gather.3.cloned.1.call-done, bf16[1536,1728]{1,0:T(8,128)(2,1)} %all-gather.5.cloned.1.call-done), kind=kOutput, calls=%fused_computation.17 | convolution fusion | flops 7247757312 | bytes 19267584 | tf_op jit(solution)/shard_map/dot_general | solution.py:173
  142.0 9.4 %convolution_convert_fusion = bf16[2048,1536]{1,0:T(8,128)(2,1)} fusion(f32[2048,1152]{0,1:T(8,128)S(1)} %fusion.9, bf16[1536,1728]{1,0:T(8,128)(2,1)} %all-gather.5.cloned.1.call-done), kind=kOutput, calls=%fused_computation.6 | convolution fusion | flops 3638820864 | bytes 17694720 | tf_op jit(solution)/shard_map/dot_general | solution.py:178
  151.4 0.0 reduce-scatter.2.cloned.1.call-update
  151.4 41.8 %reduce-scatter.2.cloned.1.call-done = bf16[256,1536]{1,0:T(8,128)(2,1)} async-done(((bf16[2048,1536]{1,0:T(8,128)(2,1)}), bf16[256,1536]{1,0:T(8,128)(2,1)}) %reduce-scatter.2.cloned.1.call-update) | async-done | bytes 786448 | tf_op jit(solution)/shard_map/reduce_scatter | solution.py:177
  193.2 2.2 %add_convert_fusion = bf16[256,1536]{1,0:T(8,128)(2,1)} fusion(f32[256,1536]{1,0:T(8,128)S(1)} %get-tuple-element.20, bf16[256,1536]{1,0:T(8,128)(2,1)} %reduce-scatter.2.cloned.1.call-done), kind=kLoop, calls=%fused_computation.32 | loop fusion | flops 1179648 | bytes 3145728 | tf_op jit(solution)/shard_map/convert_element_type | solution.py:185
  (25 shorter events, 0.3 us)
Async XLA Ops:
  6.5 16.6 %copy-start = (bf16[1536,256]{1,0:T(8,128)(2,1)S(1)}, bf16[1536,256]{1,0:T(8,128)(2,1)}, u32[]{:S(2)}) copy-start(bf16[1536,256]{1,0:T(8,128)(2,1)} %param.17) | copy-start | bytes 2359300
  6.5 4.0 %copy-start.4 = (s32[16]{0:T(128)S(1)}, s32[16]{0:T(128)}, u32[]{:S(2)}) copy-start(s32[16]{0:T(128)} %param.25) | copy-start | bytes 196
  6.5 87.9 %all-gather.5.cloned.1.call-start = ((), (), s32[]{:S(2)}) async-start(), calls=%async_computation.4 | async-start | bytes 5849088 | tf_op jit(solution)/shard_map/all_gather | solution.py:115
  13.4 8.8 %copy-start.5 = (s32[3,128]{1,0:T(4,128)S(1)}, s32[3,128]{1,0:T(4,128)}, u32[]{:S(2)}) copy-start(s32[3,128]{1,0:T(4,128)} %param.27) | copy-start | bytes 4612
  13.4 9.4 %copy-start.1 = (bf16[256,1536]{1,0:T(8,128)(2,1)S(1)}, bf16[256,1536]{1,0:T(8,128)(2,1)}, u32[]{:S(2)}) copy-start(bf16[256,1536]{1,0:T(8,128)(2,1)} %param.14) | copy-start | bytes 2359300
  13.4 9.7 %copy-start.6 = (f32[1536]{0:T(1024)S(1)}, f32[1536]{0:T(1024)}, u32[]{:S(2)}) copy-start(f32[1536]{0:T(1024)} %param.15) | copy-start | bytes 18436
  13.4 27.5 %all-to-all-start = ((bf16[16,2,64,256]{3,2,1,0:T(8,128)(2,1)}), bf16[16,2,64,256]{3,2,1,0:T(8,128)(2,1)S(1)}, u32[]{:S(2)}, u32[]{:S(2)}) async-start(bf16[16,2,64,256]{3,2,1,0:T(8,128)(2,1)} %bitcast.13), calls=%async_computation | async-start | bytes 2097152 | tf_op jit(solution)/shard_map/all_to_all | solution.py:124
  42.3 18.5 %all-to-all-start.1 = ((bf16[8,2,64,256]{3,2,1,0:T(8,128)(2,1)}), bf16[8,2,64,256]{3,2,1,0:T(8,128)(2,1)S(1)}, u32[]{:S(2)}, u32[]{:S(2)}) async-start(bf16[8,2,64,256]{3,2,1,0:T(8,128)(2,1)} %broadcast_in_dim.17), calls=%async_computation.1 | async-start | bytes 1048576 | tf_op jit(solution)/shard_map/all_to_all | solution.py:128
  50.9 80.0 %all-gather.3.cloned.1.call-start = ((), (), s32[]{:S(2)}) async-start(), calls=%async_computation.3 | async-start | bytes 7077888 | tf_op jit(solution)/shard_map/all_gather | solution.py:172
  55.8 5.1 %copy-start.2 = (bf16[1,512,256]{2,1,0:T(8,128)(2,1)S(1)}, bf16[1,512,256]{2,1,0:T(8,128)(2,1)}, u32[]{:S(2)}) copy-start(bf16[1,512,256]{2,1,0:T(8,128)(2,1)} %param.24) | copy-start | bytes 786436
  55.8 17.7 %collective-permute-start.3 = (bf16[256,256]{1,0:T(8,128)(2,1)S(1)}, bf16[256,256]{1,0:T(8,128)(2,1)S(1)}, u32[]{:S(2)}, u32[]{:S(2)}) collective-permute-start(bf16[256,256]{1,0:T(8,128)(2,1)S(1)} %pad_maximum_fusion), channel_id=1, source_target_pairs={{0,1},{1,2},{2,3},{3,4},{4,5},{5,6},{6,7},{7,0},{8,9},{9,10},{10,1... | collective-permute-start | bytes 393224 | tf_op jit(solution)/shard_map/ppermute | solution.py:148
  57.4 15.1 %collective-permute-start.2 = (bf16[256,256]{1,0:T(8,128)(2,1)S(1)}, bf16[256,256]{1,0:T(8,128)(2,1)}, u32[]{:S(2)}, u32[]{:S(2)}) collective-permute-start(bf16[256,256]{1,0:T(8,128)(2,1)S(1)} %pad_maximum_fusion), channel_id=1, source_target_pairs={{0,2},{1,3},{2,4},{3,5},{4,6},{5,7},{6,0},{7,1},{8,10},{9,11},{10,... | collective-permute-start | bytes 393224 | tf_op jit(solution)/shard_map/ppermute | solution.py:148
  58.6 13.0 %collective-permute-start.1 = (bf16[256,256]{1,0:T(8,128)(2,1)S(1)}, bf16[256,256]{1,0:T(8,128)(2,1)}, u32[]{:S(2)}, u32[]{:S(2)}) collective-permute-start(bf16[256,256]{1,0:T(8,128)(2,1)S(1)} %pad_maximum_fusion), channel_id=1, source_target_pairs={{0,3},{1,4},{2,5},{3,6},{4,7},{5,0},{6,1},{7,2},{8,11},{9,12},{10,... | collective-permute-start | bytes 393224 | tf_op jit(solution)/shard_map/ppermute | solution.py:148
  60.3 10.5 %collective-permute-start = (bf16[256,256]{1,0:T(8,128)(2,1)S(1)}, bf16[256,256]{1,0:T(8,128)(2,1)}, u32[]{:S(2)}, u32[]{:S(2)}) collective-permute-start(bf16[256,256]{1,0:T(8,128)(2,1)S(1)} %pad_maximum_fusion), channel_id=1, source_target_pairs={{0,4},{1,5},{2,6},{3,7},{4,0},{5,1},{6,2},{7,3},{8,12},{9,13},{10,... | collective-permute-start | bytes 393224 | tf_op jit(solution)/shard_map/ppermute | solution.py:148
  89.0 4.1 %copy-start.3 = (f32[1536]{0:T(1024)S(1)}, f32[1536]{0:T(1024)}, u32[]{:S(2)}) copy-start(f32[1536]{0:T(1024)} %param.19) | copy-start | bytes 18436
  94.2 99.0 %reduce-scatter.2.cloned.1.call-start = ((), (), s32[]{:S(2)}) async-start(), calls=%async_computation.5 | async-start | bytes 7077888 | tf_op jit(solution)/shard_map/reduce_scatter | solution.py:177
Sparse Core Ops, SparseCore 0:
  9.5 69.3 all-gather.4
  94.3 36.5 all-gather.2
  151.6 41.5 reduce-scatter.1

commit v15 on v12

--- a/solution.py
+++ b/solution.py
@@ -141,6 +141,7 @@
     new_vals = keyval_full[:, HD:].astype(jnp.bfloat16)
     new_keyval = jnp.concatenate([new_keys, new_vals], 1)
     back = WINDOW // tok_rows
+    new_keyval, query_full = lax.optimization_barrier((new_keyval, query_full))
     blocks = [
         lax.ppermute(new_keyval, "mlp", [(i, (i + shift) % n_mlp) for i in range(n_mlp)])
         for shift in range(back, 0, -1)

time: 201 us -> 193 us (0.960)
  waiting for transfers between devices: 89 us -> 81.2 us
    all_to_all x1, waiting for transfers between devices: 8.81 us -> 0.7 us  [body(): lax.all_to_all(outgoing, 'req', split_axis=0, concat_axis=0, tiled=True)]
  transfers between devices with their start and end apart: 8 -> 8, of which waited for: 3 -> 3; matrix products, arithmetic and copies ran while one was open for 15% -> 15% of each run, Pallas kernels for 5% -> 6%
where the time goes in v15:
time: 193 us
  waiting for transfers between devices  81.2 us (42%)
  matrix products  30.1 us (16%)
  blocking collectives  17.5 us (9%)
  local copies, waits for them, and re-layouts  16.5 us (9%)
  between operations  15.2 us (8%)
  starting transfers between devices  14.3 us (7%)
  Pallas kernels  10.8 us (6%)
  other arithmetic  6.99 us (4%)
    reduce_scatter x1, waiting for transfers between devices, body(): lax.psum_scatter(lax.dot_general(hidden, down_full, (((1,), (1,)), ((), (...  41.6 us
    all_gather x1, waiting for transfers between devices, body(): all_rows = lax.all_gather(ffn_in, 'mlp', axis=0, tiled=True)  38.9 us
    all_gather x1, blocking collectives, body(): levels = lax.all_gather(my_part, 'mlp', axis=1, tiled=True)  17.5 us
    dot_general x1, matrix products, body(): jnp.dot(all_rows, packed[:, :2 * ff_cols], preferred_element_type=jnp.flo...  11.1 us
    pallas_call x1, Pallas kernels, attend_window(): pl.pallas_call(_attend_kernel, grid_spec=pltpu.PrefetchScalarGridSpec(num...  10.8 us
    dot_general x1, matrix products, body(): lax.dot_general(hidden, down_full, (((1,), (1,)), ((), ())), preferred_el...  9.56 us
    all_to_all x1, starting transfers between devices, body(): lax.all_to_all(outgoing, 'req', split_axis=0, concat_axis=0, tiled=True)  8.73 us
    ppermute x4, starting transfers between devices, body(): lax.ppermute(new_keyval, 'mlp', [(i, (i + shift) % n_mlp) for i in range(...  5.33 us
  transfers between devices with their start and end apart: 8, of which 3 were waited for; matrix products, arithmetic and copies ran while one was open for 15% of the time, Pallas kernels for 6%

profile of v15, /device:TPU:1, one launch (start us, length us, event | category | flops | bytes accessed | tf_op | source)
XLA Modules:
  0.0 192.7 jit_solution(17356069877657809454)
XLA Ops:
  6.5 0.0 copy-start
  6.5 0.0 copy-start.4
  6.5 0.0 all-gather.5.cloned.1.call-start
  6.5 2.0 %concatenate.46 = bf16[96,1728]{1,0:T(8,128)(2,1)} concatenate(bf16[96,576]{1,0:T(8,128)(2,1)} %param.20, bf16[96,576]{1,0:T(8,128)(2,1)} %param.21, bf16[96,576]{1,0:T(8,128)(2,1)} %param.22), dimensions={1} | concatenate | bytes 663552 | tf_op jit(solution)/shard_map/concatenate | solution.py:116
  8.5 0.0 all-gather.5.cloned.1.call-update
  8.5 0.7 compare_select_fusion.8
  9.2 1.3 gather_fusion
  10.5 0.0 copy-done.4
  10.6 0.1 copy.24
  10.6 0.1 reshape.315
  10.7 1.1 constant_dynamic-slice_fusion
  11.8 1.6 gather_fusion.3
  13.4 0.0 copy-start.5
  13.4 0.0 copy-start.1
  13.4 0.0 copy-start.6
  13.4 8.7 %all-to-all-start = ((bf16[16,2,64,256]{3,2,1,0:T(8,128)(2,1)}), bf16[16,2,64,256]{3,2,1,0:T(8,128)(2,1)S(1)}, u32[]{:S(2)}, u32[]{:S(2)}) async-start(bf16[16,2,64,256]{3,2,1,0:T(8,128)(2,1)} %bitcast.13), calls=%async_computation | async-start | bytes 2097152 | tf_op jit(solution)/shard_map/all_to_all | solution.py:124
  22.2 0.0 all-gather.3.cloned.1.call-start
  22.2 0.0 copy-done.5
  22.3 0.7 gather_fusion.2
  22.9 0.0 copy-done.1
  22.9 0.2 fusion.19
  23.2 0.0 copy-done
  23.2 0.0 copy-done.6
  23.2 0.4 fusion.26
  23.7 0.7 gather_fusion.1
  24.4 0.1 constant_dynamic-slice_fusion.1
  24.4 0.6 fusion.46
  26.9 0.1 compare_select_fusion.9
  26.9 0.1 fusion.45
  27.1 1.3 fusion.28
  28.4 5.0 %fusion.24.q_ref = f32[256,1536]{1,0:T(8,128)} fusion(bf16[1536,1536]{1,0:T(8,128)(2,1)} %param.16, bf16[256,1536]{1,0:T(8,128)(2,1)S(1)} %copy-done.1, f32[1536]{0:T(1024)S(1)} %copy-done.6, f32[256]{0:T(256)S(1)} %add_rsqrt_fusion.1), kind=kOutput, calls=%fused_computation.40 | convolution fusion | flops 1209532416 | bytes 7085056 | tf_op jit(solution)/shard_map/dot_general | solution.py:131
  33.3 0.0 copy-start.2
  33.3 2.0 %collective-permute-start.3 = (bf16[256,256]{1,0:T(8,128)(2,1)S(1)}, bf16[256,256]{1,0:T(8,128)(2,1)S(1)}, u32[]{:S(2)}, u32[]{:S(2)}) collective-permute-start(bf16[256,256]{1,0:T(8,128)(2,1)S(1)} %pad_maximum_fusion), channel_id=1, source_target_pairs={{0,1},{1,2},{2,3},{3,4},{4,5},{5,6},{6,7},{7,0},{8,9},{9,10},{10,1... | collective-permute-start | bytes 393224 | tf_op jit(solution)/shard_map/ppermute | solution.py:146
  35.4 1.2 collective-permute-start.2
  36.6 1.6 collective-permute-start.1
  38.1 0.5 collective-permute-start
  38.7 0.2 dynamic-slice_reduce_fusion
  38.8 0.7 fusion.31
  39.5 0.7 pad_add_fusion.2.where_ref
  40.2 0.7 all-to-all-done
  40.9 0.6 gather_fusion.4
  41.5 17.5 %all_gather.9 = bf16[2,512,256]{2,1,0:T(8,128)(2,1)S(1)} all-gather(bf16[2,64,256]{2,1,0:T(8,128)(2,1)S(1)} %gather_fusion.4), channel_id=1, replica_groups=mesh['req'=16,'mlp'=8] {'mlp'}, dimensions={1}, use_global_device_ids=true | all-gather | bytes 589824 | tf_op jit(solution)/shard_map/all_gather | solution.py:127
  59.1 0.0 copy-done.2
  59.1 0.0 collective-permute-done
  59.1 0.9 constant_dynamic-update-slice_fusion.4
  60.0 0.0 collective-permute-done.1
  60.0 0.9 constant_dynamic-update-slice_fusion.3
  61.0 0.0 collective-permute-done.2
  61.0 0.9 constant_dynamic-update-slice_fusion.2
  61.9 0.0 collective-permute-done.3
  62.0 4.7 %gather_fusion.5 = bf16[1280,256]{1,0:T(8,128)(2,1)} fusion(bf16[2816,256]{1,0:T(8,128)(2,1)S(1)} %constant_dynamic-update-slice_fusion, s32[2048]{0:T(1024)S(1)} %pad_clamp_fusion), kind=kCustom, calls=%fused_computation.5 | custom fusion | bytes 1315840 | tf_op jit(solution)/shard_map/jit(_take)/gather | solution.py:164
  66.6 10.8 %shard_map.136 = bf16[256,1536]{1,0:T(8,128)(2,1)} custom-call(s32[2]{0:T(128)} %pad_add_fusion.2.where_ref, f32[256,1536]{1,0:T(8,128)} %fusion.24.q_ref, f32[256,128]{1,0:T(8,128)} %get-tuple-element.18.cos_ref, f32[256,128]{1,0:T(8,128)} %get-tuple-element.11.sin_ref, bf16[1280,256]{1,0:T(8,128)(2,1)} %gather_fusion.5), custom_call_target="tpu_custom_call" | custom-call | tf_op jit(solution)/shard_map/pallas_call | solution.py:64
  77.4 4.1 %multiply_reduce_fusion = (f32[256]{0:T(256)S(1)}, f32[256,1536]{1,0:T(8,128)S(1)}) fusion(bf16[256,1536]{1,0:T(8,128)(2,1)} %shard_map.136, bf16[1536,1536]{1,0:T(8,128)(2,1)} %param.18, bf16[256,1536]{1,0:T(8,128)(2,1)S(1)} %copy-done.1), kind=kOutput, calls=%fused_computation.34 | convolution fusion | flops 1210318592 | bytes 7865344 | tf_op jit(solution)/shard_map/dot_general | solution.py:167
  81.4 0.0 copy-done.3
  81.5 1.1 multiply_convert_fusion
  82.5 0.0 all-gather.3.cloned.1.call-update
  82.6 0.2 reduce-scatter.2.cloned.1.call-start
  82.8 0.0 all-gather.5.cloned.1.call-done
  82.8 38.9 %all-gather.3.cloned.1.call-done = bf16[2048,1536]{1,0:T(8,128)(2,1)} async-done(((bf16[256,1536]{1,0:T(8,128)(2,1)}), bf16[2048,1536]{1,0:T(8,128)(2,1)}) %all-gather.3.cloned.1.call-update) | async-done | bytes 6291472 | tf_op jit(solution)/shard_map/all_gather | solution.py:170
  121.7 11.1 %fusion.9 = f32[2048,1152]{0,1:T(8,128)S(1)} fusion(bf16[2048,1536]{1,0:T(8,128)(2,1)} %all-gather.3.cloned.1.call-done, bf16[1536,1728]{1,0:T(8,128)(2,1)} %all-gather.5.cloned.1.call-done), kind=kOutput, calls=%fused_computation.17 | convolution fusion | flops 7247757312 | bytes 19267584 | tf_op jit(solution)/shard_map/dot_general | solution.py:171
  132.8 9.6 %convolution_convert_fusion = bf16[2048,1536]{1,0:T(8,128)(2,1)} fusion(f32[2048,1152]{0,1:T(8,128)S(1)} %fusion.9, bf16[1536,1728]{1,0:T(8,128)(2,1)} %all-gather.5.cloned.1.call-done), kind=kOutput, calls=%fused_computation.6 | convolution fusion | flops 3638820864 | bytes 17694720 | tf_op jit(solution)/shard_map/dot_general | solution.py:176
  142.3 0.0 reduce-scatter.2.cloned.1.call-update
  142.4 41.6 %reduce-scatter.2.cloned.1.call-done = bf16[256,1536]{1,0:T(8,128)(2,1)} async-done(((bf16[2048,1536]{1,0:T(8,128)(2,1)}), bf16[256,1536]{1,0:T(8,128)(2,1)}) %reduce-scatter.2.cloned.1.call-update) | async-done | bytes 786448 | tf_op jit(solution)/shard_map/reduce_scatter | solution.py:175
  183.9 2.2 %add_convert_fusion = bf16[256,1536]{1,0:T(8,128)(2,1)} fusion(f32[256,1536]{1,0:T(8,128)S(1)} %get-tuple-element.20, bf16[256,1536]{1,0:T(8,128)(2,1)} %reduce-scatter.2.cloned.1.call-done), kind=kLoop, calls=%fused_computation.32 | loop fusion | flops 1179648 | bytes 3145728 | tf_op jit(solution)/shard_map/convert_element_type | solution.py:183
  (22 shorter events, 0.2 us)
Async XLA Ops:
  6.5 16.6 %copy-start = (bf16[1536,256]{1,0:T(8,128)(2,1)S(1)}, bf16[1536,256]{1,0:T(8,128)(2,1)}, u32[]{:S(2)}) copy-start(bf16[1536,256]{1,0:T(8,128)(2,1)} %param.17) | copy-start | bytes 2359300
  6.5 4.0 %copy-start.4 = (s32[16]{0:T(128)S(1)}, s32[16]{0:T(128)}, u32[]{:S(2)}) copy-start(s32[16]{0:T(128)} %param.25) | copy-start | bytes 196
  6.5 76.3 %all-gather.5.cloned.1.call-start = ((), (), s32[]{:S(2)}) async-start(), calls=%async_computation.3 | async-start | bytes 5849088 | tf_op jit(solution)/shard_map/all_gather | solution.py:115
  13.4 8.8 %copy-start.5 = (s32[3,128]{1,0:T(4,128)S(1)}, s32[3,128]{1,0:T(4,128)}, u32[]{:S(2)}) copy-start(s32[3,128]{1,0:T(4,128)} %param.27) | copy-start | bytes 4612
  13.4 9.5 %copy-start.1 = (bf16[256,1536]{1,0:T(8,128)(2,1)S(1)}, bf16[256,1536]{1,0:T(8,128)(2,1)}, u32[]{:S(2)}) copy-start(bf16[256,1536]{1,0:T(8,128)(2,1)} %param.14) | copy-start | bytes 2359300
  13.4 9.8 %copy-start.6 = (f32[1536]{0:T(1024)S(1)}, f32[1536]{0:T(1024)}, u32[]{:S(2)}) copy-start(f32[1536]{0:T(1024)} %param.15) | copy-start | bytes 18436
  13.4 27.5 %all-to-all-start = ((bf16[16,2,64,256]{3,2,1,0:T(8,128)(2,1)}), bf16[16,2,64,256]{3,2,1,0:T(8,128)(2,1)S(1)}, u32[]{:S(2)}, u32[]{:S(2)}) async-start(bf16[16,2,64,256]{3,2,1,0:T(8,128)(2,1)} %bitcast.13), calls=%async_computation | async-start | bytes 2097152 | tf_op jit(solution)/shard_map/all_to_all | solution.py:124
  22.2 99.5 %all-gather.3.cloned.1.call-start = ((), (), s32[]{:S(2)}) async-start(), calls=%async_computation.2 | async-start | bytes 7077888 | tf_op jit(solution)/shard_map/all_gather | solution.py:170
  33.3 25.7 %copy-start.2 = (bf16[1,512,256]{2,1,0:T(8,128)(2,1)S(1)}, bf16[1,512,256]{2,1,0:T(8,128)(2,1)}, u32[]{:S(2)}) copy-start(bf16[1,512,256]{2,1,0:T(8,128)(2,1)} %param.24) | copy-start | bytes 786436
  33.3 28.6 %collective-permute-start.3 = (bf16[256,256]{1,0:T(8,128)(2,1)S(1)}, bf16[256,256]{1,0:T(8,128)(2,1)S(1)}, u32[]{:S(2)}, u32[]{:S(2)}) collective-permute-start(bf16[256,256]{1,0:T(8,128)(2,1)S(1)} %pad_maximum_fusion), channel_id=1, source_target_pairs={{0,1},{1,2},{2,3},{3,4},{4,5},{5,6},{6,7},{7,0},{8,9},{9,10},{10,1... | collective-permute-start | bytes 393224 | tf_op jit(solution)/shard_map/ppermute | solution.py:146
  35.4 25.6 %collective-permute-start.2 = (bf16[256,256]{1,0:T(8,128)(2,1)S(1)}, bf16[256,256]{1,0:T(8,128)(2,1)}, u32[]{:S(2)}, u32[]{:S(2)}) collective-permute-start(bf16[256,256]{1,0:T(8,128)(2,1)S(1)} %pad_maximum_fusion), channel_id=1, source_target_pairs={{0,2},{1,3},{2,4},{3,5},{4,6},{5,7},{6,0},{7,1},{8,10},{9,11},{10,... | collective-permute-start | bytes 393224 | tf_op jit(solution)/shard_map/ppermute | solution.py:146
  36.6 23.5 %collective-permute-start.1 = (bf16[256,256]{1,0:T(8,128)(2,1)S(1)}, bf16[256,256]{1,0:T(8,128)(2,1)}, u32[]{:S(2)}, u32[]{:S(2)}) collective-permute-start(bf16[256,256]{1,0:T(8,128)(2,1)S(1)} %pad_maximum_fusion), channel_id=1, source_target_pairs={{0,3},{1,4},{2,5},{3,6},{4,7},{5,0},{6,1},{7,2},{8,11},{9,12},{10,... | collective-permute-start | bytes 393224 | tf_op jit(solution)/shard_map/ppermute | solution.py:146
  38.1 21.0 %collective-permute-start = (bf16[256,256]{1,0:T(8,128)(2,1)S(1)}, bf16[256,256]{1,0:T(8,128)(2,1)}, u32[]{:S(2)}, u32[]{:S(2)}) collective-permute-start(bf16[256,256]{1,0:T(8,128)(2,1)S(1)} %pad_maximum_fusion), channel_id=1, source_target_pairs={{0,4},{1,5},{2,6},{3,7},{4,0},{5,1},{6,2},{7,3},{8,12},{9,13},{10,... | collective-permute-start | bytes 393224 | tf_op jit(solution)/shard_map/ppermute | solution.py:146
  77.4 4.1 %copy-start.3 = (f32[1536]{0:T(1024)S(1)}, f32[1536]{0:T(1024)}, u32[]{:S(2)}) copy-start(f32[1536]{0:T(1024)} %param.19) | copy-start | bytes 18436
  82.6 101.4 %reduce-scatter.2.cloned.1.call-start = ((), (), s32[]{:S(2)}) async-start(), calls=%async_computation.4 | async-start | bytes 7077888 | tf_op jit(solution)/shard_map/reduce_scatter | solution.py:175
Sparse Core Ops, SparseCore 0:
  9.5 69.3 all-gather.4
  82.7 38.9 all-gather.2
  142.5 41.3 reduce-scatter.1

commit v16 on v15

--- a/solution.py
+++ b/solution.py
@@ -76,6 +76,32 @@
         ),
         out_shape=jax.ShapeDtypeStruct((rows, width), jnp.bfloat16),
     )(where, query_full, cosine, sine, window)
+
+
+def _ffn_kernel(x_ref, w_ref, o_ref):
+    rows = x_ref[...]
+    width = w_ref.shape[1] // 3
+    gate = jnp.dot(rows, w_ref[:, :width], preferred_element_type=jnp.float32)
+    upward = jnp.dot(rows, w_ref[:, width : 2 * width], preferred_element_type=jnp.float32)
+    hidden = (jax.nn.gelu(gate, approximate=True) * upward).astype(jnp.bfloat16)
+    partial_down = lax.dot_general(
+        hidden, w_ref[:, 2 * width :], (((1,), (1,)), ((), ())), preferred_element_type=jnp.float32
+    )
+    o_ref[...] = partial_down.astype(o_ref.dtype)
+
+
+def ffn_block(all_rows, packed, block_rows=512):
+    rows, model = all_rows.shape
+    return pl.pallas_call(
+        _ffn_kernel,
+        grid=(rows // block_rows,),
+        in_specs=[
+            pl.BlockSpec((block_rows, model), lambda i: (i, 0)),
+            pl.BlockSpec(packed.shape, lambda i: (0, 0)),
+        ],
+        out_specs=pl.BlockSpec((block_rows, model), lambda i: (i, 0)),
+        out_shape=jax.ShapeDtypeStruct((rows, model), jnp.bfloat16),
+    )(all_rows, packed)
 
 
 def body(
@@ -112,10 +138,9 @@
     total = len_zero + len_one + my_lengths[2]
 
     ff_cols = w_gate.shape[1]
-    packed = lax.all_gather(
-        jnp.concatenate([w_gate, w_up, w_down], 1), "req", axis=0, tiled=True
-    )
-    down_full = packed[:, 2 * ff_cols :]
+    lanes = -(-ff_cols // 128) * 128
+    padded = [jnp.pad(part, ((0, 0), (0, lanes - ff_cols))) for part in (w_gate, w_up, w_down)]
+    packed = lax.all_gather(jnp.concatenate(padded, 1), "req", axis=0, tiled=True)
 
     wanted = jnp.stack([level_zero, leaf_parent], 1)
     local_slot = wanted % node_dev
@@ -168,17 +193,9 @@
     resid = (tokens.astype(jnp.float32) + attn_out).astype(jnp.bfloat16)
     ffn_in = rms_scale(resid, ffn_gain).astype(jnp.bfloat16)
     all_rows = lax.all_gather(ffn_in, "mlp", axis=0, tiled=True)
-    gate_up = jnp.dot(all_rows, packed[:, : 2 * ff_cols], preferred_element_type=jnp.float32)
-    gate = gate_up[:, :ff_cols]
-    upward = gate_up[:, ff_cols:]
-    hidden = (jax.nn.gelu(gate, approximate=True) * upward).astype(jnp.bfloat16)
+    partial_down = ffn_block(all_rows, packed)
     summed = lax.psum_scatter(
-        lax.dot_general(
-            hidden, down_full, (((1,), (1,)), ((), ())), preferred_element_type=jnp.float32
-        ).astype(jnp.bfloat16),
-        "mlp",
-        scatter_dimension=0,
-        tiled=True,
+        partial_down, "mlp", scatter_dimension=0, tiled=True
     ).astype(jnp.float32)
     return (resid.astype(jnp.float32) + summed).astype(jnp.bfloat16)
 

time: 193 us -> 194 us (level)
  matrix products: 30.1 us -> 9.45 us
  Pallas kernels: 10.8 us -> 30.4 us
  local copies, waits for them, and re-layouts: 16.5 us -> 14.5 us
    dot_general x2 -> x0, matrix products: 20.7 us -> none  [the longest x1 11.1 us: body(): jnp.dot(all_rows, packed[:, :2 * ff_cols], preferred_element_type=jnp.flo...]
    pallas_call x0 -> x1, Pallas kernels: none -> 19.7 us  [ffn_block(): pl.pallas_call(_ffn_kernel, grid=(rows // block_rows,), in_specs=[pl.Bloc...]
    concatenate x1 -> x0, local copies, waits for them, and re-layouts: 1.97 us -> none  [body(): jnp.concatenate([w_gate, w_up, w_down], 1)]
where the time goes in v16:
time: 194 us
  waiting for transfers between devices  82.1 us (42%)
  Pallas kernels  30.4 us (16%)
  blocking collectives  18.5 us (10%)
  between operations  15.2 us (8%)
  local copies, waits for them, and re-layouts  14.5 us (7%)
  starting transfers between devices  14.3 us (7%)
  matrix products  9.45 us (5%)
  other arithmetic  8.89 us (5%)
    reduce_scatter x1, waiting for transfers between devices, body(): lax.psum_scatter(partial_down, 'mlp', scatter_dimension=0, tiled=True)  41.7 us
    all_gather x1, waiting for transfers between devices, body(): all_rows = lax.all_gather(ffn_in, 'mlp', axis=0, tiled=True)  40 us
    pallas_call x1, Pallas kernels, ffn_block(): pl.pallas_call(_ffn_kernel, grid=(rows // block_rows,), in_specs=[pl.Bloc...  19.7 us
    all_gather x1, blocking collectives, body(): levels = lax.all_gather(my_part, 'mlp', axis=1, tiled=True)  18.5 us
    pallas_call x1, Pallas kernels, attend_window(): pl.pallas_call(_attend_kernel, grid_spec=pltpu.PrefetchScalarGridSpec(num...  10.7 us
    all_to_all x1, starting transfers between devices, body(): lax.all_to_all(outgoing, 'req', split_axis=0, concat_axis=0, tiled=True)  8.73 us
    ppermute x4, starting transfers between devices, body(): lax.ppermute(new_keyval, 'mlp', [(i, (i + shift) % n_mlp) for i in range(...  5.33 us
    dot_general x1, matrix products, body(): query_full = jnp.dot(normed, w_query, preferred_element_type=jnp.float32)  4.97 us
  transfers between devices with their start and end apart: 8, of which 3 were waited for; matrix products, arithmetic and copies ran while one was open for 15% of the time, Pallas kernels for 6%

profile of v16, /device:TPU:1, one launch (start us, length us, event | category | flops | bytes accessed | tf_op | source)
XLA Modules:
  0.0 193.5 jit_solution(4702355290267725321)
XLA Ops:
  6.5 0.0 copy-start
  6.5 0.0 copy-start.4
  6.5 0.0 all-gather.5.cloned.1.call-start
  6.5 1.9 fusion.10
  8.4 0.0 all-gather.5.cloned.1.call-update
  8.5 0.7 compare_select_fusion.8
  9.1 1.3 gather_fusion
  10.4 0.0 copy-done.4
  10.5 0.1 copy.24
  10.6 0.1 reshape.315
  10.7 1.1 constant_dynamic-slice_fusion
  11.7 1.6 gather_fusion.3
  13.3 0.0 copy-start.5
  13.4 0.0 copy-start.1
  13.4 0.0 copy-start.6
  13.4 8.7 %all-to-all-start = ((bf16[16,2,64,256]{3,2,1,0:T(8,128)(2,1)}), bf16[16,2,64,256]{3,2,1,0:T(8,128)(2,1)S(1)}, u32[]{:S(2)}, u32[]{:S(2)}) async-start(bf16[16,2,64,256]{3,2,1,0:T(8,128)(2,1)} %bitcast.13), calls=%async_computation | async-start | bytes 2097152 | tf_op jit(solution)/shard_map/all_to_all | solution.py:149
  22.1 0.0 all-gather.3.cloned.1.call-start
  22.1 0.0 copy-done.5
  22.2 0.7 gather_fusion.2
  22.8 0.0 copy-done.1
  22.8 0.2 fusion.2
  23.1 0.0 copy-done
  23.1 0.0 copy-done.6
  23.1 0.4 fusion.15
  23.6 0.7 gather_fusion.1
  24.3 0.1 constant_dynamic-slice_fusion.1
  24.3 0.6 fusion.31
  26.8 0.1 compare_select_fusion.9
  26.9 0.1 fusion.30
  27.0 1.3 fusion.17
  28.3 5.0 %fusion.13.q_ref = f32[256,1536]{1,0:T(8,128)} fusion(bf16[1536,1536]{1,0:T(8,128)(2,1)} %param.16, bf16[256,1536]{1,0:T(8,128)(2,1)S(1)} %copy-done.1, f32[1536]{0:T(1024)S(1)} %copy-done.6, f32[256]{0:T(256)S(1)} %add_rsqrt_fusion.1), kind=kOutput, calls=%fused_computation.32 | convolution fusion | flops 1209532416 | bytes 7085056 | tf_op jit(solution)/shard_map/dot_general | solution.py:156
  33.3 0.0 copy-start.2
  33.3 2.0 %collective-permute-start.3 = (bf16[256,256]{1,0:T(8,128)(2,1)S(1)}, bf16[256,256]{1,0:T(8,128)(2,1)S(1)}, u32[]{:S(2)}, u32[]{:S(2)}) collective-permute-start(bf16[256,256]{1,0:T(8,128)(2,1)S(1)} %pad_maximum_fusion), channel_id=1, source_target_pairs={{0,1},{1,2},{2,3},{3,4},{4,5},{5,6},{6,7},{7,0},{8,9},{9,10},{10,1... | collective-permute-start | bytes 393224 | tf_op jit(solution)/shard_map/ppermute | solution.py:171
  35.3 1.2 collective-permute-start.2
  36.5 1.5 collective-permute-start.1
  38.1 0.5 collective-permute-start
  38.6 0.2 dynamic-slice_reduce_fusion
  38.8 0.7 fusion.20
  39.5 0.7 pad_add_fusion.2.where_ref
  40.1 0.3 all-to-all-done
  40.5 0.6 gather_fusion.4
  41.0 18.5 %all_gather.9 = bf16[2,512,256]{2,1,0:T(8,128)(2,1)S(1)} all-gather(bf16[2,64,256]{2,1,0:T(8,128)(2,1)S(1)} %gather_fusion.4), channel_id=1, replica_groups=mesh['req'=16,'mlp'=8] {'mlp'}, dimensions={1}, use_global_device_ids=true | all-gather | bytes 589824 | tf_op jit(solution)/shard_map/all_gather | solution.py:152
  59.6 0.0 copy-done.2
  59.6 0.0 collective-permute-done
  59.6 0.9 constant_dynamic-update-slice_fusion.4
  60.6 0.0 collective-permute-done.1
  60.6 0.9 constant_dynamic-update-slice_fusion.3
  61.5 0.0 collective-permute-done.2
  61.5 0.9 constant_dynamic-update-slice_fusion.2
  62.4 0.0 collective-permute-done.3
  62.5 4.7 %gather_fusion.5 = bf16[1280,256]{1,0:T(8,128)(2,1)} fusion(bf16[2816,256]{1,0:T(8,128)(2,1)S(1)} %constant_dynamic-update-slice_fusion, s32[2048]{0:T(1024)S(1)} %pad_clamp_fusion), kind=kCustom, calls=%fused_computation.5 | custom fusion | bytes 1315840 | tf_op jit(solution)/shard_map/jit(_take)/gather | solution.py:189
  67.1 10.7 %shard_map.136 = bf16[256,1536]{1,0:T(8,128)(2,1)} custom-call(s32[2]{0:T(128)} %pad_add_fusion.2.where_ref, f32[256,1536]{1,0:T(8,128)} %fusion.13.q_ref, f32[256,128]{1,0:T(8,128)} %get-tuple-element.18.cos_ref, f32[256,128]{1,0:T(8,128)} %get-tuple-element.11.sin_ref, bf16[1280,256]{1,0:T(8,128)(2,1)} %gather_fusion.5), custom_call_target="tpu_custom_call" | custom-call | tf_op jit(solution)/shard_map/pallas_call | solution.py:64
  77.9 0.0 copy-start.3
  77.9 4.1 %multiply_reduce_fusion = (f32[256]{0:T(256)S(1)}, f32[256,1536]{1,0:T(8,128)S(1)}) fusion(bf16[256,1536]{1,0:T(8,128)(2,1)} %shard_map.136, bf16[1536,1536]{1,0:T(8,128)(2,1)} %param.18, bf16[256,1536]{1,0:T(8,128)(2,1)S(1)} %copy-done.1), kind=kOutput, calls=%fused_computation.16 | convolution fusion | flops 1210318592 | bytes 7865344 | tf_op jit(solution)/shard_map/dot_general | solution.py:192
  82.0 0.0 copy-done.3
  82.0 1.1 multiply_convert_fusion
  83.1 0.0 all-gather.3.cloned.1.call-update
  83.1 0.2 reduce-scatter.2.cloned.1.call-start
  83.3 0.0 all-gather.5.cloned.1.call-done.w_ref
  83.3 40.0 %all-gather.3.cloned.1.call-done.x_ref = bf16[2048,1536]{1,0:T(8,128)(2,1)} async-done(((bf16[256,1536]{1,0:T(8,128)(2,1)}), bf16[2048,1536]{1,0:T(8,128)(2,1)}) %all-gather.3.cloned.1.call-update) | async-done | bytes 6291472 | tf_op jit(solution)/shard_map/all_gather | solution.py:195
  123.4 19.7 %shard_map.137 = bf16[2048,1536]{1,0:T(8,128)(2,1)} custom-call(bf16[2048,1536]{1,0:T(8,128)(2,1)} %all-gather.3.cloned.1.call-done.x_ref, bf16[1536,1920]{1,0:T(8,128)(2,1)} %all-gather.5.cloned.1.call-done.w_ref), custom_call_target="tpu_custom_call" | custom-call | tf_op jit(solution)/shard_map/pallas_call | solution.py:95
  143.1 0.0 reduce-scatter.2.cloned.1.call-update
  143.1 41.7 %reduce-scatter.2.cloned.1.call-done = bf16[256,1536]{1,0:T(8,128)(2,1)} async-done(((bf16[2048,1536]{1,0:T(8,128)(2,1)}), bf16[256,1536]{1,0:T(8,128)(2,1)}) %reduce-scatter.2.cloned.1.call-update) | async-done | bytes 786448 | tf_op jit(solution)/shard_map/reduce_scatter | solution.py:197
  184.8 2.2 %add_convert_fusion = bf16[256,1536]{1,0:T(8,128)(2,1)} fusion(f32[256,1536]{1,0:T(8,128)S(1)} %get-tuple-element.20, bf16[256,1536]{1,0:T(8,128)(2,1)} %reduce-scatter.2.cloned.1.call-done), kind=kLoop, calls=%fused_computation.14 | loop fusion | flops 1179648 | bytes 3145728 | tf_op jit(solution)/shard_map/convert_element_type | solution.py:200
  (21 shorter events, 0.2 us)
Async XLA Ops:
  6.5 16.6 %copy-start = (bf16[1536,256]{1,0:T(8,128)(2,1)S(1)}, bf16[1536,256]{1,0:T(8,128)(2,1)}, u32[]{:S(2)}) copy-start(bf16[1536,256]{1,0:T(8,128)(2,1)} %param.17) | copy-start | bytes 2359300
  6.5 3.9 %copy-start.4 = (s32[16]{0:T(128)S(1)}, s32[16]{0:T(128)}, u32[]{:S(2)}) copy-start(s32[16]{0:T(128)} %param.25) | copy-start | bytes 196
  6.5 76.8 %all-gather.5.cloned.1.call-start = ((), (), s32[]{:S(2)}) async-start(), calls=%async_computation.3 | async-start | bytes 6266880 | tf_op jit(solution)/shard_map/all_gather | solution.py:143
  13.3 8.8 %copy-start.5 = (s32[3,128]{1,0:T(4,128)S(1)}, s32[3,128]{1,0:T(4,128)}, u32[]{:S(2)}) copy-start(s32[3,128]{1,0:T(4,128)} %param.27) | copy-start | bytes 4612
  13.4 9.5 %copy-start.1 = (bf16[256,1536]{1,0:T(8,128)(2,1)S(1)}, bf16[256,1536]{1,0:T(8,128)(2,1)}, u32[]{:S(2)}) copy-start(bf16[256,1536]{1,0:T(8,128)(2,1)} %param.14) | copy-start | bytes 2359300
  13.4 9.8 %copy-start.6 = (f32[1536]{0:T(1024)S(1)}, f32[1536]{0:T(1024)}, u32[]{:S(2)}) copy-start(f32[1536]{0:T(1024)} %param.15) | copy-start | bytes 18436
  13.4 27.1 %all-to-all-start = ((bf16[16,2,64,256]{3,2,1,0:T(8,128)(2,1)}), bf16[16,2,64,256]{3,2,1,0:T(8,128)(2,1)S(1)}, u32[]{:S(2)}, u32[]{:S(2)}) async-start(bf16[16,2,64,256]{3,2,1,0:T(8,128)(2,1)} %bitcast.13), calls=%async_computation | async-start | bytes 2097152 | tf_op jit(solution)/shard_map/all_to_all | solution.py:149
  22.1 101.3 %all-gather.3.cloned.1.call-start = ((), (), s32[]{:S(2)}) async-start(), calls=%async_computation.2 | async-start | bytes 7077888 | tf_op jit(solution)/shard_map/all_gather | solution.py:195
  33.3 26.3 %copy-start.2 = (bf16[1,512,256]{2,1,0:T(8,128)(2,1)S(1)}, bf16[1,512,256]{2,1,0:T(8,128)(2,1)}, u32[]{:S(2)}) copy-start(bf16[1,512,256]{2,1,0:T(8,128)(2,1)} %param.24) | copy-start | bytes 786436
  33.3 29.2 %collective-permute-start.3 = (bf16[256,256]{1,0:T(8,128)(2,1)S(1)}, bf16[256,256]{1,0:T(8,128)(2,1)S(1)}, u32[]{:S(2)}, u32[]{:S(2)}) collective-permute-start(bf16[256,256]{1,0:T(8,128)(2,1)S(1)} %pad_maximum_fusion), channel_id=1, source_target_pairs={{0,1},{1,2},{2,3},{3,4},{4,5},{5,6},{6,7},{7,0},{8,9},{9,10},{10,1... | collective-permute-start | bytes 393224 | tf_op jit(solution)/shard_map/ppermute | solution.py:171
  35.3 26.2 %collective-permute-start.2 = (bf16[256,256]{1,0:T(8,128)(2,1)S(1)}, bf16[256,256]{1,0:T(8,128)(2,1)}, u32[]{:S(2)}, u32[]{:S(2)}) collective-permute-start(bf16[256,256]{1,0:T(8,128)(2,1)S(1)} %pad_maximum_fusion), channel_id=1, source_target_pairs={{0,2},{1,3},{2,4},{3,5},{4,6},{5,7},{6,0},{7,1},{8,10},{9,11},{10,... | collective-permute-start | bytes 393224 | tf_op jit(solution)/shard_map/ppermute | solution.py:171
  36.5 24.1 %collective-permute-start.1 = (bf16[256,256]{1,0:T(8,128)(2,1)S(1)}, bf16[256,256]{1,0:T(8,128)(2,1)}, u32[]{:S(2)}, u32[]{:S(2)}) collective-permute-start(bf16[256,256]{1,0:T(8,128)(2,1)S(1)} %pad_maximum_fusion), channel_id=1, source_target_pairs={{0,3},{1,4},{2,5},{3,6},{4,7},{5,0},{6,1},{7,2},{8,11},{9,12},{10,... | collective-permute-start | bytes 393224 | tf_op jit(solution)/shard_map/ppermute | solution.py:171
  38.1 21.6 %collective-permute-start = (bf16[256,256]{1,0:T(8,128)(2,1)S(1)}, bf16[256,256]{1,0:T(8,128)(2,1)}, u32[]{:S(2)}, u32[]{:S(2)}) collective-permute-start(bf16[256,256]{1,0:T(8,128)(2,1)S(1)} %pad_maximum_fusion), channel_id=1, source_target_pairs={{0,4},{1,5},{2,6},{3,7},{4,0},{5,1},{6,2},{7,3},{8,12},{9,13},{10,... | collective-permute-start | bytes 393224 | tf_op jit(solution)/shard_map/ppermute | solution.py:171
  77.9 4.1 %copy-start.3 = (f32[1536]{0:T(1024)S(1)}, f32[1536]{0:T(1024)}, u32[]{:S(2)}) copy-start(f32[1536]{0:T(1024)} %param.19) | copy-start | bytes 18436
  83.1 101.7 %reduce-scatter.2.cloned.1.call-start = ((), (), s32[]{:S(2)}) async-start(), calls=%async_computation.4 | async-start | bytes 7077888 | tf_op jit(solution)/shard_map/reduce_scatter | solution.py:197
Sparse Core Ops, SparseCore 0:
  9.5 71.1 all-gather.4
  83.2 40.1 all-gather.2
  143.2 41.5 reduce-scatter.1

commit v17 on v15

--- a/solution.py
+++ b/solution.py
@@ -57,7 +57,7 @@
         o_ref[:, cols] = (mixed / denom).astype(o_ref.dtype)
 
 
-def attend_window(query_full, cosine, sine, window, where, heads_per_step=4):
+def attend_window(query_full, cosine, sine, window, where, heads_per_step=12):
     rows, width = query_full.shape
     span = window.shape[0]
     step_cols = heads_per_step * HD

time: 193 us -> 193 us (level)
  transfers between devices with their start and end apart: 8 -> 8, of which waited for: 3 -> 3; matrix products, arithmetic and copies ran while one was open for 15% -> 15% of each run, Pallas kernels for 6% -> 5%
where the time goes in v17:
time: 193 us; the launch traced here: 192 us
  waiting for transfers between devices  81 us (42%)
  matrix products  30.1 us (16%)
  blocking collectives  17.7 us (9%)
  local copies, waits for them, and re-layouts  16.5 us (9%)
  between operations  15.2 us (8%)
  starting transfers between devices  14.4 us (7%)
  Pallas kernels  10.5 us (5%)
  other arithmetic  6.99 us (4%)
    reduce_scatter x1, waiting for transfers between devices, body(): lax.psum_scatter(lax.dot_general(hidden, down_full, (((1,), (1,)), ((), (...  41.6 us
    all_gather x1, waiting for transfers between devices, body(): all_rows = lax.all_gather(ffn_in, 'mlp', axis=0, tiled=True)  38.7 us
    all_gather x1, blocking collectives, body(): levels = lax.all_gather(my_part, 'mlp', axis=1, tiled=True)  17.7 us
    dot_general x1, matrix products, body(): jnp.dot(all_rows, packed[:, :2 * ff_cols], preferred_element_type=jnp.flo...  11.1 us
    pallas_call x1, Pallas kernels, attend_window(): pl.pallas_call(_attend_kernel, grid_spec=pltpu.PrefetchScalarGridSpec(num...  10.5 us
    dot_general x1, matrix products, body(): lax.dot_general(hidden, down_full, (((1,), (1,)), ((), ())), preferred_el...  9.56 us
    all_to_all x1, starting transfers between devices, body(): lax.all_to_all(outgoing, 'req', split_axis=0, concat_axis=0, tiled=True)  8.73 us
    ppermute x4, starting transfers between devices, body(): lax.ppermute(new_keyval, 'mlp', [(i, (i + shift) % n_mlp) for i in range(...  5.33 us
  transfers between devices with their start and end apart: 8, of which 3 were waited for; matrix products, arithmetic and copies ran while one was open for 15% of the time, Pallas kernels for 5%

profile of v17, /device:TPU:1, one launch (start us, length us, event | category | flops | bytes accessed | tf_op | source)
XLA Modules:
  0.0 192.5 jit_solution(2298573466402526588)
XLA Ops:
  6.5 0.0 copy-start
  6.5 0.0 copy-start.4
  6.5 0.0 all-gather.5.cloned.1.call-start
  6.5 2.0 %concatenate.46 = bf16[96,1728]{1,0:T(8,128)(2,1)} concatenate(bf16[96,576]{1,0:T(8,128)(2,1)} %param.20, bf16[96,576]{1,0:T(8,128)(2,1)} %param.21, bf16[96,576]{1,0:T(8,128)(2,1)} %param.22), dimensions={1} | concatenate | bytes 663552 | tf_op jit(solution)/shard_map/concatenate | solution.py:116
  8.5 0.0 all-gather.5.cloned.1.call-update
  8.5 0.7 compare_select_fusion.8
  9.2 1.3 gather_fusion
  10.5 0.0 copy-done.4
  10.6 0.1 copy.24
  10.6 0.1 reshape.315
  10.7 1.1 constant_dynamic-slice_fusion
  11.8 1.6 gather_fusion.3
  13.4 0.0 copy-start.5
  13.4 0.0 copy-start.6
  13.4 8.7 %all-to-all-start = ((bf16[16,2,64,256]{3,2,1,0:T(8,128)(2,1)}), bf16[16,2,64,256]{3,2,1,0:T(8,128)(2,1)S(1)}, u32[]{:S(2)}, u32[]{:S(2)}) async-start(bf16[16,2,64,256]{3,2,1,0:T(8,128)(2,1)} %bitcast.13), calls=%async_computation | async-start | bytes 2097152 | tf_op jit(solution)/shard_map/all_to_all | solution.py:124
  22.2 0.0 all-gather.3.cloned.1.call-start
  22.2 0.0 copy-done.5
  22.3 0.7 gather_fusion.2
  22.9 0.0 copy-done.1
  22.9 0.2 fusion.19
  23.2 0.0 copy-done
  23.2 0.0 copy-done.6
  23.2 0.4 fusion.26
  23.7 0.7 gather_fusion.1
  24.4 0.1 constant_dynamic-slice_fusion.1
  24.4 0.6 fusion.46
  26.9 0.1 compare_select_fusion.9
  26.9 0.1 fusion.45
  27.1 1.3 fusion.28
  28.4 5.0 %fusion.24.q_ref = f32[256,1536]{1,0:T(8,128)} fusion(bf16[1536,1536]{1,0:T(8,128)(2,1)} %param.16, bf16[256,1536]{1,0:T(8,128)(2,1)S(1)} %copy-done.1, f32[1536]{0:T(1024)S(1)} %copy-done.6, f32[256]{0:T(256)S(1)} %add_rsqrt_fusion.1), kind=kOutput, calls=%fused_computation.40 | convolution fusion | flops 1209532416 | bytes 7085056 | tf_op jit(solution)/shard_map/dot_general | solution.py:131
  33.3 0.0 copy-start.2
  33.3 2.0 %collective-permute-start.3 = (bf16[256,256]{1,0:T(8,128)(2,1)S(1)}, bf16[256,256]{1,0:T(8,128)(2,1)S(1)}, u32[]{:S(2)}, u32[]{:S(2)}) collective-permute-start(bf16[256,256]{1,0:T(8,128)(2,1)S(1)} %pad_maximum_fusion), channel_id=1, source_target_pairs={{0,1},{1,2},{2,3},{3,4},{4,5},{5,6},{6,7},{7,0},{8,9},{9,10},{10,1... | collective-permute-start | bytes 393224 | tf_op jit(solution)/shard_map/ppermute | solution.py:146
  35.4 1.2 collective-permute-start.2
  36.6 1.6 collective-permute-start.1
  38.1 0.5 collective-permute-start
  38.7 0.2 dynamic-slice_reduce_fusion
  38.8 0.7 fusion.31
  39.5 0.7 pad_add_fusion.2.where_ref
  40.2 0.7 all-to-all-done
  40.9 0.6 gather_fusion.4
  41.5 17.7 %all_gather.9 = bf16[2,512,256]{2,1,0:T(8,128)(2,1)S(1)} all-gather(bf16[2,64,256]{2,1,0:T(8,128)(2,1)S(1)} %gather_fusion.4), channel_id=1, replica_groups=mesh['req'=16,'mlp'=8] {'mlp'}, dimensions={1}, use_global_device_ids=true | all-gather | bytes 589824 | tf_op jit(solution)/shard_map/all_gather | solution.py:127
  59.2 0.0 copy-done.2
  59.3 0.0 collective-permute-done
  59.3 0.9 constant_dynamic-update-slice_fusion.4
  60.2 0.0 collective-permute-done.1
  60.2 0.9 constant_dynamic-update-slice_fusion.3
  61.1 0.0 collective-permute-done.2
  61.2 0.9 constant_dynamic-update-slice_fusion.2
  62.1 0.0 collective-permute-done.3
  62.1 4.7 %gather_fusion.5 = bf16[1280,256]{1,0:T(8,128)(2,1)} fusion(bf16[2816,256]{1,0:T(8,128)(2,1)S(1)} %constant_dynamic-update-slice_fusion, s32[2048]{0:T(1024)S(1)} %pad_clamp_fusion), kind=kCustom, calls=%fused_computation.5 | custom fusion | bytes 1315840 | tf_op jit(solution)/shard_map/jit(_take)/gather | solution.py:164
  66.8 10.5 %shard_map.136 = bf16[256,1536]{1,0:T(8,128)(2,1)} custom-call(s32[2]{0:T(128)} %pad_add_fusion.2.where_ref, f32[256,1536]{1,0:T(8,128)} %fusion.24.q_ref, f32[256,128]{1,0:T(8,128)} %get-tuple-element.18.cos_ref, f32[256,128]{1,0:T(8,128)} %get-tuple-element.11.sin_ref, bf16[1280,256]{1,0:T(8,128)(2,1)} %gather_fusion.5), custom_call_target="tpu_custom_call" | custom-call | tf_op jit(solution)/shard_map/pallas_call | solution.py:64
  77.3 0.0 copy-start.3
  77.3 4.1 %multiply_reduce_fusion = (f32[256]{0:T(256)S(1)}, f32[256,1536]{1,0:T(8,128)S(1)}) fusion(bf16[256,1536]{1,0:T(8,128)(2,1)} %shard_map.136, bf16[1536,1536]{1,0:T(8,128)(2,1)} %param.18, bf16[256,1536]{1,0:T(8,128)(2,1)S(1)} %copy-done.1), kind=kOutput, calls=%fused_computation.34 | convolution fusion | flops 1210318592 | bytes 7865344 | tf_op jit(solution)/shard_map/dot_general | solution.py:167
  81.4 0.0 copy-done.3
  81.4 1.1 multiply_convert_fusion
  82.5 0.0 all-gather.3.cloned.1.call-update
  82.5 0.3 reduce-scatter.2.cloned.1.call-start
  82.8 0.0 all-gather.5.cloned.1.call-done
  82.8 38.7 %all-gather.3.cloned.1.call-done = bf16[2048,1536]{1,0:T(8,128)(2,1)} async-done(((bf16[256,1536]{1,0:T(8,128)(2,1)}), bf16[2048,1536]{1,0:T(8,128)(2,1)}) %all-gather.3.cloned.1.call-update) | async-done | bytes 6291472 | tf_op jit(solution)/shard_map/all_gather | solution.py:170
  121.5 11.1 %fusion.9 = f32[2048,1152]{0,1:T(8,128)S(1)} fusion(bf16[2048,1536]{1,0:T(8,128)(2,1)} %all-gather.3.cloned.1.call-done, bf16[1536,1728]{1,0:T(8,128)(2,1)} %all-gather.5.cloned.1.call-done), kind=kOutput, calls=%fused_computation.17 | convolution fusion | flops 7247757312 | bytes 19267584 | tf_op jit(solution)/shard_map/dot_general | solution.py:171
  132.6 9.6 %convolution_convert_fusion = bf16[2048,1536]{1,0:T(8,128)(2,1)} fusion(f32[2048,1152]{0,1:T(8,128)S(1)} %fusion.9, bf16[1536,1728]{1,0:T(8,128)(2,1)} %all-gather.5.cloned.1.call-done), kind=kOutput, calls=%fused_computation.6 | convolution fusion | flops 3638820864 | bytes 17694720 | tf_op jit(solution)/shard_map/dot_general | solution.py:176
  142.2 0.0 reduce-scatter.2.cloned.1.call-update
  142.2 41.6 %reduce-scatter.2.cloned.1.call-done = bf16[256,1536]{1,0:T(8,128)(2,1)} async-done(((bf16[2048,1536]{1,0:T(8,128)(2,1)}), bf16[256,1536]{1,0:T(8,128)(2,1)}) %reduce-scatter.2.cloned.1.call-update) | async-done | bytes 786448 | tf_op jit(solution)/shard_map/reduce_scatter | solution.py:175
  183.8 2.2 %add_convert_fusion = bf16[256,1536]{1,0:T(8,128)(2,1)} fusion(f32[256,1536]{1,0:T(8,128)S(1)} %get-tuple-element.20, bf16[256,1536]{1,0:T(8,128)(2,1)} %reduce-scatter.2.cloned.1.call-done), kind=kLoop, calls=%fused_computation.32 | loop fusion | flops 1179648 | bytes 3145728 | tf_op jit(solution)/shard_map/convert_element_type | solution.py:183
  (22 shorter events, 0.2 us)
Async XLA Ops:
  6.5 16.6 %copy-start = (bf16[1536,256]{1,0:T(8,128)(2,1)S(1)}, bf16[1536,256]{1,0:T(8,128)(2,1)}, u32[]{:S(2)}) copy-start(bf16[1536,256]{1,0:T(8,128)(2,1)} %param.17) | copy-start | bytes 2359300
  6.5 4.0 %copy-start.4 = (s32[16]{0:T(128)S(1)}, s32[16]{0:T(128)}, u32[]{:S(2)}) copy-start(s32[16]{0:T(128)} %param.25) | copy-start | bytes 196
  6.5 76.3 %all-gather.5.cloned.1.call-start = ((), (), s32[]{:S(2)}) async-start(), calls=%async_computation.3 | async-start | bytes 5849088 | tf_op jit(solution)/shard_map/all_gather | solution.py:115
  13.4 8.8 %copy-start.5 = (s32[3,128]{1,0:T(4,128)S(1)}, s32[3,128]{1,0:T(4,128)}, u32[]{:S(2)}) copy-start(s32[3,128]{1,0:T(4,128)} %param.27) | copy-start | bytes 4612
  13.4 9.5 %copy-start.1 = (bf16[256,1536]{1,0:T(8,128)(2,1)S(1)}, bf16[256,1536]{1,0:T(8,128)(2,1)}, u32[]{:S(2)}) copy-start(bf16[256,1536]{1,0:T(8,128)(2,1)} %param.14) | copy-start | bytes 2359300
  13.4 9.8 %copy-start.6 = (f32[1536]{0:T(1024)S(1)}, f32[1536]{0:T(1024)}, u32[]{:S(2)}) copy-start(f32[1536]{0:T(1024)} %param.15) | copy-start | bytes 18436
  13.4 27.5 %all-to-all-start = ((bf16[16,2,64,256]{3,2,1,0:T(8,128)(2,1)}), bf16[16,2,64,256]{3,2,1,0:T(8,128)(2,1)S(1)}, u32[]{:S(2)}, u32[]{:S(2)}) async-start(bf16[16,2,64,256]{3,2,1,0:T(8,128)(2,1)} %bitcast.13), calls=%async_computation | async-start | bytes 2097152 | tf_op jit(solution)/shard_map/all_to_all | solution.py:124
  22.2 99.3 %all-gather.3.cloned.1.call-start = ((), (), s32[]{:S(2)}) async-start(), calls=%async_computation.2 | async-start | bytes 7077888 | tf_op jit(solution)/shard_map/all_gather | solution.py:170
  33.3 25.9 %copy-start.2 = (bf16[1,512,256]{2,1,0:T(8,128)(2,1)S(1)}, bf16[1,512,256]{2,1,0:T(8,128)(2,1)}, u32[]{:S(2)}) copy-start(bf16[1,512,256]{2,1,0:T(8,128)(2,1)} %param.24) | copy-start | bytes 786436
  33.3 28.8 %collective-permute-start.3 = (bf16[256,256]{1,0:T(8,128)(2,1)S(1)}, bf16[256,256]{1,0:T(8,128)(2,1)S(1)}, u32[]{:S(2)}, u32[]{:S(2)}) collective-permute-start(bf16[256,256]{1,0:T(8,128)(2,1)S(1)} %pad_maximum_fusion), channel_id=1, source_target_pairs={{0,1},{1,2},{2,3},{3,4},{4,5},{5,6},{6,7},{7,0},{8,9},{9,10},{10,1... | collective-permute-start | bytes 393224 | tf_op jit(solution)/shard_map/ppermute | solution.py:146
  35.4 25.8 %collective-permute-start.2 = (bf16[256,256]{1,0:T(8,128)(2,1)S(1)}, bf16[256,256]{1,0:T(8,128)(2,1)}, u32[]{:S(2)}, u32[]{:S(2)}) collective-permute-start(bf16[256,256]{1,0:T(8,128)(2,1)S(1)} %pad_maximum_fusion), channel_id=1, source_target_pairs={{0,2},{1,3},{2,4},{3,5},{4,6},{5,7},{6,0},{7,1},{8,10},{9,11},{10,... | collective-permute-start | bytes 393224 | tf_op jit(solution)/shard_map/ppermute | solution.py:146
  36.6 23.6 %collective-permute-start.1 = (bf16[256,256]{1,0:T(8,128)(2,1)S(1)}, bf16[256,256]{1,0:T(8,128)(2,1)}, u32[]{:S(2)}, u32[]{:S(2)}) collective-permute-start(bf16[256,256]{1,0:T(8,128)(2,1)S(1)} %pad_maximum_fusion), channel_id=1, source_target_pairs={{0,3},{1,4},{2,5},{3,6},{4,7},{5,0},{6,1},{7,2},{8,11},{9,12},{10,... | collective-permute-start | bytes 393224 | tf_op jit(solution)/shard_map/ppermute | solution.py:146
  38.1 21.1 %collective-permute-start = (bf16[256,256]{1,0:T(8,128)(2,1)S(1)}, bf16[256,256]{1,0:T(8,128)(2,1)}, u32[]{:S(2)}, u32[]{:S(2)}) collective-permute-start(bf16[256,256]{1,0:T(8,128)(2,1)S(1)} %pad_maximum_fusion), channel_id=1, source_target_pairs={{0,4},{1,5},{2,6},{3,7},{4,0},{5,1},{6,2},{7,3},{8,12},{9,13},{10,... | collective-permute-start | bytes 393224 | tf_op jit(solution)/shard_map/ppermute | solution.py:146
  77.3 4.1 %copy-start.3 = (f32[1536]{0:T(1024)S(1)}, f32[1536]{0:T(1024)}, u32[]{:S(2)}) copy-start(f32[1536]{0:T(1024)} %param.19) | copy-start | bytes 18436
  82.5 101.2 %reduce-scatter.2.cloned.1.call-start = ((), (), s32[]{:S(2)}) async-start(), calls=%async_computation.4 | async-start | bytes 7077888 | tf_op jit(solution)/shard_map/reduce_scatter | solution.py:175
Sparse Core Ops, SparseCore 0:
  9.5 69.3 all-gather.4
  82.6 38.8 all-gather.2
  142.3 41.3 reduce-scatter.1
